TPU v7x, 32 devices: a whole 2x2x4 slice. The times are simulated.
32 devices in a mesh: grid: 8 (over z, x), mem: 4 (over y, core).
Axes of the slice: x: 2, y: 2, z: 4, core: 2. Of those that a mesh axis runs over, the one named last changes fastest.
Arguments:
- members: bfloat16 [80, 4, 16, 512], P('mem', None, 'grid'), may hold values from -0.8984375 to 0.8984375
- innovation: float32 [4, 16, 512], P(None, 'grid'), may hold values from -6 to 6
- observed_count: int32 [16, 512], P('grid'), may hold values from 0 to 3
- obs_precision: float32 [4], replicated, may hold values from 0.5 to 4
Outputs:
- recentred: bfloat16 [80, 4, 16, 512], P('mem', None, 'grid')
- increment: float32 [4, 16, 512], P('mem', 'grid')
All inputs are finite; a program needn't handle non-finite values.
Results may differ from a plain program's by a relative error of at most 0.0004.
Values may be sent and summed in bfloat16 or wider, within the bound.
No kernel may reach another device: no remote copies, remote signals or barrier semaphores. Data moves between devices by JAX's collectives and lax.ppermute only.
A program may use at most 64 MiB of HBM per device.

v0:
```python
import jax
import jax.numpy as jnp
from jax import lax
from jax.sharding import PartitionSpec as P

PASSES = 2
ITERS = 2


diffusion = 0.25


def padded(value, sides, width):
    for axis, dim in sides:
        devices, length = (lax.axis_size(axis), value.shape[dim])
        up = [(i, (i + 1) % devices) for i in range(devices - 1)]
        down = [(j, i) for i, j in up]
        last = lax.slice_in_dim(value, length - width, length, axis=dim)
        leading = lax.slice_in_dim(value, 0, width, axis=dim)
        before = lax.ppermute(last, axis, up)
        after = lax.ppermute(leading, axis, down)
        value = jnp.concatenate([before, value, after], axis=dim)
    return value


def smooth(field):
    for sweep_index in range(PASSES):
        extended = padded(field, (("grid", 2),), 1)
        centre = extended[:, :, 1:-1]
        field = centre + diffusion * (extended[:, :, :-2] + extended[:, :, 2:] - 2.0 * centre)
    for sweep_index in range(PASSES):
        field = field + diffusion * (jnp.roll(field, 1, 3) + jnp.roll(field, -1, 3) - 2.0 * field)
    return field


def member_total(product):
    summed = jnp.sum(product, axis=0)
    return summed


def norm_of(residual):
    return lax.psum(jnp.sum(residual * residual), ("grid", "mem"))


def local(members, innovation, observed_count, obs_precision):
    mem_index = lax.axis_index("mem")
    level_share = members.shape[1] // lax.axis_size("mem")
    perturbed = lax.all_to_all(members, "mem", split_axis=1, concat_axis=0, tiled=True)
    precision = lax.dynamic_slice_in_dim(obs_precision, mem_index * level_share, level_share, 0)
    local_innovation = lax.dynamic_slice_in_dim(innovation, mem_index * level_share, level_share, 0)
    weight = observed_count.astype(jnp.float32)[None] * precision[:, None, None]
    gradient = smooth(perturbed * (weight * local_innovation)[None])
    carried = jnp.zeros_like(gradient)
    residual = gradient
    direction = residual
    norm_now = norm_of(residual)
    for iteration in range(ITERS):
        smoothed = smooth(direction)
        total = member_total(perturbed * smoothed)
        back = smooth(perturbed * (weight * total)[None])
        image, smoothed = (direction + back, smoothed)
        step_size = norm_now / lax.psum(jnp.sum(direction * image), ("grid", "mem"))
        carried = carried + step_size * smoothed
        residual = residual - step_size * image
        if iteration + 1 < ITERS:
            norm_next = norm_of(residual)
            direction = residual + norm_next / norm_now * direction
            norm_now = norm_next
    increment = member_total(perturbed * carried)
    whole = lax.all_gather(increment, "mem", axis=0, tiled=True)
    recentred = (members.astype(jnp.float32) + whole[None]).astype(jnp.bfloat16)
    return (recentred, increment)


def solution(mesh):
    placed = (P("mem", None, "grid", None), P(None, "grid", None), P("grid", None), P())
    return jax.shard_map(
        local,
        mesh=mesh,
        in_specs=placed,
        out_specs=(P("mem", None, "grid", None), P("mem", "grid", None)),
        check_vma=False,
    )
```

profile of v0, /device:TPU:0, one launch (start us, length us, event | category | flops | bytes accessed | tf_op | source)
XLA Modules:
  0.0 294.0 jit_solution(12753605812569267372)
XLA Ops:
  2.3 4.3 %all-to-all-start = ((bf16[20,4,2,512]{3,2,0,1:T(2,128)(2,1)}), bf16[20,4,2,512]{3,2,0,1:T(2,128)(2,1)S(1)}, u32[]{:S(2)}, u32[]{:S(2)}) async-start(bf16[20,4,2,512]{3,2,0,1:T(2,128)(2,1)} %copy.7), calls=%async_computation | async-start | bytes 327680 | tf_op jit(solution)/shard_map/all_to_all | solution.py:48
  12.0 3.9 %collective-permute-start = (f32[80,1,1,512]{3,2,0,1:T(1,128)S(1)}, f32[80,1,1,512]{3,2,0,1:T(1,128)S(1)}, u32[]{:S(2)}, u32[]{:S(2)}) collective-permute-start(f32[80,1,1,512]{3,2,0,1:T(1,128)S(1)} %get-tuple-element.69), channel_id=1, source_target_pairs={{0,4},{4,8},{8,12},{12,16},{16,20},{20,24},{24,28},{1,5},{5,9},{9,... | collective-permute-start | bytes 491528 | tf_op jit(solution)/shard_map/ppermute | solution.py:20
  18.9 4.2 %collective-permute-done.1 = f32[80,1,1,512]{3,2,0,1:T(1,128)S(1)} collective-permute-done((f32[80,1,1,512]{3,2,0,1:T(1,128)S(1)}, f32[80,1,1,512]{3,2,0,1:T(1,128)S(1)}, u32[]{:S(2)}, u32[]{:S(2)}) %collective-permute-start.1) | collective-permute-done | bytes 163872 | tf_op jit(solution)/shard_map/ppermute | solution.py:21
  24.1 4.4 %collective-permute-start.2 = (f32[80,1,1,512]{3,2,0,1:T(1,128)S(1)}, f32[80,1,1,512]{3,2,0,1:T(1,128)S(1)}, u32[]{:S(2)}, u32[]{:S(2)}) collective-permute-start(f32[80,1,1,512]{3,2,0,1:T(1,128)S(1)} %get-tuple-element.67), channel_id=1, source_target_pairs={{0,4},{4,8},{8,12},{12,16},{16,20},{20,24},{24,28},{1,5},{5,9},{9,... | collective-permute-start | bytes 491528 | tf_op jit(solution)/shard_map/ppermute | solution.py:20
  31.3 4.5 %collective-permute-done.3 = f32[80,1,1,512]{3,2,0,1:T(1,128)S(1)} collective-permute-done((f32[80,1,1,512]{3,2,0,1:T(1,128)S(1)}, f32[80,1,1,512]{3,2,0,1:T(1,128)S(1)}, u32[]{:S(2)}, u32[]{:S(2)}) %collective-permute-start.3) | collective-permute-done | bytes 163872 | tf_op jit(solution)/shard_map/ppermute | solution.py:21
  39.7 4.5 %collective-permute-start.4 = (f32[80,1,1,512]{3,2,0,1:T(1,128)S(1)}, f32[80,1,1,512]{3,2,0,1:T(1,128)S(1)}, u32[]{:S(2)}, u32[]{:S(2)}) collective-permute-start(f32[80,1,1,512]{3,2,0,1:T(1,128)S(1)} %get-tuple-element.57), channel_id=1, source_target_pairs={{0,4},{4,8},{8,12},{12,16},{16,20},{20,24},{24,28},{1,5},{5,9},{9,... | collective-permute-start | bytes 491528 | tf_op jit(solution)/shard_map/ppermute | solution.py:20
  47.1 4.9 %collective-permute-done.5 = f32[80,1,1,512]{3,2,0,1:T(1,128)S(1)} collective-permute-done((f32[80,1,1,512]{3,2,0,1:T(1,128)S(1)}, f32[80,1,1,512]{3,2,0,1:T(1,128)S(1)}, u32[]{:S(2)}, u32[]{:S(2)}) %collective-permute-start.5) | collective-permute-done | bytes 163872 | tf_op jit(solution)/shard_map/ppermute | solution.py:21
  53.0 4.5 %collective-permute-start.6 = (f32[80,1,1,512]{3,2,0,1:T(1,128)S(1)}, f32[80,1,1,512]{3,2,0,1:T(1,128)S(1)}, u32[]{:S(2)}, u32[]{:S(2)}) collective-permute-start(f32[80,1,1,512]{3,2,0,1:T(1,128)S(1)} %get-tuple-element.55), channel_id=1, source_target_pairs={{0,4},{4,8},{8,12},{12,16},{16,20},{20,24},{24,28},{1,5},{5,9},{9,... | collective-permute-start | bytes 491528 | tf_op jit(solution)/shard_map/ppermute | solution.py:20
  60.3 5.1 %collective-permute-done.7 = f32[80,1,1,512]{3,2,0,1:T(1,128)S(1)} collective-permute-done((f32[80,1,1,512]{3,2,0,1:T(1,128)S(1)}, f32[80,1,1,512]{3,2,0,1:T(1,128)S(1)}, u32[]{:S(2)}, u32[]{:S(2)}) %collective-permute-start.7) | collective-permute-done | bytes 163872 | tf_op jit(solution)/shard_map/ppermute | solution.py:21
  70.1 4.5 %collective-permute-start.8 = (f32[80,1,1,512]{3,2,0,1:T(1,128)S(1)}, f32[80,1,1,512]{3,2,0,1:T(1,128)S(1)}, u32[]{:S(2)}, u32[]{:S(2)}) collective-permute-start(f32[80,1,1,512]{3,2,0,1:T(1,128)S(1)} %get-tuple-element.45), channel_id=1, source_target_pairs={{0,4},{4,8},{8,12},{12,16},{16,20},{20,24},{24,28},{1,5},{5,9},{9,... | collective-permute-start | bytes 491528 | tf_op jit(solution)/shard_map/ppermute | solution.py:20
  77.5 5.1 %collective-permute-done.9 = f32[80,1,1,512]{3,2,0,1:T(1,128)S(1)} collective-permute-done((f32[80,1,1,512]{3,2,0,1:T(1,128)S(1)}, f32[80,1,1,512]{3,2,0,1:T(1,128)S(1)}, u32[]{:S(2)}, u32[]{:S(2)}) %collective-permute-start.9) | collective-permute-done | bytes 163872 | tf_op jit(solution)/shard_map/ppermute | solution.py:21
  83.5 4.5 %collective-permute-start.10 = (f32[80,1,1,512]{3,2,0,1:T(1,128)S(1)}, f32[80,1,1,512]{3,2,0,1:T(1,128)S(1)}, u32[]{:S(2)}, u32[]{:S(2)}) collective-permute-start(f32[80,1,1,512]{3,2,0,1:T(1,128)S(1)} %get-tuple-element.43), channel_id=1, source_target_pairs={{0,4},{4,8},{8,12},{12,16},{16,20},{20,24},{24,28},{1,5},{5,9},{9,... | collective-permute-start | bytes 491528 | tf_op jit(solution)/shard_map/ppermute | solution.py:20
  90.9 5.1 %collective-permute-done.11 = f32[80,1,1,512]{3,2,0,1:T(1,128)S(1)} collective-permute-done((f32[80,1,1,512]{3,2,0,1:T(1,128)S(1)}, f32[80,1,1,512]{3,2,0,1:T(1,128)S(1)}, u32[]{:S(2)}, u32[]{:S(2)}) %collective-permute-start.11) | collective-permute-done | bytes 163872 | tf_op jit(solution)/shard_map/ppermute | solution.py:21
  100.5 41.8 %all-reduce = (f32[]{:T(128)}, f32[]{:T(128)}) all-reduce(f32[]{:T(128)} %get-tuple-element.3, f32[]{:T(128)} %get-tuple-element.2), channel_id=1, replica_groups=mesh['grid'=8,'mem'=4] {'grid','mem'}, use_global_device_ids=true, to_apply=%region_1.2 | all-reduce | flops 2 | bytes 16 | tf_op jit(solution)/shard_map/psum | solution.py:42
  144.6 40.8 %psum.30 = f32[]{:T(128)} all-reduce(f32[]{:T(128)} %multiply_reduce_fusion.2), channel_id=1, replica_groups=mesh['grid'=8,'mem'=4] {'grid','mem'}, use_global_device_ids=true, to_apply=%region_6.7 | all-reduce | flops 1 | bytes 8 | tf_op jit(solution)/shard_map/psum | solution.py:42
  187.2 4.2 %collective-permute-start.12 = (f32[80,1,1,512]{3,2,0,1:T(1,128)S(1)}, f32[80,1,1,512]{3,2,0,1:T(1,128)S(1)}, u32[]{:S(2)}, u32[]{:S(2)}) collective-permute-start(f32[80,1,1,512]{3,2,0,1:T(1,128)S(1)} %get-tuple-element.33), channel_id=1, source_target_pairs={{0,4},{4,8},{8,12},{12,16},{16,20},{20,24},{24,28},{1,5},{5,9},{9,... | collective-permute-start | bytes 491528 | tf_op jit(solution)/shard_map/ppermute | solution.py:20
  192.7 5.1 %collective-permute-done.12 = f32[80,1,1,512]{3,2,0,1:T(1,128)S(1)} collective-permute-done((f32[80,1,1,512]{3,2,0,1:T(1,128)S(1)}, f32[80,1,1,512]{3,2,0,1:T(1,128)S(1)}, u32[]{:S(2)}, u32[]{:S(2)}) %collective-permute-start.12) | collective-permute-done | bytes 163872 | tf_op jit(solution)/shard_map/ppermute | solution.py:20
  206.0 4.4 %collective-permute-done.15 = f32[80,1,1,512]{3,2,0,1:T(1,128)S(1)} collective-permute-done((f32[80,1,1,512]{3,2,0,1:T(1,128)S(1)}, f32[80,1,1,512]{3,2,0,1:T(1,128)S(1)}, u32[]{:S(2)}, u32[]{:S(2)}) %collective-permute-start.15) | collective-permute-done | bytes 163872 | tf_op jit(solution)/shard_map/ppermute | solution.py:21
  215.0 3.7 %collective-permute-start.16 = (f32[80,1,1,512]{3,2,0,1:T(1,128)S(1)}, f32[80,1,1,512]{3,2,0,1:T(1,128)S(1)}, u32[]{:S(2)}, u32[]{:S(2)}) collective-permute-start(f32[80,1,1,512]{3,2,0,1:T(1,128)S(1)} %get-tuple-element.21), channel_id=1, source_target_pairs={{0,4},{4,8},{8,12},{12,16},{16,20},{20,24},{24,28},{1,5},{5,9},{9,... | collective-permute-start | bytes 491528 | tf_op jit(solution)/shard_map/ppermute | solution.py:20
  221.6 4.4 %collective-permute-done.17 = f32[80,1,1,512]{3,2,0,1:T(1,128)S(1)} collective-permute-done((f32[80,1,1,512]{3,2,0,1:T(1,128)S(1)}, f32[80,1,1,512]{3,2,0,1:T(1,128)S(1)}, u32[]{:S(2)}, u32[]{:S(2)}) %collective-permute-start.17) | collective-permute-done | bytes 163872 | tf_op jit(solution)/shard_map/ppermute | solution.py:21
  227.0 4.4 %collective-permute-start.18 = (f32[80,1,1,512]{3,2,0,1:T(1,128)S(1)}, f32[80,1,1,512]{3,2,0,1:T(1,128)S(1)}, u32[]{:S(2)}, u32[]{:S(2)}) collective-permute-start(f32[80,1,1,512]{3,2,0,1:T(1,128)S(1)} %get-tuple-element.19), channel_id=1, source_target_pairs={{0,4},{4,8},{8,12},{12,16},{16,20},{20,24},{24,28},{1,5},{5,9},{9,... | collective-permute-start | bytes 491528 | tf_op jit(solution)/shard_map/ppermute | solution.py:20
  234.2 5.1 %collective-permute-done.19 = f32[80,1,1,512]{3,2,0,1:T(1,128)S(1)} collective-permute-done((f32[80,1,1,512]{3,2,0,1:T(1,128)S(1)}, f32[80,1,1,512]{3,2,0,1:T(1,128)S(1)}, u32[]{:S(2)}, u32[]{:S(2)}) %collective-permute-start.19) | collective-permute-done | bytes 163872 | tf_op jit(solution)/shard_map/ppermute | solution.py:21
  243.6 42.2 %psum.31 = f32[]{:T(128)} all-reduce(f32[]{:T(128)} %fusion), channel_id=1, replica_groups=mesh['grid'=8,'mem'=4] {'grid','mem'}, use_global_device_ids=true, to_apply=%region_9.10 | all-reduce | flops 1 | bytes 8 | tf_op jit(solution)/shard_map/psum | solution.py:62
  287.4 5.7 %all-gather.1 = f32[4,2,512]{2,1,0:T(2,128)S(1)} all-gather(f32[1,2,512]{2,1,0:T(2,128)S(1)} %bitcast.46), channel_id=2, replica_groups=mesh['grid'=8,'mem'=4] {'mem'}, dimensions={0}, use_global_device_ids=true | all-gather | bytes 20480 | tf_op jit(solution)/shard_map/all_gather | solution.py:70
  (96 shorter events, 67.5 us)
Async XLA Ops:
  2.3 9.2 %all-to-all-start = ((bf16[20,4,2,512]{3,2,0,1:T(2,128)(2,1)}), bf16[20,4,2,512]{3,2,0,1:T(2,128)(2,1)S(1)}, u32[]{:S(2)}, u32[]{:S(2)}) async-start(bf16[20,4,2,512]{3,2,0,1:T(2,128)(2,1)} %copy.7), calls=%async_computation | async-start | bytes 327680 | tf_op jit(solution)/shard_map/all_to_all | solution.py:48
  6.6 1.2 copy-start.1
  12.0 6.9 %collective-permute-start = (f32[80,1,1,512]{3,2,0,1:T(1,128)S(1)}, f32[80,1,1,512]{3,2,0,1:T(1,128)S(1)}, u32[]{:S(2)}, u32[]{:S(2)}) collective-permute-start(f32[80,1,1,512]{3,2,0,1:T(1,128)S(1)} %get-tuple-element.69), channel_id=1, source_target_pairs={{0,4},{4,8},{8,12},{12,16},{16,20},{20,24},{24,28},{1,5},{5,9},{9,... | collective-permute-start | bytes 491528 | tf_op jit(solution)/shard_map/ppermute | solution.py:20
  15.9 7.2 %collective-permute-start.1 = (f32[80,1,1,512]{3,2,0,1:T(1,128)S(1)}, f32[80,1,1,512]{3,2,0,1:T(1,128)S(1)}, u32[]{:S(2)}, u32[]{:S(2)}) collective-permute-start(f32[80,1,1,512]{3,2,0,1:T(1,128)S(1)} %get-tuple-element.70), channel_id=1, source_target_pairs={{4,0},{8,4},{12,8},{16,12},{20,16},{24,20},{28,24},{5,1},{9,5},{13... | collective-permute-start | bytes 491528 | tf_op jit(solution)/shard_map/ppermute | solution.py:21
  24.1 7.2 %collective-permute-start.2 = (f32[80,1,1,512]{3,2,0,1:T(1,128)S(1)}, f32[80,1,1,512]{3,2,0,1:T(1,128)S(1)}, u32[]{:S(2)}, u32[]{:S(2)}) collective-permute-start(f32[80,1,1,512]{3,2,0,1:T(1,128)S(1)} %get-tuple-element.67), channel_id=1, source_target_pairs={{0,4},{4,8},{8,12},{12,16},{16,20},{20,24},{24,28},{1,5},{5,9},{9,... | collective-permute-start | bytes 491528 | tf_op jit(solution)/shard_map/ppermute | solution.py:20
  28.5 7.3 %collective-permute-start.3 = (f32[80,1,1,512]{3,2,0,1:T(1,128)S(1)}, f32[80,1,1,512]{3,2,0,1:T(1,128)S(1)}, u32[]{:S(2)}, u32[]{:S(2)}) collective-permute-start(f32[80,1,1,512]{3,2,0,1:T(1,128)S(1)} %get-tuple-element.68), channel_id=1, source_target_pairs={{4,0},{8,4},{12,8},{16,12},{20,16},{24,20},{28,24},{5,1},{9,5},{13... | collective-permute-start | bytes 491528 | tf_op jit(solution)/shard_map/ppermute | solution.py:21
  39.7 7.4 %collective-permute-start.4 = (f32[80,1,1,512]{3,2,0,1:T(1,128)S(1)}, f32[80,1,1,512]{3,2,0,1:T(1,128)S(1)}, u32[]{:S(2)}, u32[]{:S(2)}) collective-permute-start(f32[80,1,1,512]{3,2,0,1:T(1,128)S(1)} %get-tuple-element.57), channel_id=1, source_target_pairs={{0,4},{4,8},{8,12},{12,16},{16,20},{20,24},{24,28},{1,5},{5,9},{9,... | collective-permute-start | bytes 491528 | tf_op jit(solution)/shard_map/ppermute | solution.py:20
  44.2 7.7 %collective-permute-start.5 = (f32[80,1,1,512]{3,2,0,1:T(1,128)S(1)}, f32[80,1,1,512]{3,2,0,1:T(1,128)S(1)}, u32[]{:S(2)}, u32[]{:S(2)}) collective-permute-start(f32[80,1,1,512]{3,2,0,1:T(1,128)S(1)} %get-tuple-element.58), channel_id=1, source_target_pairs={{4,0},{8,4},{12,8},{16,12},{20,16},{24,20},{28,24},{5,1},{9,5},{13... | collective-permute-start | bytes 491528 | tf_op jit(solution)/shard_map/ppermute | solution.py:21
  53.0 7.4 %collective-permute-start.6 = (f32[80,1,1,512]{3,2,0,1:T(1,128)S(1)}, f32[80,1,1,512]{3,2,0,1:T(1,128)S(1)}, u32[]{:S(2)}, u32[]{:S(2)}) collective-permute-start(f32[80,1,1,512]{3,2,0,1:T(1,128)S(1)} %get-tuple-element.55), channel_id=1, source_target_pairs={{0,4},{4,8},{8,12},{12,16},{16,20},{20,24},{24,28},{1,5},{5,9},{9,... | collective-permute-start | bytes 491528 | tf_op jit(solution)/shard_map/ppermute | solution.py:20
  57.5 7.9 %collective-permute-start.7 = (f32[80,1,1,512]{3,2,0,1:T(1,128)S(1)}, f32[80,1,1,512]{3,2,0,1:T(1,128)S(1)}, u32[]{:S(2)}, u32[]{:S(2)}) collective-permute-start(f32[80,1,1,512]{3,2,0,1:T(1,128)S(1)} %get-tuple-element.56), channel_id=1, source_target_pairs={{4,0},{8,4},{12,8},{16,12},{20,16},{24,20},{28,24},{5,1},{9,5},{13... | collective-permute-start | bytes 491528 | tf_op jit(solution)/shard_map/ppermute | solution.py:21
  70.1 7.4 %collective-permute-start.8 = (f32[80,1,1,512]{3,2,0,1:T(1,128)S(1)}, f32[80,1,1,512]{3,2,0,1:T(1,128)S(1)}, u32[]{:S(2)}, u32[]{:S(2)}) collective-permute-start(f32[80,1,1,512]{3,2,0,1:T(1,128)S(1)} %get-tuple-element.45), channel_id=1, source_target_pairs={{0,4},{4,8},{8,12},{12,16},{16,20},{20,24},{24,28},{1,5},{5,9},{9,... | collective-permute-start | bytes 491528 | tf_op jit(solution)/shard_map/ppermute | solution.py:20
  74.7 7.9 %collective-permute-start.9 = (f32[80,1,1,512]{3,2,0,1:T(1,128)S(1)}, f32[80,1,1,512]{3,2,0,1:T(1,128)S(1)}, u32[]{:S(2)}, u32[]{:S(2)}) collective-permute-start(f32[80,1,1,512]{3,2,0,1:T(1,128)S(1)} %get-tuple-element.46), channel_id=1, source_target_pairs={{4,0},{8,4},{12,8},{16,12},{20,16},{24,20},{28,24},{5,1},{9,5},{13... | collective-permute-start | bytes 491528 | tf_op jit(solution)/shard_map/ppermute | solution.py:21
  83.5 7.4 %collective-permute-start.10 = (f32[80,1,1,512]{3,2,0,1:T(1,128)S(1)}, f32[80,1,1,512]{3,2,0,1:T(1,128)S(1)}, u32[]{:S(2)}, u32[]{:S(2)}) collective-permute-start(f32[80,1,1,512]{3,2,0,1:T(1,128)S(1)} %get-tuple-element.43), channel_id=1, source_target_pairs={{0,4},{4,8},{8,12},{12,16},{16,20},{20,24},{24,28},{1,5},{5,9},{9,... | collective-permute-start | bytes 491528 | tf_op jit(solution)/shard_map/ppermute | solution.py:20
  88.1 7.9 %collective-permute-start.11 = (f32[80,1,1,512]{3,2,0,1:T(1,128)S(1)}, f32[80,1,1,512]{3,2,0,1:T(1,128)S(1)}, u32[]{:S(2)}, u32[]{:S(2)}) collective-permute-start(f32[80,1,1,512]{3,2,0,1:T(1,128)S(1)} %get-tuple-element.44), channel_id=1, source_target_pairs={{4,0},{8,4},{12,8},{16,12},{20,16},{24,20},{28,24},{5,1},{9,5},{13... | collective-permute-start | bytes 491528 | tf_op jit(solution)/shard_map/ppermute | solution.py:21
  187.2 10.6 %collective-permute-start.12 = (f32[80,1,1,512]{3,2,0,1:T(1,128)S(1)}, f32[80,1,1,512]{3,2,0,1:T(1,128)S(1)}, u32[]{:S(2)}, u32[]{:S(2)}) collective-permute-start(f32[80,1,1,512]{3,2,0,1:T(1,128)S(1)} %get-tuple-element.33), channel_id=1, source_target_pairs={{0,4},{4,8},{8,12},{12,16},{16,20},{20,24},{24,28},{1,5},{5,9},{9,... | collective-permute-start | bytes 491528 | tf_op jit(solution)/shard_map/ppermute | solution.py:20
  191.4 7.2 %collective-permute-start.13 = (f32[80,1,1,512]{3,2,0,1:T(1,128)S(1)}, f32[80,1,1,512]{3,2,0,1:T(1,128)S(1)}, u32[]{:S(2)}, u32[]{:S(2)}) collective-permute-start(f32[80,1,1,512]{3,2,0,1:T(1,128)S(1)} %get-tuple-element.34), channel_id=1, source_target_pairs={{4,0},{8,4},{12,8},{16,12},{20,16},{24,20},{28,24},{5,1},{9,5},{13... | collective-permute-start | bytes 491528 | tf_op jit(solution)/shard_map/ppermute | solution.py:21
  199.6 6.4 %collective-permute-start.14 = (f32[80,1,1,512]{3,2,0,1:T(1,128)S(1)}, f32[80,1,1,512]{3,2,0,1:T(1,128)S(1)}, u32[]{:S(2)}, u32[]{:S(2)}) collective-permute-start(f32[80,1,1,512]{3,2,0,1:T(1,128)S(1)} %get-tuple-element.31), channel_id=1, source_target_pairs={{0,4},{4,8},{8,12},{12,16},{16,20},{20,24},{24,28},{1,5},{5,9},{9,... | collective-permute-start | bytes 491528 | tf_op jit(solution)/shard_map/ppermute | solution.py:20
  203.1 7.2 %collective-permute-start.15 = (f32[80,1,1,512]{3,2,0,1:T(1,128)S(1)}, f32[80,1,1,512]{3,2,0,1:T(1,128)S(1)}, u32[]{:S(2)}, u32[]{:S(2)}) collective-permute-start(f32[80,1,1,512]{3,2,0,1:T(1,128)S(1)} %get-tuple-element.32), channel_id=1, source_target_pairs={{4,0},{8,4},{12,8},{16,12},{20,16},{24,20},{28,24},{5,1},{9,5},{13... | collective-permute-start | bytes 491528 | tf_op jit(solution)/shard_map/ppermute | solution.py:21
  215.0 6.5 %collective-permute-start.16 = (f32[80,1,1,512]{3,2,0,1:T(1,128)S(1)}, f32[80,1,1,512]{3,2,0,1:T(1,128)S(1)}, u32[]{:S(2)}, u32[]{:S(2)}) collective-permute-start(f32[80,1,1,512]{3,2,0,1:T(1,128)S(1)} %get-tuple-element.21), channel_id=1, source_target_pairs={{0,4},{4,8},{8,12},{12,16},{16,20},{20,24},{24,28},{1,5},{5,9},{9,... | collective-permute-start | bytes 491528 | tf_op jit(solution)/shard_map/ppermute | solution.py:20
  218.8 7.2 %collective-permute-start.17 = (f32[80,1,1,512]{3,2,0,1:T(1,128)S(1)}, f32[80,1,1,512]{3,2,0,1:T(1,128)S(1)}, u32[]{:S(2)}, u32[]{:S(2)}) collective-permute-start(f32[80,1,1,512]{3,2,0,1:T(1,128)S(1)} %get-tuple-element.22), channel_id=1, source_target_pairs={{4,0},{8,4},{12,8},{16,12},{20,16},{24,20},{28,24},{5,1},{9,5},{13... | collective-permute-start | bytes 491528 | tf_op jit(solution)/shard_map/ppermute | solution.py:21
  227.0 7.2 %collective-permute-start.18 = (f32[80,1,1,512]{3,2,0,1:T(1,128)S(1)}, f32[80,1,1,512]{3,2,0,1:T(1,128)S(1)}, u32[]{:S(2)}, u32[]{:S(2)}) collective-permute-start(f32[80,1,1,512]{3,2,0,1:T(1,128)S(1)} %get-tuple-element.19), channel_id=1, source_target_pairs={{0,4},{4,8},{8,12},{12,16},{16,20},{20,24},{24,28},{1,5},{5,9},{9,... | collective-permute-start | bytes 491528 | tf_op jit(solution)/shard_map/ppermute | solution.py:20
  231.4 7.9 %collective-permute-start.19 = (f32[80,1,1,512]{3,2,0,1:T(1,128)S(1)}, f32[80,1,1,512]{3,2,0,1:T(1,128)S(1)}, u32[]{:S(2)}, u32[]{:S(2)}) collective-permute-start(f32[80,1,1,512]{3,2,0,1:T(1,128)S(1)} %get-tuple-element.20), channel_id=1, source_target_pairs={{4,0},{8,4},{12,8},{16,12},{20,16},{24,20},{28,24},{5,1},{9,5},{13... | collective-permute-start | bytes 491528 | tf_op jit(solution)/shard_map/ppermute | solution.py:21
  287.1 6.0 %copy-start = (bf16[20,4,2,512]{3,2,1,0:T(2,128)(2,1)S(1)}, bf16[20,4,2,512]{3,2,1,0:T(2,128)(2,1)}, u32[]{:S(2)}) copy-start(bf16[20,4,2,512]{3,2,1,0:T(2,128)(2,1)} %param.4) | copy-start | bytes 491524
  287.4 5.7 %copy-start.2 = (f32[2,512]{1,0:T(2,128)}, f32[2,512]{1,0:T(2,128)S(1)}, u32[]{:S(2)}) copy-start(f32[2,512]{1,0:T(2,128)S(1)} %multiply_reduce_fusion) | copy-start | bytes 12292
  (1 other events, 0.7 us)
where the time goes:
time: 295 us; the launch traced here: 294 us
  blocking collectives  131 us (44%)
  waiting for transfers between devices  64.3 us (22%)
  starting transfers between devices  59.9 us (20%)
  other arithmetic  23 us (8%)
  local copies, waits for them, and re-layouts  11.1 us (4%)
  between operations  5.15 us (2%)
    psum x2, blocking collectives, norm_of(): return lax.psum(jnp.sum(residual * residual), ('grid', 'mem'))  82.7 us
    ppermute x10, waiting for transfers between devices, padded(): after = lax.ppermute(leading, axis, down)  43.5 us
    ppermute x10, starting transfers between devices, padded(): before = lax.ppermute(last, axis, up)  42.3 us
    psum x1, blocking collectives, local(): step_size = norm_now / lax.psum(jnp.sum(direction * image), ('grid', 'mem'))  42.2 us
    ppermute x10, waiting for transfers between devices, padded(): before = lax.ppermute(last, axis, up)  18.5 us
    ppermute x10, starting transfers between devices, padded(): after = lax.ppermute(leading, axis, down)  13.3 us
    add x10, other arithmetic, smooth(): centre + diffusion * (extended[:, :, :-2] + extended[:, :, 2:] - 2.0 * ce...  7.27 us
    add x6, other arithmetic, smooth(): field + diffusion * (jnp.roll(field, 1, 3) + jnp.roll(field, -1, 3) - 2.0...  6.6 us
  transfers between devices with their start and end apart: 21, of which 21 were waited for; matrix products, arithmetic and copies ran while one was open for 1% of the time, Pallas kernels for 0%

commit v1 on v0

--- a/solution.py
+++ b/solution.py
@@ -72,12 +72,99 @@
     return (recentred, increment)
 
 
+def smooth_rows(field):
+    for sweep_index in range(PASSES):
+        edge = jnp.zeros_like(field[..., :1, :])
+        north = jnp.concatenate([edge, field[..., :-1, :]], axis=-2)
+        south = jnp.concatenate([field[..., 1:, :], edge], axis=-2)
+        field = field + diffusion * (north + south - 2.0 * field)
+    for sweep_index in range(PASSES):
+        field = field + diffusion * (jnp.roll(field, 1, -1) + jnp.roll(field, -1, -1) - 2.0 * field)
+    return field
+
+
+def all_sum(values):
+    devices = lax.axis_size("grid") * lax.axis_size("mem")
+    row = jnp.zeros((128,), jnp.float32).at[: values.shape[0]].set(values)
+    gathered = lax.all_to_all(jnp.broadcast_to(row, (devices, 128)), ("grid", "mem"), 0, 0, tiled=True)
+    return jnp.sum(gathered, axis=0)
+
+
+def local_by_level(members, innovation, observed_count, obs_precision):
+    grid_size = lax.axis_size("grid")
+    mem_size = lax.axis_size("mem")
+    count, levels, rows, nlon = members.shape
+    copies = grid_size // levels
+    nlat = rows * grid_size
+    grid_index = lax.axis_index("grid")
+    mem_index = lax.axis_index("mem")
+    level = grid_index // copies
+    chunk_level = [j // copies for j in range(grid_size)]
+
+    sent = jnp.stack([members[:, l] for l in chunk_level], axis=0)
+    got = lax.all_to_all(sent, "grid", 0, 0, tiled=True)
+    mine = jnp.transpose(got, (1, 0, 2, 3)).reshape(count, nlat, nlon)
+    extra = jnp.stack(
+        [jnp.stack([innovation[l], observed_count.astype(jnp.float32)]) for l in chunk_level], axis=0
+    )
+    extra = lax.all_to_all(extra, "grid", 0, 0, tiled=True)
+    extra = jnp.transpose(extra, (1, 0, 2, 3)).reshape(2, nlat, nlon)
+    precision = lax.dynamic_index_in_dim(obs_precision, level, 0, keepdims=False)
+    weight = extra[1] * precision
+    widened = mine.astype(jnp.float32)
+
+    span = nlat // copies
+    own = (lax.broadcasted_iota(jnp.int32, (nlat, nlon), 0) // span) == grid_index % copies
+    first = mem_index == 0
+
+    def squares(field):
+        return jnp.sum(jnp.where(own[None], field * field, 0.0))
+
+    def weighted(total):
+        return jnp.where(first, jnp.sum(jnp.where(own, weight * total * total, 0.0)), 0.0)
+
+    def project(field):
+        return lax.psum(jnp.sum(widened * field, axis=0), "mem")
+
+    residual = smooth_rows(widened * (weight * extra[0])[None])
+    total1 = project(smooth_rows(residual))
+    image = residual + smooth_rows(widened * (weight * total1)[None])
+    projected_image = project(smooth_rows(image))
+    first_sums = all_sum(jnp.stack([squares(residual), weighted(total1)]))
+    norm_now = first_sums[0]
+    step1 = norm_now / (norm_now + first_sums[1])
+    residual_next = residual - step1 * image
+    norm_next = all_sum(jnp.stack([squares(residual_next)]))[0]
+    beta = norm_next / norm_now
+    direction = residual_next + beta * residual
+    total2 = (total1 - step1 * projected_image) + beta * total1
+    second_sums = all_sum(jnp.stack([squares(direction), weighted(total2)]))
+    step2 = norm_next / (second_sums[0] + second_sums[1])
+    increment = step1 * total1 + step2 * total2
+
+    spread = lax.all_to_all(increment.reshape(grid_size, rows, nlon), "grid", 0, 0, tiled=True)
+    whole = spread.reshape(levels, copies, rows, nlon)[:, 0]
+    share = levels // mem_size
+    mine_out = lax.dynamic_slice_in_dim(whole, mem_index * share, share, 0)
+    recentred = (members.astype(jnp.float32) + whole[None]).astype(jnp.bfloat16)
+    return (recentred, mine_out)
+
+
 def solution(mesh):
     placed = (P("mem", None, "grid", None), P(None, "grid", None), P("grid", None), P())
-    return jax.shard_map(
-        local,
-        mesh=mesh,
-        in_specs=placed,
-        out_specs=(P("mem", None, "grid", None), P("mem", "grid", None)),
-        check_vma=False,
-    )
+    grid_size, mem_size = mesh.shape["grid"], mesh.shape["mem"]
+    body = local
+
+    def chosen(members, innovation, observed_count, obs_precision):
+        levels = members.shape[1]
+        fits = grid_size % levels == 0 and grid_size // levels <= 2 and levels % mem_size == 0 and ITERS == 2
+        pick = local_by_level if fits else body
+        return jax.shard_map(
+            pick,
+            mesh=mesh,
+            in_specs=placed,
+            out_specs=(P("mem", None, "grid", None), P("mem", "grid", None)),
+            check_vma=False,
+        )(members, innovation, observed_count, obs_precision)
+
+    return chosen

time: 295 us -> 123 us (0.42)
  blocking collectives: 131 us -> 29.6 us
  starting transfers between devices: 59.9 us -> 21.2 us
  waiting for transfers between devices: 64.3 us -> 26.8 us
  local copies, waits for them, and re-layouts: 11.1 us -> 19.1 us
  other arithmetic: 23 us -> 19.5 us
    psum x3 -> x2, blocking collectives: 125 us -> 20.7 us  [project(): return lax.psum(jnp.sum(widened * field, axis=0), 'mem')]
    ppermute x20 -> x0, waiting for transfers between devices: 61.9 us -> none  [the longest x10 43.5 us: padded(): after = lax.ppermute(leading, axis, down)]
    ppermute x20 -> x0, starting transfers between devices: 55.6 us -> none  [the longest x10 42.3 us: padded(): before = lax.ppermute(last, axis, up)]
    all_to_all x1 -> x5, waiting for transfers between devices: 2.37 us -> 26.8 us  [the longest x2 10.7 us: all_sum(): lax.all_to_all(jnp.broadcast_to(row, (devices, 128)), ('grid', 'mem'), 0,...]
    all_to_all x1 -> x5, starting transfers between devices: 4.26 us -> 21.2 us  [the longest x1 7.28 us: local_by_level(): extra = lax.all_to_all(extra, 'grid', 0, 0, tiled=True)]
    add x17 -> x12, other arithmetic: 13.9 us -> 4.32 us  [the longest x4 2.47 us: smooth_rows(): field + diffusion * (jnp.roll(field, 1, -1) + jnp.roll(field, -1, -1) - 2...]
    all_to_all x0 -> x1, blocking collectives: none -> 8.95 us  [all_sum(): lax.all_to_all(jnp.broadcast_to(row, (devices, 128)), ('grid', 'mem'), 0,...]
    all_gather x1 -> x0, blocking collectives: 5.74 us -> none  [local(): whole = lax.all_gather(increment, 'mem', axis=0, tiled=True)]
  transfers between devices with their start and end apart: 21 -> 5, of which waited for: 21 -> 5; matrix products, arithmetic and copies ran while one was open for 1% -> 8% of each run, Pallas kernels for 0% -> 0%
where the time goes in v1:
time: 123 us; the launch traced here: 122 us
  blocking collectives  29.6 us (24%)
  waiting for transfers between devices  26.8 us (22%)
  starting transfers between devices  21.2 us (17%)
  other arithmetic  19.5 us (16%)
  local copies, waits for them, and re-layouts  19.1 us (16%)
  between operations  5.99 us (5%)
    psum x2, blocking collectives, project(): return lax.psum(jnp.sum(widened * field, axis=0), 'mem')  20.7 us
    all_to_all x2, waiting for transfers between devices, all_sum(): lax.all_to_all(jnp.broadcast_to(row, (devices, 128)), ('grid', 'mem'), 0,...  10.7 us
    all_to_all x1, blocking collectives, all_sum(): lax.all_to_all(jnp.broadcast_to(row, (devices, 128)), ('grid', 'mem'), 0,...  8.95 us
    all_to_all x1, waiting for transfers between devices, local_by_level(): got = lax.all_to_all(sent, 'grid', 0, 0, tiled=True)  7.6 us
    all_to_all x1, starting transfers between devices, local_by_level(): extra = lax.all_to_all(extra, 'grid', 0, 0, tiled=True)  7.28 us
    all_to_all x1, waiting for transfers between devices, local_by_level(): lax.all_to_all(increment.reshape(grid_size, rows, nlon), 'grid', 0, 0, ti...  6.62 us
    all_to_all x2, starting transfers between devices, all_sum(): lax.all_to_all(jnp.broadcast_to(row, (devices, 128)), ('grid', 'mem'), 0,...  6.33 us
    unnamed x11, local copies, waits for them, and re-layouts  5.14 us
  transfers between devices with their start and end apart: 5, of which 5 were waited for; matrix products, arithmetic and copies ran while one was open for 8% of the time, Pallas kernels for 0%

profile of v1, /device:TPU:0, one launch (start us, length us, event | category | flops | bytes accessed | tf_op | source)
XLA Modules:
  0.0 122.1 jit_solution(157087438368064626)
XLA Ops:
  0.6 0.7 convert_bitcast_fusion.1
  1.4 0.7 fusion.63
  6.9 7.3 %all-to-all-start.1 = ((f32[8,2,2,512]{3,2,1,0:T(2,128)}), f32[8,2,2,512]{3,2,1,0:T(2,128)S(1)}, u32[]{:S(2)}, u32[]{:S(2)}) async-start(f32[8,2,2,512]{3,2,1,0:T(2,128)} %constant_dynamic-update-slice_fusion), calls=%async_computation.1 | async-start | bytes 131072 | tf_op jit(solution)/shard_map/all_to_all | solution.py:110
  19.3 1.8 %all-to-all-done.1 = f32[8,2,2,512]{3,2,1,0:T(2,128)S(1)} async-done(((f32[8,2,2,512]{3,2,1,0:T(2,128)}), f32[8,2,2,512]{3,2,1,0:T(2,128)S(1)}, u32[]{:S(2)}, u32[]{:S(2)}) %all-to-all-start.1) | async-done | bytes 65568 | tf_op jit(solution)/shard_map/all_to_all | solution.py:110
  21.1 4.2 %all-to-all-start = ((bf16[8,20,2,512]{3,2,1,0:T(2,128)(2,1)}), bf16[8,20,2,512]{3,2,1,0:T(2,128)(2,1)S(1)}, u32[]{:S(2)}, u32[]{:S(2)}) async-start(bf16[8,20,2,512]{3,2,1,0:T(2,128)(2,1)} %bitcast_dynamic-update-slice_fusion.1), calls=%async_computation | async-start | bytes 655360 | tf_op jit(solution)/shard_map/all_to_all | solution.py:105
  27.4 7.6 %all-to-all-done = bf16[8,20,2,512]{3,2,1,0:T(2,128)(2,1)S(1)} async-done(((bf16[8,20,2,512]{3,2,1,0:T(2,128)(2,1)}), bf16[8,20,2,512]{3,2,1,0:T(2,128)(2,1)S(1)}, u32[]{:S(2)}, u32[]{:S(2)}) %all-to-all-start) | async-done | bytes 327712 | tf_op jit(solution)/shard_map/all_to_all | solution.py:105
  38.1 0.9 select_reduce_fusion.2
  41.3 10.3 %psum.14 = f32[16,512]{1,0:T(8,128)S(1)} all-reduce(f32[16,512]{1,0:T(8,128)S(1)} %fusion.13), channel_id=1, replica_groups=mesh['grid'=8,'mem'=4] {'mem'}, use_global_device_ids=true, to_apply=%region_2.3 | all-reduce | flops 8192 | bytes 65536 | tf_op jit(solution)/shard_map/psum | solution.py:127
  53.1 0.8 fusion.46
  53.9 1.1 fusion.45
  56.9 3.8 %all-to-all-start.2 = ((f32[32,1,128]{2,1,0:T(1,128)}), f32[32,1,128]{2,1,0:T(1,128)S(1)}, u32[]{:S(2)}, u32[]{:S(2)}) async-start(f32[32,1,128]{2,1,0:T(1,128)} %broadcast_in_dim.42), calls=%async_computation.2 | async-start | bytes 32768 | tf_op jit(solution)/shard_map/all_to_all | solution.py:89
  60.7 1.5 %fusion.16 = f32[20,16,512]{2,1,0:T(8,128)S(1)} fusion(f32[20,16,512]{2,1,0:T(8,128)S(1)} %multiply_add_fusion.2, f32[20,16,511]{2,1,0:T(8,128)} %get-tuple-element.63, f32[20,16,1]{2,1,0:T(8,128)} %get-tuple-element.65, f32[20,16,1]{2,1,0:T(8,128)} %get-tuple-element.64, f32[20,16,511]{2,1,0:T(8,128)S(1)} %get-tuple-element.62), kind=kLoop, calls=%fused_computation.21 | loop fusion | flops 1146880 | bytes 2621440 | tf_op jit(solution)/shard_map/add | solution.py:82
  62.2 1.1 fusion.44
  63.3 0.8 fusion.43
  64.1 3.8 %all-to-all-done.2 = f32[32,1,128]{2,1,0:T(1,128)S(1)} async-done(((f32[32,1,128]{2,1,0:T(1,128)}), f32[32,1,128]{2,1,0:T(1,128)S(1)}, u32[]{:S(2)}, u32[]{:S(2)}) %all-to-all-start.2) | async-done | bytes 16416 | tf_op jit(solution)/shard_map/all_to_all | solution.py:89
  70.2 2.1 %select_reduce_fusion.1 = (f32[]{:T(128)}, f32[20,16,512]{2,1,0:T(8,128)S(1)}) fusion(f32[20,16,512]{2,1,0:T(8,128)S(1)} %get-tuple-element.41, f32[]{:T(128)S(6)} %div.31, pred[16,512]{1,0:T(8,128)(4,1)S(1)} %select_compare_fusion, f32[20,16,512]{2,1,0:T(8,128)S(1)} %fusion.16, f32[20,16,1]{2,1,0:T(8,128)} %get-tuple-element.59, ...), kind=kLoop, calls=%fused_computation.41 | loop fusion | flops 2129919 | bytes 3285000 | tf_op jit(solution)/shard_map/reduce_sum | solution.py:121
  73.6 2.5 %all-to-all-start.3 = ((f32[32,1,128]{2,1,0:T(1,128)}), f32[32,1,128]{2,1,0:T(1,128)S(1)}, u32[]{:S(2)}, u32[]{:S(2)}) async-start(f32[32,1,128]{2,1,0:T(1,128)} %broadcast_in_dim.43), calls=%async_computation.3 | async-start | bytes 32768 | tf_op jit(solution)/shard_map/all_to_all | solution.py:89
  76.3 7.0 %all-to-all-done.3 = f32[32,1,128]{2,1,0:T(1,128)S(1)} async-done(((f32[32,1,128]{2,1,0:T(1,128)}), f32[32,1,128]{2,1,0:T(1,128)S(1)}, u32[]{:S(2)}, u32[]{:S(2)}) %all-to-all-start.3) | async-done | bytes 16416 | tf_op jit(solution)/shard_map/all_to_all | solution.py:89
  83.9 0.9 select_reduce_fusion
  86.7 10.4 %psum.15 = f32[16,512]{1,0:T(8,128)S(1)} all-reduce(f32[16,512]{1,0:T(8,128)S(1)} %fusion.28), channel_id=1, replica_groups=mesh['grid'=8,'mem'=4] {'mem'}, use_global_device_ids=true, to_apply=%region_9.10 | all-reduce | flops 8192 | bytes 65536 | tf_op jit(solution)/shard_map/psum | solution.py:127
  99.2 8.9 %all_to_all.33 = f32[32,1,128]{2,1,0:T(1,128)S(1)} all-to-all(f32[32,1,128]{2,1,0:T(1,128)S(1)} %broadcast_in_dim.44), channel_id=1, replica_groups=mesh['grid'=8,'mem'=4] {'grid','mem'}, dimensions={0} | all-to-all | bytes 32768 | tf_op jit(solution)/shard_map/all_to_all | solution.py:89
  110.7 3.3 %all-to-all-start.5 = ((f32[8,2,512]{2,1,0:T(2,128)}), f32[8,2,512]{2,1,0:T(2,128)S(1)}, u32[]{:S(2)}, u32[]{:S(2)}) async-start(f32[8,2,512]{2,1,0:T(2,128)} %reshape.159), calls=%async_computation.5 | async-start | bytes 65536 | tf_op jit(solution)/shard_map/all_to_all | solution.py:145
  114.1 6.6 %all-to-all-done.5 = f32[8,2,512]{2,1,0:T(2,128)S(1)} async-done(((f32[8,2,512]{2,1,0:T(2,128)}), f32[8,2,512]{2,1,0:T(2,128)S(1)}, u32[]{:S(2)}, u32[]{:S(2)}) %all-to-all-start.5) | async-done | bytes 32800 | tf_op jit(solution)/shard_map/all_to_all | solution.py:145
  120.7 0.8 add_convert_fusion
  (82 shorter events, 27.1 us)
Async XLA Ops:
  0.6 13.6 %copy-start = (bf16[20,4,2,512]{3,2,1,0:T(2,128)(2,1)S(1)}, bf16[20,4,2,512]{3,2,1,0:T(2,128)(2,1)}, u32[]{:S(2)}) copy-start(bf16[20,4,2,512]{3,2,1,0:T(2,128)(2,1)} %param.10) | copy-start | bytes 491524
  6.9 14.2 %all-to-all-start.1 = ((f32[8,2,2,512]{3,2,1,0:T(2,128)}), f32[8,2,2,512]{3,2,1,0:T(2,128)S(1)}, u32[]{:S(2)}, u32[]{:S(2)}) async-start(f32[8,2,2,512]{3,2,1,0:T(2,128)} %constant_dynamic-update-slice_fusion), calls=%async_computation.1 | async-start | bytes 131072 | tf_op jit(solution)/shard_map/all_to_all | solution.py:110
  21.1 13.9 %all-to-all-start = ((bf16[8,20,2,512]{3,2,1,0:T(2,128)(2,1)}), bf16[8,20,2,512]{3,2,1,0:T(2,128)(2,1)S(1)}, u32[]{:S(2)}, u32[]{:S(2)}) async-start(bf16[8,20,2,512]{3,2,1,0:T(2,128)(2,1)} %bitcast_dynamic-update-slice_fusion.1), calls=%async_computation | async-start | bytes 655360 | tf_op jit(solution)/shard_map/all_to_all | solution.py:105
  25.4 0.7 copy-start.1
  56.9 11.0 %all-to-all-start.2 = ((f32[32,1,128]{2,1,0:T(1,128)}), f32[32,1,128]{2,1,0:T(1,128)S(1)}, u32[]{:S(2)}, u32[]{:S(2)}) async-start(f32[32,1,128]{2,1,0:T(1,128)} %broadcast_in_dim.42), calls=%async_computation.2 | async-start | bytes 32768 | tf_op jit(solution)/shard_map/all_to_all | solution.py:89
  73.6 9.7 %all-to-all-start.3 = ((f32[32,1,128]{2,1,0:T(1,128)}), f32[32,1,128]{2,1,0:T(1,128)S(1)}, u32[]{:S(2)}, u32[]{:S(2)}) async-start(f32[32,1,128]{2,1,0:T(1,128)} %broadcast_in_dim.43), calls=%async_computation.3 | async-start | bytes 32768 | tf_op jit(solution)/shard_map/all_to_all | solution.py:89
  110.7 10.0 %all-to-all-start.5 = ((f32[8,2,512]{2,1,0:T(2,128)}), f32[8,2,512]{2,1,0:T(2,128)S(1)}, u32[]{:S(2)}, u32[]{:S(2)}) async-start(f32[8,2,512]{2,1,0:T(2,128)} %reshape.159), calls=%async_computation.5 | async-start | bytes 65536 | tf_op jit(solution)/shard_map/all_to_all | solution.py:145

commit v2 on v1

--- a/solution.py
+++ b/solution.py
@@ -83,11 +83,13 @@
     return field
 
 
-def all_sum(values):
+def exchange(values, rows_for):
     devices = lax.axis_size("grid") * lax.axis_size("mem")
-    row = jnp.zeros((128,), jnp.float32).at[: values.shape[0]].set(values)
-    gathered = lax.all_to_all(jnp.broadcast_to(row, (devices, 128)), ("grid", "mem"), 0, 0, tiled=True)
-    return jnp.sum(gathered, axis=0)
+    nlon = rows_for.shape[-1]
+    head = jnp.zeros((nlon,), jnp.float32).at[: values.shape[0]].set(values)
+    head = jnp.broadcast_to(head, (devices, 1, nlon))
+    parcel = jnp.concatenate([head, rows_for], axis=1)
+    return lax.all_to_all(parcel, ("grid", "mem"), 0, 0, tiled=True)
 
 
 def local_by_level(members, innovation, observed_count, obs_precision):
@@ -99,19 +101,14 @@
     grid_index = lax.axis_index("grid")
     mem_index = lax.axis_index("mem")
     level = grid_index // copies
-    chunk_level = [j // copies for j in range(grid_size)]
 
-    sent = jnp.stack([members[:, l] for l in chunk_level], axis=0)
-    got = lax.all_to_all(sent, "grid", 0, 0, tiled=True)
-    mine = jnp.transpose(got, (1, 0, 2, 3)).reshape(count, nlat, nlon)
-    extra = jnp.stack(
-        [jnp.stack([innovation[l], observed_count.astype(jnp.float32)]) for l in chunk_level], axis=0
-    )
-    extra = lax.all_to_all(extra, "grid", 0, 0, tiled=True)
-    extra = jnp.transpose(extra, (1, 0, 2, 3)).reshape(2, nlat, nlon)
+    counts = jnp.broadcast_to(observed_count.astype(jnp.bfloat16), (1, levels, rows, nlon))
+    packed = jnp.repeat(jnp.concatenate([members, counts], axis=0), copies, axis=1)
+    got = lax.all_to_all(packed, "grid", 1, 2, tiled=True)[:, 0]
+    innov = lax.all_to_all(jnp.repeat(innovation, copies, axis=0), "grid", 0, 1, tiled=True)[0]
     precision = lax.dynamic_index_in_dim(obs_precision, level, 0, keepdims=False)
-    weight = extra[1] * precision
-    widened = mine.astype(jnp.float32)
+    weight = got[count].astype(jnp.float32) * precision
+    widened = got[:count].astype(jnp.float32)
 
     span = nlat // copies
     own = (lax.broadcasted_iota(jnp.int32, (nlat, nlon), 0) // span) == grid_index % copies
@@ -123,27 +120,33 @@
     def weighted(total):
         return jnp.where(first, jnp.sum(jnp.where(own, weight * total * total, 0.0)), 0.0)
 
-    def project(field):
-        return lax.psum(jnp.sum(widened * field, axis=0), "mem")
+    def by_target(field):
+        return jnp.repeat(field.reshape(grid_size, rows, nlon), mem_size, axis=0)
 
-    residual = smooth_rows(widened * (weight * extra[0])[None])
-    total1 = project(smooth_rows(residual))
+    residual = smooth_rows(widened * (weight * innov)[None])
+    total1 = lax.psum(jnp.sum(widened * smooth_rows(residual), axis=0), "mem")
     image = residual + smooth_rows(widened * (weight * total1)[None])
-    projected_image = project(smooth_rows(image))
-    first_sums = all_sum(jnp.stack([squares(residual), weighted(total1)]))
-    norm_now = first_sums[0]
-    step1 = norm_now / (norm_now + first_sums[1])
+    image_part = jnp.sum(widened * smooth_rows(image), axis=0)
+
+    got1 = exchange(jnp.stack([squares(residual), weighted(total1)]), by_target(total1))
+    norm_now = jnp.sum(got1[:, 0, 0])
+    step1 = norm_now / (norm_now + jnp.sum(got1[:, 0, 1]))
+    total1_rows = got1.reshape(levels, copies * mem_size, 1 + rows, nlon)[:, 0, 1:]
+
     residual_next = residual - step1 * image
-    norm_next = all_sum(jnp.stack([squares(residual_next)]))[0]
+    got2 = exchange(jnp.stack([squares(residual_next)]), by_target(image_part))
+    norm_next = jnp.sum(got2[:, 0, 0])
     beta = norm_next / norm_now
+    image_rows = jnp.sum(got2.reshape(levels, copies, mem_size, 1 + rows, nlon)[:, 0, :, 1:], axis=1)
+
     direction = residual_next + beta * residual
-    total2 = (total1 - step1 * projected_image) + beta * total1
-    second_sums = all_sum(jnp.stack([squares(direction), weighted(total2)]))
-    step2 = norm_next / (second_sums[0] + second_sums[1])
-    increment = step1 * total1 + step2 * total2
+    weight_rows = observed_count.astype(jnp.float32)[None] * obs_precision[:, None, None]
+    total2_rows = (total1_rows - step1 * image_rows) + beta * total1_rows
+    q2 = jnp.where(first, jnp.sum(weight_rows * total2_rows * total2_rows), 0.0)
+    got3 = exchange(jnp.stack([squares(direction), q2]), jnp.zeros((grid_size * mem_size, 0, nlon), jnp.float32))
+    step2 = norm_next / (jnp.sum(got3[:, 0, 0]) + jnp.sum(got3[:, 0, 1]))
+    whole = step1 * total1_rows + step2 * total2_rows
 
-    spread = lax.all_to_all(increment.reshape(grid_size, rows, nlon), "grid", 0, 0, tiled=True)
-    whole = spread.reshape(levels, copies, rows, nlon)[:, 0]
     share = levels // mem_size
     mine_out = lax.dynamic_slice_in_dim(whole, mem_index * share, share, 0)
     recentred = (members.astype(jnp.float32) + whole[None]).astype(jnp.bfloat16)

time: 123 us -> 111 us (0.902)
  blocking collectives: 29.6 us -> 23 us
  local copies, waits for them, and re-layouts: 19.1 us -> 13.7 us
  starting transfers between devices: 21.2 us -> 17.3 us
  between operations: 5.99 us -> 7.61 us
  waiting for transfers between devices: 26.8 us -> 28.1 us
    psum x2 -> x1, blocking collectives: 20.7 us -> 10.3 us  [local_by_level(): total1 = lax.psum(jnp.sum(widened * smooth_rows(residual), axis=0), 'mem')]
    reduce_sum x5 -> x7, other arithmetic: 0.86 us -> 5.35 us  [the longest x1 1.69 us: local_by_level(): step1 = norm_now / (norm_now + jnp.sum(got1[:, 0, 1]))]
    unnamed x11 -> x6, local copies, waits for them, and re-layouts: 5.14 us -> 0.66 us
    unnamed x7 -> x0, other arithmetic: 4.22 us -> none
    all_to_all x5 -> x4, starting transfers between devices: 21.2 us -> 17.3 us  [the longest x1 7.41 us: local_by_level(): lax.all_to_all(jnp.repeat(innovation, copies, axis=0), 'grid', 0, 1, tile...]
    all_to_all x1, blocking collectives: 8.95 us -> 12.8 us  [exchange(): return lax.all_to_all(parcel, ('grid', 'mem'), 0, 0, tiled=True)]
    concatenate x0 -> x3, other arithmetic: none -> 2.08 us  [the longest x1 1.14 us: local_by_level(): jnp.concatenate([members, counts], axis=0)]
    broadcast_in_dim x3 -> x8, local copies, waits for them, and re-layouts: 1.25 us -> 3.06 us  [the longest x1 1.34 us: local_by_level(): jnp.repeat(innovation, copies, axis=0)]
  transfers between devices with their start and end apart: 5 -> 4, of which waited for: 5 -> 4; matrix products, arithmetic and copies ran while one was open for 8% -> 5% of each run, Pallas kernels for 0% -> 0%
where the time goes in v2:
time: 111 us; the launch traced here: 110 us
  waiting for transfers between devices  28.1 us (25%)
  blocking collectives  23 us (21%)
  other arithmetic  20.5 us (18%)
  starting transfers between devices  17.3 us (16%)
  local copies, waits for them, and re-layouts  13.7 us (12%)
  between operations  7.61 us (7%)
    all_to_all x2, waiting for transfers between devices, exchange(): return lax.all_to_all(parcel, ('grid', 'mem'), 0, 0, tiled=True)  14.7 us
    all_to_all x1, blocking collectives, exchange(): return lax.all_to_all(parcel, ('grid', 'mem'), 0, 0, tiled=True)  12.8 us
    psum x1, blocking collectives, local_by_level(): total1 = lax.psum(jnp.sum(widened * smooth_rows(residual), axis=0), 'mem')  10.3 us
    all_to_all x1, waiting for transfers between devices, local_by_level(): got = lax.all_to_all(packed, 'grid', 1, 2, tiled=True)[:, 0]  8 us
    all_to_all x1, starting transfers between devices, local_by_level(): lax.all_to_all(jnp.repeat(innovation, copies, axis=0), 'grid', 0, 1, tile...  7.41 us
    all_to_all x2, starting transfers between devices, exchange(): return lax.all_to_all(parcel, ('grid', 'mem'), 0, 0, tiled=True)  6.47 us
    all_to_all x1, waiting for transfers between devices, local_by_level(): lax.all_to_all(jnp.repeat(innovation, copies, axis=0), 'grid', 0, 1, tile...  5.37 us
    reduce_sum x3, other arithmetic, squares(): return jnp.sum(jnp.where(own[None], field * field, 0.0))  3.91 us
  transfers between devices with their start and end apart: 4, of which 4 were waited for; matrix products, arithmetic and copies ran while one was open for 5% of the time, Pallas kernels for 0%

profile of v2, /device:TPU:0, one launch (start us, length us, event | category | flops | bytes accessed | tf_op | source)
XLA Modules:
  0.0 110.3 jit_solution(4415647576855443435)
XLA Ops:
  0.6 1.3 %broadcast_in_dim.59 = f32[4,2,2,512]{3,2,1,0:T(2,128)} broadcast(f32[4,2,512]{2,1,0:T(2,128)} %param.11), dimensions={0,2,3} | broadcast | bytes 49152 | tf_op jit(solution)/shard_map/broadcast_in_dim | solution.py:108
  2.0 7.4 %all-to-all-start.1 = ((f32[8,2,512]{2,1,0:T(2,128)}), f32[8,2,512]{2,1,0:T(2,128)S(1)}, u32[]{:S(2)}, u32[]{:S(2)}) async-start(f32[8,2,512]{2,1,0:T(2,128)} %bitcast.2), calls=%async_computation.1 | async-start | bytes 65536 | tf_op jit(solution)/shard_map/all_to_all | solution.py:108
  9.4 1.1 %pad_maximum_fusion.2 = bf16[21,4,2,512]{3,2,1,0:T(2,128)(2,1)S(1)} fusion(bf16[1,4,2,512]{3,2,1,0:T(2,128)(2,1)S(1)} %broadcast_in_dim.57, bf16[20,4,2,512]{3,2,1,0:T(2,128)(2,1)} %param.10), kind=kLoop, calls=%fused_computation.55 | loop fusion | flops 86016 | bytes 344064 | tf_op jit(solution)/shard_map/concatenate | solution.py:106
  10.7 5.4 %all-to-all-done.1 = f32[8,2,512]{2,1,0:T(2,128)S(1)} async-done(((f32[8,2,512]{2,1,0:T(2,128)}), f32[8,2,512]{2,1,0:T(2,128)S(1)}, u32[]{:S(2)}, u32[]{:S(2)}) %all-to-all-start.1) | async-done | bytes 32800 | tf_op jit(solution)/shard_map/all_to_all | solution.py:108
  16.1 0.9 broadcast_in_dim.58
  17.0 3.4 %all-to-all-start = ((bf16[21,8,2,512]{3,2,0,1:T(2,128)(2,1)}), bf16[21,8,2,512]{3,2,0,1:T(2,128)(2,1)S(1)}, u32[]{:S(2)}, u32[]{:S(2)}) async-start(bf16[21,8,2,512]{3,2,0,1:T(2,128)(2,1)} %bitcast), calls=%async_computation | async-start | bytes 688128 | tf_op jit(solution)/shard_map/all_to_all | solution.py:107
  21.8 8.0 %all-to-all-done = bf16[21,8,2,512]{3,2,0,1:T(2,128)(2,1)S(1)} async-done(((bf16[21,8,2,512]{3,2,0,1:T(2,128)(2,1)}), bf16[21,8,2,512]{3,2,0,1:T(2,128)(2,1)S(1)}, u32[]{:S(2)}, u32[]{:S(2)}) %all-to-all-start) | async-done | bytes 344096 | tf_op jit(solution)/shard_map/all_to_all | solution.py:107
  33.8 0.9 select_reduce_fusion.2
  37.0 10.3 %psum.7 = f32[16,512]{1,0:T(8,128)S(1)} all-reduce(f32[16,512]{1,0:T(8,128)S(1)} %fusion.13), channel_id=1, replica_groups=mesh['grid'=8,'mem'=4] {'mem'}, use_global_device_ids=true, to_apply=%region_2.3 | all-reduce | flops 8192 | bytes 65536 | tf_op jit(solution)/shard_map/psum | solution.py:127
  48.9 1.1 fusion.40
  52.2 0.8 pad_maximum_fusion
  53.0 3.9 %all-to-all-start.2 = ((f32[32,3,512]{2,1,0:T(4,128)}), f32[32,3,512]{2,1,0:T(4,128)}, u32[]{:S(2)}, u32[]{:S(2)}) async-start(f32[32,3,512]{2,1,0:T(4,128)} %pad_maximum_fusion), calls=%async_computation.2 | async-start | bytes 524288 | tf_op jit(solution)/shard_map/all_to_all | solution.py:92
  56.9 1.4 %fusion.16 = f32[20,16,512]{2,1,0:T(8,128)S(1)} fusion(f32[20,16,512]{2,1,0:T(8,128)S(1)} %multiply_add_fusion.2, f32[20,16,511]{2,1,0:T(8,128)} %get-tuple-element.75, f32[20,16,1]{2,1,0:T(8,128)} %get-tuple-element.77, f32[20,16,1]{2,1,0:T(8,128)S(1)} %get-tuple-element.76, f32[20,16,511]{2,1,0:T(8,128)S(1)} %get-tuple-element.74), kind=kLoop, calls=%fused_computation.21 | loop fusion | flops 1146880 | bytes 2621440 | tf_op jit(solution)/shard_map/add | solution.py:82
  59.0 1.1 %fusion.39 = (f32[20,16,511]{2,1,0:T(8,128)S(1)}, f32[20,16,511]{2,1,0:T(8,128)}) fusion(f32[20,16,512]{2,1,0:T(8,128)S(1)} %fusion.16), kind=kLoop, calls=%fused_computation.86 | loop fusion | bytes 2616320 | tf_op jit(solution)/shard_map/jit(_roll_static)/slice | solution.py:82
  60.1 7.3 %all-to-all-done.2 = f32[32,3,512]{2,1,0:T(4,128)} async-done(((f32[32,3,512]{2,1,0:T(4,128)}), f32[32,3,512]{2,1,0:T(4,128)}, u32[]{:S(2)}, u32[]{:S(2)}) %all-to-all-start.2) | async-done | bytes 196640 | tf_op jit(solution)/shard_map/all_to_all | solution.py:92
  67.4 1.7 %slice_reduce_fusion.4 = (f32[]{:T(128)}, f32[]{:T(128)}) fusion(f32[32,3,512]{2,1,0:T(4,128)} %all-to-all-done.2), kind=kLoop, calls=%fused_computation.66 | loop fusion | flops 62 | bytes 264 | tf_op jit(solution)/shard_map/reduce_sum | solution.py:133
  71.0 2.2 %select_reduce_fusion.1 = (f32[]{:T(128)}, f32[20,16,512]{2,1,0:T(8,128)S(1)}) fusion(f32[20,16,512]{2,1,0:T(8,128)S(1)} %get-tuple-element.55, f32[]{:T(128)S(6)} %div.31, pred[16,512]{1,0:T(8,128)(4,1)S(1)} %select_compare_fusion, f32[20,16,512]{2,1,0:T(8,128)S(1)} %fusion.16, f32[20,16,1]{2,1,0:T(8,128)} %get-tuple-element.71, ...), kind=kLoop, calls=%fused_computation.40 | loop fusion | flops 2129919 | bytes 3285000 | tf_op jit(solution)/shard_map/reduce_sum | solution.py:118
  76.4 12.8 %all_to_all.33 = f32[32,3,512]{2,1,0:T(4,128)S(1)} all-to-all(f32[32,3,512]{2,1,0:T(4,128)S(1)} %pad_maximum_fusion.1), channel_id=1, replica_groups=mesh['grid'=8,'mem'=4] {'grid','mem'}, dimensions={0} | all-to-all | bytes 393216 | tf_op jit(solution)/shard_map/all_to_all | solution.py:92
  91.2 0.8 select_reduce_fusion
  92.0 1.4 %fusion.29 = (f32[]{:T(128)}, f32[4,2,512]{2,1,0:T(2,128)S(1)}) fusion(f32[2,512]{1,0:T(2,128)S(1)} %get-tuple-element.107, f32[4]{0:T(128)S(1)} %copy-done.2, f32[]{:T(128)S(6)} %div.32, f32[4,2,512]{2,1,0:T(2,128)S(1)} %slice_reduce_fusion, f32[]{:T(128)S(6)} %div.31, f32[4,8,3,512]{3,2,1,0:T(4,128)} %bitcast.6), kind=kLoop, calls=%fused_computation.61 | loop fusion | flops 32767 | bytes 53276 | tf_op jit(solution)/shard_map/reduce_sum | solution.py:145
  95.5 2.6 %all-to-all-start.4 = ((f32[32,1,512]{2,1,0:T(1,128)}), f32[32,1,512]{2,1,0:T(1,128)S(1)}, u32[]{:S(2)}, u32[]{:S(2)}) async-start(f32[32,1,512]{2,1,0:T(1,128)} %broadcast_in_dim.66), calls=%async_computation.4 | async-start | bytes 131072 | tf_op jit(solution)/shard_map/all_to_all | solution.py:92
  98.1 7.4 %all-to-all-done.4 = f32[32,1,512]{2,1,0:T(1,128)S(1)} async-done(((f32[32,1,512]{2,1,0:T(1,128)}), f32[32,1,512]{2,1,0:T(1,128)S(1)}, u32[]{:S(2)}, u32[]{:S(2)}) %all-to-all-start.4) | async-done | bytes 65568 | tf_op jit(solution)/shard_map/all_to_all | solution.py:92
  108.1 0.8 multiply_add_fusion.8
  108.9 0.8 add_convert_fusion
  (74 shorter events, 17.8 us)
Async XLA Ops:
  2.0 7.4 %copy-start.1 = (s32[2,512]{1,0:T(2,128)S(1)}, s32[2,512]{1,0:T(2,128)}, u32[]{:S(2)}) copy-start(s32[2,512]{1,0:T(2,128)} %param.12) | copy-start | bytes 12292
  2.0 14.1 %all-to-all-start.1 = ((f32[8,2,512]{2,1,0:T(2,128)}), f32[8,2,512]{2,1,0:T(2,128)S(1)}, u32[]{:S(2)}, u32[]{:S(2)}) async-start(f32[8,2,512]{2,1,0:T(2,128)} %bitcast.2), calls=%async_computation.1 | async-start | bytes 65536 | tf_op jit(solution)/shard_map/all_to_all | solution.py:108
  17.0 12.8 %all-to-all-start = ((bf16[21,8,2,512]{3,2,0,1:T(2,128)(2,1)}), bf16[21,8,2,512]{3,2,0,1:T(2,128)(2,1)S(1)}, u32[]{:S(2)}, u32[]{:S(2)}) async-start(bf16[21,8,2,512]{3,2,0,1:T(2,128)(2,1)} %bitcast), calls=%async_computation | async-start | bytes 688128 | tf_op jit(solution)/shard_map/all_to_all | solution.py:107
  20.4 0.7 copy-start.2
  53.0 14.5 %all-to-all-start.2 = ((f32[32,3,512]{2,1,0:T(4,128)}), f32[32,3,512]{2,1,0:T(4,128)}, u32[]{:S(2)}, u32[]{:S(2)}) async-start(f32[32,3,512]{2,1,0:T(4,128)} %pad_maximum_fusion), calls=%async_computation.2 | async-start | bytes 524288 | tf_op jit(solution)/shard_map/all_to_all | solution.py:92
  93.4 15.5 %copy-start = (bf16[20,4,2,512]{3,2,1,0:T(2,128)(2,1)S(1)}, bf16[20,4,2,512]{3,2,1,0:T(2,128)(2,1)}, u32[]{:S(2)}) copy-start(bf16[20,4,2,512]{3,2,1,0:T(2,128)(2,1)} %param.10) | copy-start | bytes 491524
  95.5 10.0 %all-to-all-start.4 = ((f32[32,1,512]{2,1,0:T(1,128)}), f32[32,1,512]{2,1,0:T(1,128)S(1)}, u32[]{:S(2)}, u32[]{:S(2)}) async-start(f32[32,1,512]{2,1,0:T(1,128)} %broadcast_in_dim.66), calls=%async_computation.4 | async-start | bytes 131072 | tf_op jit(solution)/shard_map/all_to_all | solution.py:92

commit v3 on v2

--- a/solution.py
+++ b/solution.py
@@ -103,9 +103,15 @@
     level = grid_index // copies
 
     counts = jnp.broadcast_to(observed_count.astype(jnp.bfloat16), (1, levels, rows, nlon))
-    packed = jnp.repeat(jnp.concatenate([members, counts], axis=0), copies, axis=1)
+    high = lax.reduce_precision(innovation, exponent_bits=8, mantissa_bits=7)
+    rest = innovation - high
+    middle = lax.reduce_precision(rest, exponent_bits=8, mantissa_bits=7)
+    low = rest - middle
+    parts = jnp.stack([high, middle, low]).astype(jnp.bfloat16)
+    packed = jnp.repeat(jnp.concatenate([members, counts, parts], axis=0), copies, axis=1)
     got = lax.all_to_all(packed, "grid", 1, 2, tiled=True)[:, 0]
-    innov = lax.all_to_all(jnp.repeat(innovation, copies, axis=0), "grid", 0, 1, tiled=True)[0]
+    split = got[count + 1 :].astype(jnp.float32)
+    innov = (split[0] + split[1]) + split[2]
     precision = lax.dynamic_index_in_dim(obs_precision, level, 0, keepdims=False)
     weight = got[count].astype(jnp.float32) * precision
     widened = got[:count].astype(jnp.float32)

time: 111 us -> 104 us (0.937)
  starting transfers between devices: 17.3 us -> 13.8 us
  waiting for transfers between devices: 28.1 us -> 25.1 us
    all_to_all x1 -> x0, starting transfers between devices: 7.41 us -> none  [local_by_level(): lax.all_to_all(jnp.repeat(innovation, copies, axis=0), 'grid', 0, 1, tile...]
    all_to_all x1 -> x0, waiting for transfers between devices: 5.37 us -> none  [local_by_level(): lax.all_to_all(jnp.repeat(innovation, copies, axis=0), 'grid', 0, 1, tile...]
    all_to_all x1, starting transfers between devices: 3.44 us -> 7.28 us  [local_by_level(): got = lax.all_to_all(packed, 'grid', 1, 2, tiled=True)[:, 0]]
    all_to_all x1, waiting for transfers between devices: 8 us -> 10.3 us  [local_by_level(): got = lax.all_to_all(packed, 'grid', 1, 2, tiled=True)[:, 0]]
    broadcast_in_dim x3 -> x1, local copies, waits for them, and re-layouts: 2.25 us -> 0.94 us  [local_by_level(): jnp.repeat(jnp.concatenate([members, counts, parts], axis=0), copies, axi...]
    concatenate x1, other arithmetic: 1.14 us -> 0.02 us  [local_by_level(): jnp.concatenate([members, counts, parts], axis=0)]
  transfers between devices with their start and end apart: 4 -> 3, of which waited for: 4 -> 3; matrix products, arithmetic and copies ran while one was open for 5% -> 4% of each run, Pallas kernels for 0% -> 0%
where the time goes in v3:
time: 104 us; the launch traced here: 103 us
  waiting for transfers between devices  25.1 us (24%)
  blocking collectives  23 us (22%)
  other arithmetic  20.2 us (19%)
  starting transfers between devices  13.8 us (13%)
  local copies, waits for them, and re-layouts  13.5 us (13%)
  between operations  7.64 us (7%)
    all_to_all x2, waiting for transfers between devices, exchange(): return lax.all_to_all(parcel, ('grid', 'mem'), 0, 0, tiled=True)  14.7 us
    all_to_all x1, blocking collectives, exchange(): return lax.all_to_all(parcel, ('grid', 'mem'), 0, 0, tiled=True)  12.8 us
    all_to_all x1, waiting for transfers between devices, local_by_level(): got = lax.all_to_all(packed, 'grid', 1, 2, tiled=True)[:, 0]  10.3 us
    psum x1, blocking collectives, local_by_level(): total1 = lax.psum(jnp.sum(widened * smooth_rows(residual), axis=0), 'mem')  10.3 us
    all_to_all x1, starting transfers between devices, local_by_level(): got = lax.all_to_all(packed, 'grid', 1, 2, tiled=True)[:, 0]  7.28 us
    all_to_all x2, starting transfers between devices, exchange(): return lax.all_to_all(parcel, ('grid', 'mem'), 0, 0, tiled=True)  6.51 us
    reduce_sum x3, other arithmetic, squares(): return jnp.sum(jnp.where(own[None], field * field, 0.0))  3.88 us
    slice x12, local copies, waits for them, and re-layouts, smooth_rows(): jnp.roll(field, -1, -1)  3.63 us
  transfers between devices with their start and end apart: 3, of which 3 were waited for; matrix products, arithmetic and copies ran while one was open for 4% of the time, Pallas kernels for 0%

profile of v3, /device:TPU:0, one launch (start us, length us, event | category | flops | bytes accessed | tf_op | source)
XLA Modules:
  0.0 103.3 jit_solution(424451604412722695)
XLA Ops:
  0.6 0.8 fusion.59
  1.4 1.0 %constant_dynamic-update-slice_fusion.4 = bf16[24,4,2,512]{3,2,1,0:T(2,128)(2,1)S(1)} fusion(bf16[20,4,2,512]{3,2,1,0:T(2,128)(2,1)} %param.10), kind=kLoop, calls=%fused_computation.82 | loop fusion | bytes 327680
  2.7 0.9 broadcast_in_dim.55
  3.6 7.3 %all-to-all-start = ((bf16[24,8,2,512]{3,2,0,1:T(2,128)(2,1)}), bf16[24,8,2,512]{3,2,0,1:T(2,128)(2,1)S(1)}, u32[]{:S(2)}, u32[]{:S(2)}) async-start(bf16[24,8,2,512]{3,2,0,1:T(2,128)(2,1)} %bitcast.3), calls=%async_computation | async-start | bytes 786432 | tf_op jit(solution)/shard_map/all_to_all | solution.py:112
  12.2 10.3 %all-to-all-done = bf16[24,8,2,512]{3,2,0,1:T(2,128)(2,1)S(1)} async-done(((bf16[24,8,2,512]{3,2,0,1:T(2,128)(2,1)}), bf16[24,8,2,512]{3,2,0,1:T(2,128)(2,1)S(1)}, u32[]{:S(2)}, u32[]{:S(2)}) %all-to-all-start) | async-done | bytes 393248 | tf_op jit(solution)/shard_map/all_to_all | solution.py:112
  26.6 0.9 select_reduce_fusion.2
  29.9 10.3 %psum.7 = f32[16,512]{1,0:T(8,128)S(1)} all-reduce(f32[16,512]{1,0:T(8,128)S(1)} %fusion.13), channel_id=1, replica_groups=mesh['grid'=8,'mem'=4] {'mem'}, use_global_device_ids=true, to_apply=%region_2.3 | all-reduce | flops 8192 | bytes 65536 | tf_op jit(solution)/shard_map/psum | solution.py:133
  40.2 0.7 select_reduce_fusion.3
  41.8 1.1 %fusion.43 = (f32[20,16,511]{2,1,0:T(8,128)S(1)}, f32[20,16,511]{2,1,0:T(8,128)}) fusion(f32[20,16,512]{2,1,0:T(8,128)S(1)} %multiply_add_fusion.2), kind=kLoop, calls=%fused_computation.101 | loop fusion | bytes 2616320 | tf_op jit(solution)/shard_map/jit(_roll_static)/slice | solution.py:82
  42.9 0.8 fusion.44
  45.1 0.8 pad_maximum_fusion
  45.9 3.9 %all-to-all-start.1 = ((f32[32,3,512]{2,1,0:T(4,128)}), f32[32,3,512]{2,1,0:T(4,128)}, u32[]{:S(2)}, u32[]{:S(2)}) async-start(f32[32,3,512]{2,1,0:T(4,128)} %pad_maximum_fusion), calls=%async_computation.1 | async-start | bytes 524288 | tf_op jit(solution)/shard_map/all_to_all | solution.py:92
  49.9 1.4 %fusion.16 = f32[20,16,512]{2,1,0:T(8,128)S(1)} fusion(f32[20,16,512]{2,1,0:T(8,128)S(1)} %multiply_add_fusion.2, f32[20,16,511]{2,1,0:T(8,128)} %get-tuple-element.75, f32[20,16,1]{2,1,0:T(8,128)} %get-tuple-element.77, f32[20,16,1]{2,1,0:T(8,128)S(1)} %get-tuple-element.76, f32[20,16,511]{2,1,0:T(8,128)S(1)} %get-tuple-element.74), kind=kLoop, calls=%fused_computation.21 | loop fusion | flops 1146880 | bytes 2621440 | tf_op jit(solution)/shard_map/add | solution.py:82
  52.0 1.1 %fusion.42 = (f32[20,16,511]{2,1,0:T(8,128)S(1)}, f32[20,16,511]{2,1,0:T(8,128)}) fusion(f32[20,16,512]{2,1,0:T(8,128)S(1)} %fusion.16), kind=kLoop, calls=%fused_computation.100 | loop fusion | bytes 2616320 | tf_op jit(solution)/shard_map/jit(_roll_static)/slice | solution.py:82
  53.1 7.3 %all-to-all-done.1 = f32[32,3,512]{2,1,0:T(4,128)} async-done(((f32[32,3,512]{2,1,0:T(4,128)}), f32[32,3,512]{2,1,0:T(4,128)}, u32[]{:S(2)}, u32[]{:S(2)}) %all-to-all-start.1) | async-done | bytes 196640 | tf_op jit(solution)/shard_map/all_to_all | solution.py:92
  60.4 1.7 %slice_reduce_fusion.4 = (f32[]{:T(128)}, f32[]{:T(128)}) fusion(f32[32,3,512]{2,1,0:T(4,128)} %all-to-all-done.1), kind=kLoop, calls=%fused_computation.74 | loop fusion | flops 62 | bytes 264 | tf_op jit(solution)/shard_map/reduce_sum | solution.py:139
  64.1 2.2 %select_reduce_fusion.1 = (f32[]{:T(128)}, f32[20,16,512]{2,1,0:T(8,128)S(1)}) fusion(f32[20,16,512]{2,1,0:T(8,128)S(1)} %get-tuple-element.55, f32[]{:T(128)S(6)} %div.31, pred[16,512]{1,0:T(8,128)(4,1)S(1)} %select_compare_fusion, f32[20,16,512]{2,1,0:T(8,128)S(1)} %fusion.16, f32[20,16,1]{2,1,0:T(8,128)} %get-tuple-element.71, ...), kind=kLoop, calls=%fused_computation.40 | loop fusion | flops 2129919 | bytes 3285000 | tf_op jit(solution)/shard_map/reduce_sum | solution.py:124
  69.5 12.8 %all_to_all.24 = f32[32,3,512]{2,1,0:T(4,128)S(1)} all-to-all(f32[32,3,512]{2,1,0:T(4,128)S(1)} %pad_maximum_fusion.1), channel_id=1, replica_groups=mesh['grid'=8,'mem'=4] {'grid','mem'}, dimensions={0} | all-to-all | bytes 393216 | tf_op jit(solution)/shard_map/all_to_all | solution.py:92
  84.3 0.8 select_reduce_fusion
  85.1 1.4 %fusion.31 = (f32[]{:T(128)}, f32[4,2,512]{2,1,0:T(2,128)S(1)}) fusion(f32[2,512]{1,0:T(2,128)S(1)} %get-tuple-element.109, f32[4]{0:T(128)S(1)} %copy-done.2, f32[]{:T(128)S(6)} %div.32, f32[4,2,512]{2,1,0:T(2,128)S(1)} %slice_reduce_fusion, f32[]{:T(128)S(6)} %div.31, f32[4,8,3,512]{3,2,1,0:T(4,128)} %bitcast.8), kind=kLoop, calls=%fused_computation.69 | loop fusion | flops 32767 | bytes 53276 | tf_op jit(solution)/shard_map/reduce_sum | solution.py:151
  88.5 2.6 %all-to-all-start.3 = ((f32[32,1,512]{2,1,0:T(1,128)}), f32[32,1,512]{2,1,0:T(1,128)S(1)}, u32[]{:S(2)}, u32[]{:S(2)}) async-start(f32[32,1,512]{2,1,0:T(1,128)} %broadcast_in_dim.62), calls=%async_computation.3 | async-start | bytes 131072 | tf_op jit(solution)/shard_map/all_to_all | solution.py:92
  91.1 7.4 %all-to-all-done.3 = f32[32,1,512]{2,1,0:T(1,128)S(1)} async-done(((f32[32,1,512]{2,1,0:T(1,128)}), f32[32,1,512]{2,1,0:T(1,128)S(1)}, u32[]{:S(2)}, u32[]{:S(2)}) %all-to-all-start.3) | async-done | bytes 65568 | tf_op jit(solution)/shard_map/all_to_all | solution.py:92
  101.1 0.8 multiply_add_fusion.8
  101.9 0.8 add_convert_fusion
  (74 shorter events, 16.4 us)
Async XLA Ops:
  1.4 1.1 %copy-start.1 = (f32[4,2,512]{2,1,0:T(2,128)S(1)}, f32[4,2,512]{2,1,0:T(2,128)}, u32[]{:S(2)}) copy-start(f32[4,2,512]{2,1,0:T(2,128)} %param.11) | copy-start | bytes 49156
  3.6 19.0 %all-to-all-start = ((bf16[24,8,2,512]{3,2,0,1:T(2,128)(2,1)}), bf16[24,8,2,512]{3,2,0,1:T(2,128)(2,1)S(1)}, u32[]{:S(2)}, u32[]{:S(2)}) async-start(bf16[24,8,2,512]{3,2,0,1:T(2,128)(2,1)} %bitcast.3), calls=%async_computation | async-start | bytes 786432 | tf_op jit(solution)/shard_map/all_to_all | solution.py:112
  10.9 0.7 copy-start.2
  45.9 14.5 %all-to-all-start.1 = ((f32[32,3,512]{2,1,0:T(4,128)}), f32[32,3,512]{2,1,0:T(4,128)}, u32[]{:S(2)}, u32[]{:S(2)}) async-start(f32[32,3,512]{2,1,0:T(4,128)} %pad_maximum_fusion), calls=%async_computation.1 | async-start | bytes 524288 | tf_op jit(solution)/shard_map/all_to_all | solution.py:92
  86.5 15.3 %copy-start = (bf16[20,4,2,512]{3,2,1,0:T(2,128)(2,1)S(1)}, bf16[20,4,2,512]{3,2,1,0:T(2,128)(2,1)}, u32[]{:S(2)}) copy-start(bf16[20,4,2,512]{3,2,1,0:T(2,128)(2,1)} %param.10) | copy-start | bytes 491524
  88.5 10.0 %all-to-all-start.3 = ((f32[32,1,512]{2,1,0:T(1,128)}), f32[32,1,512]{2,1,0:T(1,128)S(1)}, u32[]{:S(2)}, u32[]{:S(2)}) async-start(f32[32,1,512]{2,1,0:T(1,128)} %broadcast_in_dim.62), calls=%async_computation.3 | async-start | bytes 131072 | tf_op jit(solution)/shard_map/all_to_all | solution.py:92

commit v4 on v3

--- a/solution.py
+++ b/solution.py
@@ -134,23 +134,38 @@
     image = residual + smooth_rows(widened * (weight * total1)[None])
     image_part = jnp.sum(widened * smooth_rows(image), axis=0)
 
-    got1 = exchange(jnp.stack([squares(residual), weighted(total1)]), by_target(total1))
+    got1 = exchange(
+        jnp.stack([squares(residual), weighted(total1)]),
+        jnp.concatenate([by_target(total1), by_target(image_part)], axis=1),
+    )
     norm_now = jnp.sum(got1[:, 0, 0])
-    step1 = norm_now / (norm_now + jnp.sum(got1[:, 0, 1]))
-    total1_rows = got1.reshape(levels, copies * mem_size, 1 + rows, nlon)[:, 0, 1:]
+    curvature1 = jnp.sum(got1[:, 0, 1])
+    step1 = norm_now / (norm_now + curvature1)
+    by_source = got1.reshape(levels, copies, mem_size, 1 + 2 * rows, nlon)[:, 0]
+    total1_rows = by_source[:, 0, 1 : 1 + rows]
+    image_rows = jnp.sum(by_source[:, :, 1 + rows :], axis=1)
 
     residual_next = residual - step1 * image
-    got2 = exchange(jnp.stack([squares(residual_next)]), by_target(image_part))
-    norm_next = jnp.sum(got2[:, 0, 0])
+    weight_rows = observed_count.astype(jnp.float32)[None] * obs_precision[:, None, None]
+    moved_rows = total1_rows - step1 * image_rows
+    got2 = exchange(
+        jnp.stack(
+            [
+                squares(residual_next),
+                jnp.sum(jnp.where(own[None], residual_next * residual, 0.0)),
+                jnp.where(first, jnp.sum(weight_rows * moved_rows * moved_rows), 0.0),
+                jnp.where(first, jnp.sum(weight_rows * moved_rows * total1_rows), 0.0),
+            ]
+        ),
+        jnp.zeros((grid_size * mem_size, 0, nlon), jnp.float32),
+    )
+    sums = jnp.sum(got2[:, 0, :4], axis=0)
+    norm_next = sums[0]
     beta = norm_next / norm_now
-    image_rows = jnp.sum(got2.reshape(levels, copies, mem_size, 1 + rows, nlon)[:, 0, :, 1:], axis=1)
-
-    direction = residual_next + beta * residual
-    weight_rows = observed_count.astype(jnp.float32)[None] * obs_precision[:, None, None]
-    total2_rows = (total1_rows - step1 * image_rows) + beta * total1_rows
-    q2 = jnp.where(first, jnp.sum(weight_rows * total2_rows * total2_rows), 0.0)
-    got3 = exchange(jnp.stack([squares(direction), q2]), jnp.zeros((grid_size * mem_size, 0, nlon), jnp.float32))
-    step2 = norm_next / (jnp.sum(got3[:, 0, 0]) + jnp.sum(got3[:, 0, 1]))
+    direction_sq = norm_next + 2.0 * beta * sums[1] + beta * beta * norm_now
+    curvature2 = sums[2] + 2.0 * beta * sums[3] + beta * beta * curvature1
+    step2 = norm_next / (direction_sq + curvature2)
+    total2_rows = moved_rows + beta * total1_rows
     whole = step1 * total1_rows + step2 * total2_rows
 
     share = levels // mem_size

time: 104 us -> 95.5 us (0.918)
  waiting for transfers between devices: 25.1 us -> 17.8 us
  blocking collectives: 23 us -> 29.5 us
  other arithmetic: 20.2 us -> 14.6 us
  starting transfers between devices: 13.8 us -> 10.3 us
  between operations: 7.64 us -> 10.6 us
  local copies, waits for them, and re-layouts: 13.5 us -> 12.2 us
    all_to_all x2 -> x1, waiting for transfers between devices: 14.7 us -> 7.41 us  [exchange(): return lax.all_to_all(parcel, ('grid', 'mem'), 0, 0, tiled=True)]
    all_to_all x1, blocking collectives: 12.8 us -> 19.2 us  [exchange(): return lax.all_to_all(parcel, ('grid', 'mem'), 0, 0, tiled=True)]
    all_to_all x2 -> x1, starting transfers between devices: 6.51 us -> 2.97 us  [exchange(): return lax.all_to_all(parcel, ('grid', 'mem'), 0, 0, tiled=True)]
    reduce_sum x5 -> x4, other arithmetic: 4.52 us -> 1.51 us  [the longest x1 0.73 us: local_by_level(): curvature1 = jnp.sum(got1[:, 0, 1])]
    reduce_sum x3 -> x2, other arithmetic: 3.88 us -> 1.85 us  [squares(): return jnp.sum(jnp.where(own[None], field * field, 0.0))]
    slice x4 -> x2, local copies, waits for them, and re-layouts: 2.18 us -> 0.36 us  [smooth_rows(): jnp.roll(field, 1, -1) + jnp.roll(field, -1, -1) - 2.0 * field]
    add x4, other arithmetic: 2.38 us -> 1.27 us  [smooth_rows(): field + diffusion * (jnp.roll(field, 1, -1) + jnp.roll(field, -1, -1) - 2...]
    reduce_sum x1, other arithmetic: 0.4 us -> 1.49 us  [local_by_level(): image_part = jnp.sum(widened * smooth_rows(image), axis=0)]
  transfers between devices with their start and end apart: 3 -> 2, of which waited for: 3 -> 2; matrix products, arithmetic and copies ran while one was open for 4% -> 1% of each run, Pallas kernels for 0% -> 0%
where the time goes in v4:
time: 95.5 us; the launch traced here: 94.9 us
  blocking collectives  29.5 us (31%)
  waiting for transfers between devices  17.8 us (19%)
  other arithmetic  14.6 us (15%)
  local copies, waits for them, and re-layouts  12.2 us (13%)
  between operations  10.6 us (11%)
  starting transfers between devices  10.3 us (11%)
    all_to_all x1, blocking collectives, exchange(): return lax.all_to_all(parcel, ('grid', 'mem'), 0, 0, tiled=True)  19.2 us
    all_to_all x1, waiting for transfers between devices, local_by_level(): got = lax.all_to_all(packed, 'grid', 1, 2, tiled=True)[:, 0]  10.3 us
    psum x1, blocking collectives, local_by_level(): total1 = lax.psum(jnp.sum(widened * smooth_rows(residual), axis=0), 'mem')  10.3 us
    all_to_all x1, waiting for transfers between devices, exchange(): return lax.all_to_all(parcel, ('grid', 'mem'), 0, 0, tiled=True)  7.41 us
    all_to_all x1, starting transfers between devices, local_by_level(): got = lax.all_to_all(packed, 'grid', 1, 2, tiled=True)[:, 0]  7.28 us
    slice x14, local copies, waits for them, and re-layouts, smooth_rows(): jnp.roll(field, -1, -1)  3.99 us
    all_to_all x1, starting transfers between devices, exchange(): return lax.all_to_all(parcel, ('grid', 'mem'), 0, 0, tiled=True)  2.97 us
    unnamed x10, local copies, waits for them, and re-layouts  2.42 us
  transfers between devices with their start and end apart: 2, of which 2 were waited for; matrix products, arithmetic and copies ran while one was open for 1% of the time, Pallas kernels for 0%

profile of v4, /device:TPU:0, one launch (start us, length us, event | category | flops | bytes accessed | tf_op | source)
XLA Modules:
  0.0 94.9 jit_solution(1100534248127824826)
XLA Ops:
  0.6 0.8 fusion.61
  1.4 1.0 %constant_dynamic-update-slice_fusion.4 = bf16[24,4,2,512]{3,2,1,0:T(2,128)(2,1)S(1)} fusion(bf16[20,4,2,512]{3,2,1,0:T(2,128)(2,1)} %param.8), kind=kLoop, calls=%fused_computation.85 | loop fusion | bytes 327680
  2.7 0.9 broadcast_in_dim.52
  3.6 7.3 %all-to-all-start = ((bf16[24,8,2,512]{3,2,0,1:T(2,128)(2,1)}), bf16[24,8,2,512]{3,2,0,1:T(2,128)(2,1)S(1)}, u32[]{:S(2)}, u32[]{:S(2)}) async-start(bf16[24,8,2,512]{3,2,0,1:T(2,128)(2,1)} %bitcast.3), calls=%async_computation | async-start | bytes 786432 | tf_op jit(solution)/shard_map/all_to_all | solution.py:112
  10.9 0.6 copy-done.2
  12.2 10.3 %all-to-all-done = bf16[24,8,2,512]{3,2,0,1:T(2,128)(2,1)S(1)} async-done(((bf16[24,8,2,512]{3,2,0,1:T(2,128)(2,1)}), bf16[24,8,2,512]{3,2,0,1:T(2,128)(2,1)S(1)}, u32[]{:S(2)}, u32[]{:S(2)}) %all-to-all-start) | async-done | bytes 393248 | tf_op jit(solution)/shard_map/all_to_all | solution.py:112
  22.6 0.7 convert_multiply_fusion
  26.6 0.9 select_reduce_fusion.2
  29.9 10.3 %psum.7 = f32[16,512]{1,0:T(8,128)S(1)} all-reduce(f32[16,512]{1,0:T(8,128)S(1)} %fusion.13), channel_id=1, replica_groups=mesh['grid'=8,'mem'=4] {'mem'}, use_global_device_ids=true, to_apply=%region_2.3 | all-reduce | flops 8192 | bytes 65536 | tf_op jit(solution)/shard_map/psum | solution.py:133
  40.2 0.7 select_reduce_fusion.3
  44.7 1.1 %fusion.37 = (f32[20,16,511]{2,1,0:T(8,128)S(1)}, f32[20,16,511]{2,1,0:T(8,128)}) fusion(f32[20,16,512]{2,1,0:T(8,128)S(1)} %fusion.23), kind=kLoop, calls=%fused_computation.99 | loop fusion | bytes 2616320 | tf_op jit(solution)/shard_map/jit(_roll_static)/slice | solution.py:82
  45.8 0.8 fusion.38
  46.6 1.5 %fusion.28 = f32[16,512]{1,0:T(8,128)S(1)} fusion(f32[20,16,512]{2,1,0:T(8,128)S(1)} %reshape.163, f32[20,16,512]{2,1,0:T(8,128)S(1)} %fusion.23, f32[20,16,511]{2,1,0:T(8,128)} %get-tuple-element.51, f32[20,16,1]{2,1,0:T(8,128)} %get-tuple-element.53, f32[20,16,1]{2,1,0:T(8,128)S(1)} %get-tuple-element.52, f32[20,16,511]{2,1,0:T(8,128)S(1)} %get-tuple-element.50), kind=kLoop, calls=%fused_computation.36 | loop fusion | flops 1466368 | bytes 2654208 | tf_op jit(solution)/shard_map/reduce_sum | solution.py:135
  48.8 0.7 select_maximum_fusion.3
  49.8 19.2 %all_to_all.19 = f32[32,5,512]{2,1,0:T(8,128)S(1)} all-to-all(f32[32,5,512]{2,1,0:T(8,128)S(1)} %pad_maximum_fusion), channel_id=1, replica_groups=mesh['grid'=8,'mem'=4] {'grid','mem'}, dimensions={0} | all-to-all | bytes 655360 | tf_op jit(solution)/shard_map/all_to_all | solution.py:92
  69.2 0.7 slice_reduce_fusion.2
  71.9 0.9 select_reduce_fusion.1
  72.8 0.7 multiply_reduce_fusion
  74.7 1.3 %select_maximum_fusion = f32[512]{0:T(512)S(1)} fusion(f32[1]{0:T(128)} %bitcast.14, f32[1]{0:T(128)} %bitcast.13, f32[1]{0:T(128)} %bitcast.12, f32[1]{0:T(128)} %bitcast.11), kind=kLoop, calls=%fused_computation.87 | loop fusion | flops 4096 | bytes 2064 | tf_op jit(solution)/shard_map/stack | solution.py:152
  76.0 0.7 broadcast_in_dim.58
  76.7 3.0 %all-to-all-start.2 = ((f32[32,1,512]{2,1,0:T(1,128)}), f32[32,1,512]{2,1,0:T(1,128)S(1)}, u32[]{:S(2)}, u32[]{:S(2)}) async-start(f32[32,1,512]{2,1,0:T(1,128)} %broadcast_in_dim.58), calls=%async_computation.2 | async-start | bytes 131072 | tf_op jit(solution)/shard_map/all_to_all | solution.py:92
  79.6 7.4 %all-to-all-done.2 = f32[32,1,512]{2,1,0:T(1,128)S(1)} async-done(((f32[32,1,512]{2,1,0:T(1,128)}), f32[32,1,512]{2,1,0:T(1,128)S(1)}, u32[]{:S(2)}, u32[]{:S(2)}) %all-to-all-start.2) | async-done | bytes 65568 | tf_op jit(solution)/shard_map/all_to_all | solution.py:92
  87.1 0.7 fusion.62
  93.5 0.8 add_convert_fusion
  (74 shorter events, 11.3 us)
Async XLA Ops:
  1.4 1.1 %copy-start.1 = (f32[4,2,512]{2,1,0:T(2,128)S(1)}, f32[4,2,512]{2,1,0:T(2,128)}, u32[]{:S(2)}) copy-start(f32[4,2,512]{2,1,0:T(2,128)} %param.9) | copy-start | bytes 49156
  3.6 19.0 %all-to-all-start = ((bf16[24,8,2,512]{3,2,0,1:T(2,128)(2,1)}), bf16[24,8,2,512]{3,2,0,1:T(2,128)(2,1)S(1)}, u32[]{:S(2)}, u32[]{:S(2)}) async-start(bf16[24,8,2,512]{3,2,0,1:T(2,128)(2,1)} %bitcast.3), calls=%async_computation | async-start | bytes 786432 | tf_op jit(solution)/shard_map/all_to_all | solution.py:112
  10.9 0.7 copy-start.2
  76.0 17.5 %copy-start = (bf16[20,4,2,512]{3,2,1,0:T(2,128)(2,1)S(1)}, bf16[20,4,2,512]{3,2,1,0:T(2,128)(2,1)}, u32[]{:S(2)}) copy-start(bf16[20,4,2,512]{3,2,1,0:T(2,128)(2,1)} %param.8) | copy-start | bytes 491524
  76.7 10.4 %all-to-all-start.2 = ((f32[32,1,512]{2,1,0:T(1,128)}), f32[32,1,512]{2,1,0:T(1,128)S(1)}, u32[]{:S(2)}, u32[]{:S(2)}) async-start(f32[32,1,512]{2,1,0:T(1,128)} %broadcast_in_dim.58), calls=%async_computation.2 | async-start | bytes 131072 | tf_op jit(solution)/shard_map/all_to_all | solution.py:92

commit v5 on v4

--- a/solution.py
+++ b/solution.py
@@ -134,16 +134,22 @@
     image = residual + smooth_rows(widened * (weight * total1)[None])
     image_part = jnp.sum(widened * smooth_rows(image), axis=0)
 
-    got1 = exchange(
-        jnp.stack([squares(residual), weighted(total1)]),
-        jnp.concatenate([by_target(total1), by_target(image_part)], axis=1),
-    )
+    if copies > 1:
+        rows_for = jnp.where(grid_index % copies == 0, by_target(total1), by_target(image_part))
+    else:
+        rows_for = jnp.concatenate([by_target(total1), by_target(image_part)], axis=1)
+    got1 = exchange(jnp.stack([squares(residual), weighted(total1)]), rows_for)
     norm_now = jnp.sum(got1[:, 0, 0])
     curvature1 = jnp.sum(got1[:, 0, 1])
     step1 = norm_now / (norm_now + curvature1)
-    by_source = got1.reshape(levels, copies, mem_size, 1 + 2 * rows, nlon)[:, 0]
-    total1_rows = by_source[:, 0, 1 : 1 + rows]
-    image_rows = jnp.sum(by_source[:, :, 1 + rows :], axis=1)
+    if copies > 1:
+        by_source = got1.reshape(levels, copies, mem_size, 1 + rows, nlon)
+        total1_rows = by_source[:, 0, 0, 1:]
+        image_rows = jnp.sum(by_source[:, 1, :, 1:], axis=1)
+    else:
+        by_source = got1.reshape(levels, mem_size, 1 + 2 * rows, nlon)
+        total1_rows = by_source[:, 0, 1 : 1 + rows]
+        image_rows = jnp.sum(by_source[:, :, 1 + rows :], axis=1)
 
     residual_next = residual - step1 * image
     weight_rows = observed_count.astype(jnp.float32)[None] * obs_precision[:, None, None]

time: 95.5 us -> 87.2 us (0.913)
  blocking collectives: 29.5 us -> 24.5 us
  local copies, waits for them, and re-layouts: 12.2 us -> 10.5 us
  other arithmetic: 14.6 us -> 13.5 us
    all_to_all x1, blocking collectives: 19.2 us -> 14.2 us  [exchange(): return lax.all_to_all(parcel, ('grid', 'mem'), 0, 0, tiled=True)]
    slice x14, local copies, waits for them, and re-layouts: 3.99 us -> 2.49 us  [smooth_rows(): jnp.roll(field, -1, -1)]
    reduce_sum x1, other arithmetic: 1.49 us -> 0.4 us  [local_by_level(): image_part = jnp.sum(widened * smooth_rows(image), axis=0)]
    unnamed x10 -> x9, local copies, waits for them, and re-layouts: 2.42 us -> 2.31 us
where the time goes in v5:
time: 87.2 us; the launch traced here: 86.7 us
  blocking collectives  24.5 us (28%)
  waiting for transfers between devices  17.8 us (20%)
  other arithmetic  13.5 us (15%)
  between operations  10.6 us (12%)
  local copies, waits for them, and re-layouts  10.5 us (12%)
  starting transfers between devices  9.85 us (11%)
    all_to_all x1, blocking collectives, exchange(): return lax.all_to_all(parcel, ('grid', 'mem'), 0, 0, tiled=True)  14.2 us
    all_to_all x1, waiting for transfers between devices, local_by_level(): got = lax.all_to_all(packed, 'grid', 1, 2, tiled=True)[:, 0]  10.3 us
    psum x1, blocking collectives, local_by_level(): total1 = lax.psum(jnp.sum(widened * smooth_rows(residual), axis=0), 'mem')  10.3 us
    all_to_all x1, waiting for transfers between devices, exchange(): return lax.all_to_all(parcel, ('grid', 'mem'), 0, 0, tiled=True)  7.41 us
    all_to_all x1, starting transfers between devices, local_by_level(): got = lax.all_to_all(packed, 'grid', 1, 2, tiled=True)[:, 0]  7.28 us
    all_to_all x1, starting transfers between devices, exchange(): return lax.all_to_all(parcel, ('grid', 'mem'), 0, 0, tiled=True)  2.57 us
    slice x14, local copies, waits for them, and re-layouts, smooth_rows(): jnp.roll(field, -1, -1)  2.49 us
    unnamed x9, local copies, waits for them, and re-layouts  2.31 us
  transfers between devices with their start and end apart: 2, of which 2 were waited for; matrix products, arithmetic and copies ran while one was open for 1% of the time, Pallas kernels for 0%

profile of v5, /device:TPU:0, one launch (start us, length us, event | category | flops | bytes accessed | tf_op | source)
XLA Modules:
  0.0 86.7 jit_solution(10481561956206714549)
XLA Ops:
  0.6 0.8 fusion.58
  1.4 1.0 %constant_dynamic-update-slice_fusion.4 = bf16[24,4,2,512]{3,2,1,0:T(2,128)(2,1)S(1)} fusion(bf16[20,4,2,512]{3,2,1,0:T(2,128)(2,1)} %param.8), kind=kLoop, calls=%fused_computation.82 | loop fusion | bytes 327680
  2.7 0.9 %broadcast_in_dim.50 = bf16[24,4,2,2,512]{4,3,0,2,1:T(2,128)(2,1)} broadcast(bf16[24,4,2,512]{3,2,0,1:T(2,128)(2,1)S(1)} %copy.31), dimensions={0,1,3,4} | broadcast | bytes 589824 | tf_op jit(solution)/shard_map/broadcast_in_dim | solution.py:111
  3.6 7.3 %all-to-all-start = ((bf16[24,8,2,512]{3,2,0,1:T(2,128)(2,1)}), bf16[24,8,2,512]{3,2,0,1:T(2,128)(2,1)S(1)}, u32[]{:S(2)}, u32[]{:S(2)}) async-start(bf16[24,8,2,512]{3,2,0,1:T(2,128)(2,1)} %bitcast.3), calls=%async_computation | async-start | bytes 786432 | tf_op jit(solution)/shard_map/all_to_all | solution.py:112
  10.9 0.6 copy-done.2
  11.6 0.6 dynamic_slice.7
  12.2 10.3 %all-to-all-done = bf16[24,8,2,512]{3,2,0,1:T(2,128)(2,1)S(1)} async-done(((bf16[24,8,2,512]{3,2,0,1:T(2,128)(2,1)}), bf16[24,8,2,512]{3,2,0,1:T(2,128)(2,1)S(1)}, u32[]{:S(2)}, u32[]{:S(2)}) %all-to-all-start) | async-done | bytes 393248 | tf_op jit(solution)/shard_map/all_to_all | solution.py:112
  22.6 0.7 convert_multiply_fusion
  23.7 0.5 copy.33
  26.6 0.9 %select_reduce_fusion.2 = (f32[]{:T(128)}, f32[20,16,512]{2,1,0:T(8,128)S(1)}) fusion(pred[16,512]{1,0:T(8,128)(4,1)S(1)} %select_compare_fusion, f32[20,16,512]{2,1,0:T(8,128)S(1)} %fusion.2, f32[20,16,1]{2,1,0:T(8,128)S(1)} %get-tuple-element.87, f32[20,16,511]{2,1,0:T(8,128)S(1)} %get-tuple-element.89, f32[20,16,511]{2,1,0:T(8,128)S(1)} %get-tuple-element.88, ...), kind=kLoop, calls=%fused_computation.46 | loop fusion | flops 1638399 | bytes 2629636 | tf_op jit(solution)/shard_map/reduce_sum | solution.py:124
  29.9 10.3 %psum.7 = f32[16,512]{1,0:T(8,128)S(1)} all-reduce(f32[16,512]{1,0:T(8,128)S(1)} %fusion.13), channel_id=1, replica_groups=mesh['grid'=8,'mem'=4] {'mem'}, use_global_device_ids=true, to_apply=%region_2.3 | all-reduce | flops 8192 | bytes 65536 | tf_op jit(solution)/shard_map/psum | solution.py:133
  40.2 0.7 select_reduce_fusion.3
  46.2 0.7 select_maximum_fusion.3
  47.1 14.2 %all_to_all.19 = f32[32,3,512]{2,1,0:T(4,128)S(1)} all-to-all(f32[32,3,512]{2,1,0:T(4,128)S(1)} %pad_maximum_fusion), channel_id=1, replica_groups=mesh['grid'=8,'mem'=4] {'grid','mem'}, dimensions={0} | all-to-all | bytes 393216 | tf_op jit(solution)/shard_map/all_to_all | solution.py:92
  61.4 0.7 slice_reduce_fusion.2
  64.0 0.9 %select_reduce_fusion.1 = (f32[]{:T(128)}, f32[]{:T(128)}) fusion(f32[20,16,512]{2,1,0:T(8,128)S(1)} %get-tuple-element.47, f32[20,16,512]{2,1,0:T(8,128)S(1)} %fusion.20, f32[]{:T(128)S(6)} %div.31, pred[16,512]{1,0:T(8,128)(4,1)S(1)} %select_compare_fusion), kind=kLoop, calls=%fused_computation.38 | loop fusion | flops 1310718 | bytes 1318924 | tf_op jit(solution)/shard_map/reduce_sum | solution.py:124
  64.9 0.7 multiply_reduce_fusion.1
  66.8 1.3 %select_maximum_fusion = f32[512]{0:T(512)S(1)} fusion(f32[1]{0:T(128)} %bitcast.12, f32[1]{0:T(128)} %bitcast.11, f32[1]{0:T(128)} %bitcast.10, f32[1]{0:T(128)} %bitcast.9), kind=kLoop, calls=%fused_computation.84 | loop fusion | flops 4096 | bytes 2064 | tf_op jit(solution)/shard_map/stack | solution.py:158
  68.1 0.7 broadcast_in_dim.55
  68.8 2.6 %all-to-all-start.2 = ((f32[32,1,512]{2,1,0:T(1,128)}), f32[32,1,512]{2,1,0:T(1,128)S(1)}, u32[]{:S(2)}, u32[]{:S(2)}) async-start(f32[32,1,512]{2,1,0:T(1,128)} %broadcast_in_dim.55), calls=%async_computation.2 | async-start | bytes 131072 | tf_op jit(solution)/shard_map/all_to_all | solution.py:92
  71.4 7.4 %all-to-all-done.2 = f32[32,1,512]{2,1,0:T(1,128)S(1)} async-done(((f32[32,1,512]{2,1,0:T(1,128)}), f32[32,1,512]{2,1,0:T(1,128)S(1)}, u32[]{:S(2)}, u32[]{:S(2)}) %all-to-all-start.2) | async-done | bytes 65568 | tf_op jit(solution)/shard_map/all_to_all | solution.py:92
  78.8 0.7 fusion.59
  85.2 0.8 add_convert_fusion
  86.1 0.6 copy.37
  (71 shorter events, 10.1 us)
Async XLA Ops:
  1.4 1.1 %copy-start.1 = (f32[4,2,512]{2,1,0:T(2,128)S(1)}, f32[4,2,512]{2,1,0:T(2,128)}, u32[]{:S(2)}) copy-start(f32[4,2,512]{2,1,0:T(2,128)} %param.9) | copy-start | bytes 49156
  3.6 19.0 %all-to-all-start = ((bf16[24,8,2,512]{3,2,0,1:T(2,128)(2,1)}), bf16[24,8,2,512]{3,2,0,1:T(2,128)(2,1)S(1)}, u32[]{:S(2)}, u32[]{:S(2)}) async-start(bf16[24,8,2,512]{3,2,0,1:T(2,128)(2,1)} %bitcast.3), calls=%async_computation | async-start | bytes 786432 | tf_op jit(solution)/shard_map/all_to_all | solution.py:112
  10.9 0.7 copy-start.2
  68.1 17.1 %copy-start = (bf16[20,4,2,512]{3,2,1,0:T(2,128)(2,1)S(1)}, bf16[20,4,2,512]{3,2,1,0:T(2,128)(2,1)}, u32[]{:S(2)}) copy-start(bf16[20,4,2,512]{3,2,1,0:T(2,128)(2,1)} %param.8) | copy-start | bytes 491524
  68.8 10.0 %all-to-all-start.2 = ((f32[32,1,512]{2,1,0:T(1,128)}), f32[32,1,512]{2,1,0:T(1,128)S(1)}, u32[]{:S(2)}, u32[]{:S(2)}) async-start(f32[32,1,512]{2,1,0:T(1,128)} %broadcast_in_dim.55), calls=%async_computation.2 | async-start | bytes 131072 | tf_op jit(solution)/shard_map/all_to_all | solution.py:92

commit v6 on v5

--- a/solution.py
+++ b/solution.py
@@ -86,10 +86,19 @@
 def exchange(values, rows_for):
     devices = lax.axis_size("grid") * lax.axis_size("mem")
     nlon = rows_for.shape[-1]
-    head = jnp.zeros((nlon,), jnp.float32).at[: values.shape[0]].set(values)
-    head = jnp.broadcast_to(head, (devices, 1, nlon))
+    lanes = [jnp.sum(v.reshape(-1, 128), axis=0) for v in values]
+    lanes.append(jnp.zeros((nlon - 128 * len(values),), jnp.float32))
+    head = jnp.broadcast_to(jnp.concatenate(lanes), (devices, 1, nlon))
     parcel = jnp.concatenate([head, rows_for], axis=1)
-    return lax.all_to_all(parcel, ("grid", "mem"), 0, 0, tiled=True)
+    got = lax.all_to_all(parcel, ("grid", "mem"), 0, 0, tiled=True)
+    sums = jnp.sum(got[:, 0].reshape(devices, nlon // 128, 128), axis=(0, 2))
+    return sums, got[:, 1:]
+
+
+def mem_total(part):
+    mem_size = lax.axis_size("mem")
+    got = lax.all_to_all(jnp.broadcast_to(part, (mem_size,) + part.shape), "mem", 0, 0, tiled=True)
+    return jnp.sum(got, axis=0)
 
 
 def local_by_level(members, innovation, observed_count, obs_precision):
@@ -121,16 +130,16 @@
     first = mem_index == 0
 
     def squares(field):
-        return jnp.sum(jnp.where(own[None], field * field, 0.0))
+        return jnp.sum(jnp.where(own[None], field * field, 0.0), axis=(0, 1))
 
     def weighted(total):
-        return jnp.where(first, jnp.sum(jnp.where(own, weight * total * total, 0.0)), 0.0)
+        return jnp.where(first, jnp.sum(jnp.where(own, weight * total * total, 0.0), axis=0), 0.0)
 
     def by_target(field):
         return jnp.repeat(field.reshape(grid_size, rows, nlon), mem_size, axis=0)
 
     residual = smooth_rows(widened * (weight * innov)[None])
-    total1 = lax.psum(jnp.sum(widened * smooth_rows(residual), axis=0), "mem")
+    total1 = mem_total(jnp.sum(widened * smooth_rows(residual), axis=0))
     image = residual + smooth_rows(widened * (weight * total1)[None])
     image_part = jnp.sum(widened * smooth_rows(image), axis=0)
 
@@ -138,34 +147,31 @@
         rows_for = jnp.where(grid_index % copies == 0, by_target(total1), by_target(image_part))
     else:
         rows_for = jnp.concatenate([by_target(total1), by_target(image_part)], axis=1)
-    got1 = exchange(jnp.stack([squares(residual), weighted(total1)]), rows_for)
-    norm_now = jnp.sum(got1[:, 0, 0])
-    curvature1 = jnp.sum(got1[:, 0, 1])
+    sums1, got1 = exchange([squares(residual), weighted(total1)], rows_for)
+    norm_now = sums1[0]
+    curvature1 = sums1[1]
     step1 = norm_now / (norm_now + curvature1)
     if copies > 1:
-        by_source = got1.reshape(levels, copies, mem_size, 1 + rows, nlon)
-        total1_rows = by_source[:, 0, 0, 1:]
-        image_rows = jnp.sum(by_source[:, 1, :, 1:], axis=1)
+        by_source = got1.reshape(levels, copies, mem_size, rows, nlon)
+        total1_rows = by_source[:, 0, 0]
+        image_rows = jnp.sum(by_source[:, 1], axis=1)
     else:
-        by_source = got1.reshape(levels, mem_size, 1 + 2 * rows, nlon)
-        total1_rows = by_source[:, 0, 1 : 1 + rows]
-        image_rows = jnp.sum(by_source[:, :, 1 + rows :], axis=1)
+        by_source = got1.reshape(levels, mem_size, 2 * rows, nlon)
+        total1_rows = by_source[:, 0, :rows]
+        image_rows = jnp.sum(by_source[:, :, rows:], axis=1)
 
     residual_next = residual - step1 * image
     weight_rows = observed_count.astype(jnp.float32)[None] * obs_precision[:, None, None]
     moved_rows = total1_rows - step1 * image_rows
-    got2 = exchange(
-        jnp.stack(
-            [
-                squares(residual_next),
-                jnp.sum(jnp.where(own[None], residual_next * residual, 0.0)),
-                jnp.where(first, jnp.sum(weight_rows * moved_rows * moved_rows), 0.0),
-                jnp.where(first, jnp.sum(weight_rows * moved_rows * total1_rows), 0.0),
-            ]
-        ),
+    sums, _ = exchange(
+        [
+            squares(residual_next),
+            jnp.sum(jnp.where(own[None], residual_next * residual, 0.0), axis=(0, 1)),
+            jnp.where(first, jnp.sum(weight_rows * moved_rows * moved_rows, axis=(0, 1)), 0.0),
+            jnp.where(first, jnp.sum(weight_rows * moved_rows * total1_rows, axis=(0, 1)), 0.0),
+        ],
         jnp.zeros((grid_size * mem_size, 0, nlon), jnp.float32),
     )
-    sums = jnp.sum(got2[:, 0, :4], axis=0)
     norm_next = sums[0]
     beta = norm_next / norm_now
     direction_sq = norm_next + 2.0 * beta * sums[1] + beta * beta * norm_now

time: 87.2 us -> 79.4 us (0.911)
  blocking collectives: 24.5 us -> 13.1 us
  waiting for transfers between devices: 17.8 us -> 22.3 us
  other arithmetic: 13.5 us -> 9.37 us
  starting transfers between devices: 9.85 us -> 13.3 us
  between operations: 10.6 us -> 9.01 us
  local copies, waits for them, and re-layouts: 10.5 us -> 11.8 us
    psum x1 -> x0, blocking collectives: 10.3 us -> none  [local_by_level(): total1 = lax.psum(jnp.sum(widened * smooth_rows(residual), axis=0), 'mem')]
    all_to_all x1 -> x2, waiting for transfers between devices: 7.41 us -> 12 us  [the longest x1 7.41 us: exchange(): got = lax.all_to_all(parcel, ('grid', 'mem'), 0, 0, tiled=True)]
    all_to_all x1 -> x2, starting transfers between devices: 2.57 us -> 6.03 us  [the longest x1 3.33 us: mem_total(): lax.all_to_all(jnp.broadcast_to(part, (mem_size,) + part.shape), 'mem', 0...]
    reduce_sum x8 -> x17, other arithmetic: 4.44 us -> 2.31 us  [the longest x1 0.76 us: weighted(): jnp.sum(jnp.where(own, weight * total * total, 0.0), axis=0)]
    another operation x2 -> x0, other arithmetic: 2.04 us -> none  [the longest x1 1.31 us: local_by_level(): jnp.stack([squares(residual_next), jnp.sum(jnp.where(own[None], residual_...]
    all_to_all x1, blocking collectives: 14.2 us -> 13.1 us  [exchange(): got = lax.all_to_all(parcel, ('grid', 'mem'), 0, 0, tiled=True)]
    unnamed x9 -> x8, local copies, waits for them, and re-layouts: 2.31 us -> 1.71 us
  transfers between devices with their start and end apart: 2 -> 3, of which waited for: 2 -> 3; matrix products, arithmetic and copies ran while one was open for 1% -> 1% of each run, Pallas kernels for 0% -> 0%
where the time goes in v6:
time: 79.4 us; the launch traced here: 78.9 us
  waiting for transfers between devices  22.3 us (28%)
  starting transfers between devices  13.3 us (17%)
  blocking collectives  13.1 us (16%)
  local copies, waits for them, and re-layouts  11.8 us (15%)
  other arithmetic  9.37 us (12%)
  between operations  9.01 us (11%)
    all_to_all x1, blocking collectives, exchange(): got = lax.all_to_all(parcel, ('grid', 'mem'), 0, 0, tiled=True)  13.1 us
    all_to_all x1, waiting for transfers between devices, local_by_level(): got = lax.all_to_all(packed, 'grid', 1, 2, tiled=True)[:, 0]  10.3 us
    all_to_all x1, waiting for transfers between devices, exchange(): got = lax.all_to_all(parcel, ('grid', 'mem'), 0, 0, tiled=True)  7.41 us
    all_to_all x1, starting transfers between devices, local_by_level(): got = lax.all_to_all(packed, 'grid', 1, 2, tiled=True)[:, 0]  7.28 us
    all_to_all x1, waiting for transfers between devices, mem_total(): lax.all_to_all(jnp.broadcast_to(part, (mem_size,) + part.shape), 'mem', 0...  4.55 us
    all_to_all x1, starting transfers between devices, mem_total(): lax.all_to_all(jnp.broadcast_to(part, (mem_size,) + part.shape), 'mem', 0...  3.33 us
    all_to_all x1, starting transfers between devices, exchange(): got = lax.all_to_all(parcel, ('grid', 'mem'), 0, 0, tiled=True)  2.7 us
    slice x14, local copies, waits for them, and re-layouts, smooth_rows(): jnp.roll(field, -1, -1)  2.49 us
  transfers between devices with their start and end apart: 3, of which 3 were waited for; matrix products, arithmetic and copies ran while one was open for 1% of the time, Pallas kernels for 0%

profile of v6, /device:TPU:0, one launch (start us, length us, event | category | flops | bytes accessed | tf_op | source)
XLA Modules:
  0.0 78.9 jit_solution(3640375685895324915)
XLA Ops:
  0.6 0.8 fusion.60
  1.4 1.0 %constant_dynamic-update-slice_fusion.4 = bf16[24,4,2,512]{3,2,1,0:T(2,128)(2,1)S(1)} fusion(bf16[20,4,2,512]{3,2,1,0:T(2,128)(2,1)} %param.4), kind=kLoop, calls=%fused_computation.81 | loop fusion | bytes 327680
  2.7 0.9 %broadcast_in_dim.62 = bf16[24,4,2,2,512]{4,3,0,2,1:T(2,128)(2,1)} broadcast(bf16[24,4,2,512]{3,2,0,1:T(2,128)(2,1)S(1)} %copy.18), dimensions={0,1,3,4} | broadcast | bytes 589824 | tf_op jit(solution)/shard_map/broadcast_in_dim | solution.py:120
  3.6 7.3 %all-to-all-start = ((bf16[24,8,2,512]{3,2,0,1:T(2,128)(2,1)}), bf16[24,8,2,512]{3,2,0,1:T(2,128)(2,1)S(1)}, u32[]{:S(2)}, u32[]{:S(2)}) async-start(bf16[24,8,2,512]{3,2,0,1:T(2,128)(2,1)} %bitcast.3), calls=%async_computation | async-start | bytes 786432 | tf_op jit(solution)/shard_map/all_to_all | solution.py:121
  10.9 0.6 copy-done.2
  11.6 0.6 dynamic_slice.7
  12.3 10.3 %all-to-all-done = bf16[24,8,2,512]{3,2,0,1:T(2,128)(2,1)S(1)} async-done(((bf16[24,8,2,512]{3,2,0,1:T(2,128)(2,1)}), bf16[24,8,2,512]{3,2,0,1:T(2,128)(2,1)S(1)}, u32[]{:S(2)}, u32[]{:S(2)}) %all-to-all-start) | async-done | bytes 393248 | tf_op jit(solution)/shard_map/all_to_all | solution.py:121
  22.9 0.5 copy.20
  23.5 0.5 reshape.193
  24.0 0.7 fusion.29
  28.9 0.4 fusion.13
  29.3 0.7 broadcast_in_dim.64
  29.9 3.3 %all-to-all-start.1 = ((f32[4,16,512]{2,1,0:T(8,128)}), f32[4,16,512]{2,1,0:T(8,128)S(1)}, u32[]{:S(2)}, u32[]{:S(2)}) async-start(f32[4,16,512]{2,1,0:T(8,128)} %broadcast_in_dim.64), calls=%async_computation.1 | async-start | bytes 262144 | tf_op jit(solution)/shard_map/all_to_all | solution.py:100
  33.3 4.5 %all-to-all-done.1 = f32[4,16,512]{2,1,0:T(8,128)S(1)} async-done(((f32[4,16,512]{2,1,0:T(8,128)}), f32[4,16,512]{2,1,0:T(8,128)S(1)}, u32[]{:S(2)}, u32[]{:S(2)}) %all-to-all-start.1) | async-done | bytes 131104 | tf_op jit(solution)/shard_map/all_to_all | solution.py:100
  37.9 0.8 fusion.30
  42.9 0.4 fusion.28
  43.6 13.1 %all_to_all.24 = f32[32,3,512]{2,1,0:T(4,128)S(1)} all-to-all(f32[32,3,512]{2,1,0:T(4,128)S(1)} %pad_maximum_fusion), channel_id=1, replica_groups=mesh['grid'=8,'mem'=4] {'grid','mem'}, dimensions={0} | all-to-all | bytes 393216 | tf_op jit(solution)/shard_map/all_to_all | solution.py:93
  57.0 0.6 fusion.62
  60.0 0.7 broadcast_in_dim.70
  60.7 2.7 %all-to-all-start.3 = ((f32[32,1,512]{2,1,0:T(1,128)}), f32[32,1,512]{2,1,0:T(1,128)S(1)}, u32[]{:S(2)}, u32[]{:S(2)}) async-start(f32[32,1,512]{2,1,0:T(1,128)} %broadcast_in_dim.70), calls=%async_computation.3 | async-start | bytes 131072 | tf_op jit(solution)/shard_map/all_to_all | solution.py:93
  63.4 7.4 %all-to-all-done.3 = f32[32,1,512]{2,1,0:T(1,128)S(1)} async-done(((f32[32,1,512]{2,1,0:T(1,128)}), f32[32,1,512]{2,1,0:T(1,128)S(1)}, u32[]{:S(2)}, u32[]{:S(2)}) %all-to-all-start.3) | async-done | bytes 65568 | tf_op jit(solution)/shard_map/all_to_all | solution.py:93
  71.0 0.6 fusion.61
  77.5 0.8 %add_convert_fusion = bf16[20,4,2,512]{3,2,1,0:T(2,128)(2,1)} fusion(bf16[20,4,2,512]{3,2,1,0:T(2,128)(2,1)S(1)} %copy-done, f32[4,2,512]{2,1,0:T(2,128)S(1)} %multiply_add_fusion.8), kind=kLoop, calls=%fused_computation.50 | loop fusion | flops 245760 | bytes 344064 | tf_op jit(solution)/shard_map/convert_element_type | solution.py:185
  78.3 0.6 constant_dynamic-slice_fusion
  (86 shorter events, 10.0 us)
Async XLA Ops:
  1.4 1.1 %copy-start.1 = (f32[4,2,512]{2,1,0:T(2,128)S(1)}, f32[4,2,512]{2,1,0:T(2,128)}, u32[]{:S(2)}) copy-start(f32[4,2,512]{2,1,0:T(2,128)} %param.5) | copy-start | bytes 49156
  3.6 19.0 %all-to-all-start = ((bf16[24,8,2,512]{3,2,0,1:T(2,128)(2,1)}), bf16[24,8,2,512]{3,2,0,1:T(2,128)(2,1)S(1)}, u32[]{:S(2)}, u32[]{:S(2)}) async-start(bf16[24,8,2,512]{3,2,0,1:T(2,128)(2,1)} %bitcast.3), calls=%async_computation | async-start | bytes 786432 | tf_op jit(solution)/shard_map/all_to_all | solution.py:121
  10.9 0.7 copy-start.2
  29.9 7.9 %all-to-all-start.1 = ((f32[4,16,512]{2,1,0:T(8,128)}), f32[4,16,512]{2,1,0:T(8,128)S(1)}, u32[]{:S(2)}, u32[]{:S(2)}) async-start(f32[4,16,512]{2,1,0:T(8,128)} %broadcast_in_dim.64), calls=%async_computation.1 | async-start | bytes 262144 | tf_op jit(solution)/shard_map/all_to_all | solution.py:100
  60.7 16.8 %copy-start = (bf16[20,4,2,512]{3,2,1,0:T(2,128)(2,1)S(1)}, bf16[20,4,2,512]{3,2,1,0:T(2,128)(2,1)}, u32[]{:S(2)}) copy-start(bf16[20,4,2,512]{3,2,1,0:T(2,128)(2,1)} %param.4) | copy-start | bytes 491524
  60.7 10.1 %all-to-all-start.3 = ((f32[32,1,512]{2,1,0:T(1,128)}), f32[32,1,512]{2,1,0:T(1,128)S(1)}, u32[]{:S(2)}, u32[]{:S(2)}) async-start(f32[32,1,512]{2,1,0:T(1,128)} %broadcast_in_dim.70), calls=%async_computation.3 | async-start | bytes 131072 | tf_op jit(solution)/shard_map/all_to_all | solution.py:93

commit v7 on v6

--- a/solution.py
+++ b/solution.py
@@ -91,8 +91,9 @@
     head = jnp.broadcast_to(jnp.concatenate(lanes), (devices, 1, nlon))
     parcel = jnp.concatenate([head, rows_for], axis=1)
     got = lax.all_to_all(parcel, ("grid", "mem"), 0, 0, tiled=True)
-    sums = jnp.sum(got[:, 0].reshape(devices, nlon // 128, 128), axis=(0, 2))
-    return sums, got[:, 1:]
+    lanes = jnp.sum(got[:, 0].reshape(devices, nlon // 128, 128), axis=0)
+    sums = jnp.dot(lanes, jnp.ones((128, 128), jnp.float32), precision=lax.Precision.HIGHEST)
+    return [jnp.tile(sums[i : i + 1], (1, nlon // 128)) for i in range(len(values))], got[:, 1:]
 
 
 def mem_total(part):

time: 79.4 us -> 70.4 us (0.89)
  between operations: 9.01 us -> 1.17 us
  local copies, waits for them, and re-layouts: 11.8 us -> 10.6 us
    slice x3 -> x1, local copies, waits for them, and re-layouts: 1.29 us -> 0.07 us  [exchange(): got[:, 1:]]
where the time goes in v7:
time: 70.4 us; the launch traced here: 69.9 us
  waiting for transfers between devices  22.3 us (32%)
  starting transfers between devices  13.3 us (19%)
  blocking collectives  13.1 us (19%)
  local copies, waits for them, and re-layouts  10.6 us (15%)
  other arithmetic  9.2 us (13%)
  between operations  1.17 us (2%)
    all_to_all x1, blocking collectives, exchange(): got = lax.all_to_all(parcel, ('grid', 'mem'), 0, 0, tiled=True)  13.1 us
    all_to_all x1, waiting for transfers between devices, local_by_level(): got = lax.all_to_all(packed, 'grid', 1, 2, tiled=True)[:, 0]  10.3 us
    all_to_all x1, waiting for transfers between devices, exchange(): got = lax.all_to_all(parcel, ('grid', 'mem'), 0, 0, tiled=True)  7.41 us
    all_to_all x1, starting transfers between devices, local_by_level(): got = lax.all_to_all(packed, 'grid', 1, 2, tiled=True)[:, 0]  7.28 us
    all_to_all x1, waiting for transfers between devices, mem_total(): lax.all_to_all(jnp.broadcast_to(part, (mem_size,) + part.shape), 'mem', 0...  4.55 us
    all_to_all x1, starting transfers between devices, mem_total(): lax.all_to_all(jnp.broadcast_to(part, (mem_size,) + part.shape), 'mem', 0...  3.33 us
    all_to_all x1, starting transfers between devices, exchange(): got = lax.all_to_all(parcel, ('grid', 'mem'), 0, 0, tiled=True)  2.7 us
    slice x14, local copies, waits for them, and re-layouts, smooth_rows(): jnp.roll(field, -1, -1)  2.49 us
  transfers between devices with their start and end apart: 3, of which 3 were waited for; matrix products, arithmetic and copies ran while one was open for 1% of the time, Pallas kernels for 0%

profile of v7, /device:TPU:0, one launch (start us, length us, event | category | flops | bytes accessed | tf_op | source)
XLA Modules:
  0.0 69.9 jit_solution(4597929367296627851)
XLA Ops:
  0.6 0.8 %fusion.72 = (bf16[2,512]{1,0:T(2,128)(2,1)S(1)}, f32[2,512]{1,0:T(2,128)S(1)}) fusion(s32[2,512]{1,0:T(2,128)} %param.6), kind=kLoop, calls=%fused_computation.154 | loop fusion | flops 2048 | bytes 10240 | tf_op jit(solution)/shard_map/convert_element_type | solution.py:115
  1.4 1.0 %constant_dynamic-update-slice_fusion.4 = bf16[24,4,2,512]{3,2,1,0:T(2,128)(2,1)S(1)} fusion(bf16[20,4,2,512]{3,2,1,0:T(2,128)(2,1)} %param.4), kind=kLoop, calls=%fused_computation.85 | loop fusion | bytes 327680
  2.7 0.9 %broadcast_in_dim.67 = bf16[24,4,2,2,512]{4,3,0,2,1:T(2,128)(2,1)} broadcast(bf16[24,4,2,512]{3,2,0,1:T(2,128)(2,1)S(1)} %copy.18), dimensions={0,1,3,4} | broadcast | bytes 589824 | tf_op jit(solution)/shard_map/broadcast_in_dim | solution.py:121
  3.6 7.3 %all-to-all-start = ((bf16[24,8,2,512]{3,2,0,1:T(2,128)(2,1)}), bf16[24,8,2,512]{3,2,0,1:T(2,128)(2,1)S(1)}, u32[]{:S(2)}, u32[]{:S(2)}) async-start(bf16[24,8,2,512]{3,2,0,1:T(2,128)(2,1)} %bitcast.3), calls=%async_computation | async-start | bytes 786432 | tf_op jit(solution)/shard_map/all_to_all | solution.py:122
  10.9 0.6 copy-done.2
  11.6 0.6 dynamic_slice.7
  12.3 10.3 %all-to-all-done = bf16[24,8,2,512]{3,2,0,1:T(2,128)(2,1)S(1)} async-done(((bf16[24,8,2,512]{3,2,0,1:T(2,128)(2,1)}), bf16[24,8,2,512]{3,2,0,1:T(2,128)(2,1)S(1)}, u32[]{:S(2)}, u32[]{:S(2)}) %all-to-all-start) | async-done | bytes 393248 | tf_op jit(solution)/shard_map/all_to_all | solution.py:122
  22.9 0.5 copy.20
  23.5 0.5 reshape.363
  24.0 0.7 fusion.29
  26.6 0.4 select_reduce_fusion.2
  28.9 0.4 fusion.13
  29.3 0.7 broadcast_in_dim.69
  29.9 3.3 %all-to-all-start.1 = ((f32[4,16,512]{2,1,0:T(8,128)}), f32[4,16,512]{2,1,0:T(8,128)S(1)}, u32[]{:S(2)}, u32[]{:S(2)}) async-start(f32[4,16,512]{2,1,0:T(8,128)} %broadcast_in_dim.69), calls=%async_computation.1 | async-start | bytes 262144 | tf_op jit(solution)/shard_map/all_to_all | solution.py:101
  33.3 4.5 %all-to-all-done.1 = f32[4,16,512]{2,1,0:T(8,128)S(1)} async-done(((f32[4,16,512]{2,1,0:T(8,128)}), f32[4,16,512]{2,1,0:T(8,128)S(1)}, u32[]{:S(2)}, u32[]{:S(2)}) %all-to-all-start.1) | async-done | bytes 131104 | tf_op jit(solution)/shard_map/all_to_all | solution.py:101
  37.9 0.8 %fusion.34 = (f32[512]{0:T(512)S(1)}, f32[1,8,2,512]{3,2,0,1:T(2,128)S(1)}) fusion(f32[1,8,2,512]{3,2,1,0:T(2,128)S(1)} %reduce_sum.172, pred[8,2]{1,0:T(8,128)(4,1)S(1)} %fusion.38, s32[]{:T(128)S(6)} %select_n.97, s32[8,2]{1,0:T(8,128)S(1)} %get-tuple-element.71, s32[8,2]{1,0:T(8,128)S(1)} %get-tuple-element.72, f32[]{:T(128)} %bitcast.4, ...), kind=kLoop, calls=%fused_computation.68 | loop fusion | flops 65024 | bytes 84120 | tf_op jit(solution)/shard_map/reduce_sum | solution.py:137
  40.7 0.4 fusion.20
  42.9 0.4 fusion.28
  43.6 13.1 %all_to_all.24 = f32[32,3,512]{2,1,0:T(4,128)S(1)} all-to-all(f32[32,3,512]{2,1,0:T(4,128)S(1)} %pad_maximum_fusion), channel_id=1, replica_groups=mesh['grid'=8,'mem'=4] {'grid','mem'}, dimensions={0} | all-to-all | bytes 393216 | tf_op jit(solution)/shard_map/all_to_all | solution.py:93
  57.5 0.7 broadcast_in_dim.75
  58.1 2.7 %all-to-all-start.3 = ((f32[32,1,512]{2,1,0:T(1,128)}), f32[32,1,512]{2,1,0:T(1,128)S(1)}, u32[]{:S(2)}, u32[]{:S(2)}) async-start(f32[32,1,512]{2,1,0:T(1,128)} %broadcast_in_dim.75), calls=%async_computation.3 | async-start | bytes 131072 | tf_op jit(solution)/shard_map/all_to_all | solution.py:93
  60.8 7.4 %all-to-all-done.3 = f32[32,1,512]{2,1,0:T(1,128)S(1)} async-done(((f32[32,1,512]{2,1,0:T(1,128)}), f32[32,1,512]{2,1,0:T(1,128)S(1)}, u32[]{:S(2)}, u32[]{:S(2)}) %all-to-all-start.3) | async-done | bytes 65568 | tf_op jit(solution)/shard_map/all_to_all | solution.py:93
  68.5 0.8 %add_convert_fusion = bf16[20,4,2,512]{3,2,1,0:T(2,128)(2,1)} fusion(bf16[20,4,2,512]{3,2,1,0:T(2,128)(2,1)S(1)} %copy-done, f32[4,2,512]{2,1,0:T(2,128)S(1)} %multiply_add_fusion.8), kind=kLoop, calls=%fused_computation.50 | loop fusion | flops 245760 | bytes 344064 | tf_op jit(solution)/shard_map/convert_element_type | solution.py:186
  69.3 0.6 constant_dynamic-slice_fusion
  (88 shorter events, 9.4 us)
Async XLA Ops:
  1.4 1.1 %copy-start.1 = (f32[4,2,512]{2,1,0:T(2,128)S(1)}, f32[4,2,512]{2,1,0:T(2,128)}, u32[]{:S(2)}) copy-start(f32[4,2,512]{2,1,0:T(2,128)} %param.5) | copy-start | bytes 49156
  3.6 19.0 %all-to-all-start = ((bf16[24,8,2,512]{3,2,0,1:T(2,128)(2,1)}), bf16[24,8,2,512]{3,2,0,1:T(2,128)(2,1)S(1)}, u32[]{:S(2)}, u32[]{:S(2)}) async-start(bf16[24,8,2,512]{3,2,0,1:T(2,128)(2,1)} %bitcast.3), calls=%async_computation | async-start | bytes 786432 | tf_op jit(solution)/shard_map/all_to_all | solution.py:122
  10.9 0.7 copy-start.2
  29.9 7.9 %all-to-all-start.1 = ((f32[4,16,512]{2,1,0:T(8,128)}), f32[4,16,512]{2,1,0:T(8,128)S(1)}, u32[]{:S(2)}, u32[]{:S(2)}) async-start(f32[4,16,512]{2,1,0:T(8,128)} %broadcast_in_dim.69), calls=%async_computation.1 | async-start | bytes 262144 | tf_op jit(solution)/shard_map/all_to_all | solution.py:101
  58.1 10.4 %copy-start = (bf16[20,4,2,512]{3,2,1,0:T(2,128)(2,1)S(1)}, bf16[20,4,2,512]{3,2,1,0:T(2,128)(2,1)}, u32[]{:S(2)}) copy-start(bf16[20,4,2,512]{3,2,1,0:T(2,128)(2,1)} %param.4) | copy-start | bytes 491524
  58.1 10.1 %all-to-all-start.3 = ((f32[32,1,512]{2,1,0:T(1,128)}), f32[32,1,512]{2,1,0:T(1,128)S(1)}, u32[]{:S(2)}, u32[]{:S(2)}) async-start(f32[32,1,512]{2,1,0:T(1,128)} %broadcast_in_dim.75), calls=%async_computation.3 | async-start | bytes 131072 | tf_op jit(solution)/shard_map/all_to_all | solution.py:93

commit v8 on v7

--- a/solution.py
+++ b/solution.py
@@ -118,13 +118,14 @@
     middle = lax.reduce_precision(rest, exponent_bits=8, mantissa_bits=7)
     low = rest - middle
     parts = jnp.stack([high, middle, low]).astype(jnp.bfloat16)
-    packed = jnp.repeat(jnp.concatenate([members, counts, parts], axis=0), copies, axis=1)
-    got = lax.all_to_all(packed, "grid", 1, 2, tiled=True)[:, 0]
-    split = got[count + 1 :].astype(jnp.float32)
+    packed = jnp.transpose(jnp.concatenate([members, counts, parts], axis=0), (1, 2, 0, 3))
+    got = lax.all_to_all(jnp.repeat(packed, copies, axis=0), "grid", 0, 0, tiled=True)
+    received = jnp.transpose(got, (2, 0, 1, 3)).reshape(count + 4, nlat, nlon).astype(jnp.float32)
+    split = received[count + 1 :]
     innov = (split[0] + split[1]) + split[2]
     precision = lax.dynamic_index_in_dim(obs_precision, level, 0, keepdims=False)
-    weight = got[count].astype(jnp.float32) * precision
-    widened = got[:count].astype(jnp.float32)
+    weight = received[count] * precision
+    widened = received[:count]
 
     span = nlat // copies
     own = (lax.broadcasted_iota(jnp.int32, (nlat, nlon), 0) // span) == grid_index % copies

time: 70.4 us -> 72.2 us (1.026)
  local copies, waits for them, and re-layouts: 10.6 us -> 12.6 us
    unnamed x8 -> x22, local copies, waits for them, and re-layouts: 1.71 us -> 3.21 us
    convert_element_type x2 -> x0, local copies, waits for them, and re-layouts: 0.96 us -> none  [local_by_level(): widened = got[:count].astype(jnp.float32)]
    reduce_sum x1, other arithmetic: 0.4 us -> 1.29 us  [local_by_level(): total1 = mem_total(jnp.sum(widened * smooth_rows(residual), axis=0))]
    slice x1 -> x3, local copies, waits for them, and re-layouts: 0.23 us -> 1.03 us  [local_by_level(): widened = received[:count]]
where the time goes in v8:
time: 72.2 us; the launch traced here: 71.7 us
  waiting for transfers between devices  21.7 us (30%)
  starting transfers between devices  13.3 us (18%)
  blocking collectives  13.1 us (18%)
  local copies, waits for them, and re-layouts  12.6 us (17%)
  other arithmetic  9.51 us (13%)
  between operations  1.2 us (2%)
    all_to_all x1, blocking collectives, exchange(): got = lax.all_to_all(parcel, ('grid', 'mem'), 0, 0, tiled=True)  13.1 us
    all_to_all x1, waiting for transfers between devices, local_by_level(): lax.all_to_all(jnp.repeat(packed, copies, axis=0), 'grid', 0, 0, tiled=True)  9.76 us
    all_to_all x1, waiting for transfers between devices, exchange(): got = lax.all_to_all(parcel, ('grid', 'mem'), 0, 0, tiled=True)  7.41 us
    all_to_all x1, starting transfers between devices, local_by_level(): lax.all_to_all(jnp.repeat(packed, copies, axis=0), 'grid', 0, 0, tiled=True)  7.28 us
    all_to_all x1, waiting for transfers between devices, mem_total(): lax.all_to_all(jnp.broadcast_to(part, (mem_size,) + part.shape), 'mem', 0...  4.55 us
    all_to_all x1, starting transfers between devices, mem_total(): lax.all_to_all(jnp.broadcast_to(part, (mem_size,) + part.shape), 'mem', 0...  3.33 us
    unnamed x22, local copies, waits for them, and re-layouts  3.21 us
    slice x14, local copies, waits for them, and re-layouts, smooth_rows(): jnp.roll(field, -1, -1)  3.19 us
  transfers between devices with their start and end apart: 3, of which 3 were waited for; matrix products, arithmetic and copies ran while one was open for 1% of the time, Pallas kernels for 0%

profile of v8, /device:TPU:0, one launch (start us, length us, event | category | flops | bytes accessed | tf_op | source)
XLA Modules:
  0.0 71.7 jit_solution(1944877117764701667)
XLA Ops:
  0.6 0.8 %fusion.71 = (bf16[2,512]{1,0:T(2,128)(2,1)S(1)}, f32[2,512]{1,0:T(2,128)S(1)}) fusion(s32[2,512]{1,0:T(2,128)} %param.6), kind=kLoop, calls=%fused_computation.149 | loop fusion | flops 2048 | bytes 10240 | tf_op jit(solution)/shard_map/convert_element_type | solution.py:115
  1.4 1.0 %constant_dynamic-update-slice_fusion.4 = bf16[24,4,2,512]{3,2,1,0:T(2,128)(2,1)S(1)} fusion(bf16[20,4,2,512]{3,2,1,0:T(2,128)(2,1)} %param.4), kind=kLoop, calls=%fused_computation.86 | loop fusion | bytes 327680
  2.7 0.9 %broadcast_in_dim.67 = bf16[4,2,2,24,512]{4,2,3,1,0:T(2,128)(2,1)} broadcast(bf16[4,2,24,512]{3,1,2,0:T(2,128)(2,1)S(1)} %copy.11), dimensions={0,2,3,4} | broadcast | bytes 589824 | tf_op jit(solution)/shard_map/broadcast_in_dim | solution.py:122
  3.6 7.3 %all-to-all-start = ((bf16[8,2,24,512]{3,1,2,0:T(2,128)(2,1)}), bf16[8,2,24,512]{3,1,2,0:T(2,128)(2,1)S(1)}, u32[]{:S(2)}, u32[]{:S(2)}) async-start(bf16[8,2,24,512]{3,1,2,0:T(2,128)(2,1)} %bitcast.4), calls=%async_computation | async-start | bytes 786432 | tf_op jit(solution)/shard_map/all_to_all | solution.py:122
  10.9 0.6 copy-done.8
  11.6 0.6 dynamic_slice.7
  12.2 0.6 copy-done.2
  12.8 9.8 %all-to-all-done = bf16[8,2,24,512]{3,1,2,0:T(2,128)(2,1)S(1)} async-done(((bf16[8,2,24,512]{3,1,2,0:T(2,128)(2,1)}), bf16[8,2,24,512]{3,1,2,0:T(2,128)(2,1)S(1)}, u32[]{:S(2)}, u32[]{:S(2)}) %all-to-all-start) | async-done | bytes 393248 | tf_op jit(solution)/shard_map/all_to_all | solution.py:122
  23.5 0.5 slice.205
  23.9 0.7 slice_add_fusion
  28.8 0.8 %fusion.60 = (f32[20,16,1]{2,1,0:T(8,128)S(1)}, f32[20,16,1]{2,1,0:T(8,128)}) fusion(f32[20,16,512]{2,1,0:T(8,128)S(1)} %fusion.8), kind=kLoop, calls=%fused_computation.138 | loop fusion | bytes 5120 | tf_op jit(solution)/shard_map/jit(_roll_static)/slice | solution.py:82
  29.6 1.3 %fusion.13 = f32[16,512]{1,0:T(8,128)S(1)} fusion(f32[20,16,512]{2,1,0:T(8,128)S(1)} %slice.205, f32[20,16,512]{2,1,0:T(8,128)S(1)} %fusion.8, f32[20,16,511]{2,1,0:T(8,128)S(1)} %get-tuple-element.36, f32[20,16,1]{2,1,0:T(8,128)} %get-tuple-element.38, f32[20,16,1]{2,1,0:T(8,128)S(1)} %get-tuple-element.37, f32[20,16,511]{2,1,0:T(8,128)S(1)} %get-tuple-element.35), kind=kLoop, calls=%fused_computation.18 | loop fusion | flops 1466368 | bytes 2654208 | tf_op jit(solution)/shard_map/reduce_sum | solution.py:144
  30.9 0.7 broadcast_in_dim.69
  31.5 3.3 %all-to-all-start.1 = ((f32[4,16,512]{2,1,0:T(8,128)}), f32[4,16,512]{2,1,0:T(8,128)S(1)}, u32[]{:S(2)}, u32[]{:S(2)}) async-start(f32[4,16,512]{2,1,0:T(8,128)} %broadcast_in_dim.69), calls=%async_computation.1 | async-start | bytes 262144 | tf_op jit(solution)/shard_map/all_to_all | solution.py:101
  34.9 4.5 %all-to-all-done.1 = f32[4,16,512]{2,1,0:T(8,128)S(1)} async-done(((f32[4,16,512]{2,1,0:T(8,128)}), f32[4,16,512]{2,1,0:T(8,128)S(1)}, u32[]{:S(2)}, u32[]{:S(2)}) %all-to-all-start.1) | async-done | bytes 131104 | tf_op jit(solution)/shard_map/all_to_all | solution.py:101
  41.4 0.4 fusion.20
  43.7 0.4 fusion.28
  44.8 13.1 %all_to_all.20 = f32[32,3,512]{2,1,0:T(4,128)S(1)} all-to-all(f32[32,3,512]{2,1,0:T(4,128)S(1)} %pad_maximum_fusion), channel_id=1, replica_groups=mesh['grid'=8,'mem'=4] {'grid','mem'}, dimensions={0} | all-to-all | bytes 393216 | tf_op jit(solution)/shard_map/all_to_all | solution.py:93
  58.4 0.6 copy-done.9
  59.3 0.7 broadcast_in_dim.75
  59.9 2.7 %all-to-all-start.3 = ((f32[32,1,512]{2,1,0:T(1,128)}), f32[32,1,512]{2,1,0:T(1,128)S(1)}, u32[]{:S(2)}, u32[]{:S(2)}) async-start(f32[32,1,512]{2,1,0:T(1,128)} %broadcast_in_dim.75), calls=%async_computation.3 | async-start | bytes 131072 | tf_op jit(solution)/shard_map/all_to_all | solution.py:93
  62.6 7.4 %all-to-all-done.3 = f32[32,1,512]{2,1,0:T(1,128)S(1)} async-done(((f32[32,1,512]{2,1,0:T(1,128)}), f32[32,1,512]{2,1,0:T(1,128)S(1)}, u32[]{:S(2)}, u32[]{:S(2)}) %all-to-all-start.3) | async-done | bytes 65568 | tf_op jit(solution)/shard_map/all_to_all | solution.py:93
  70.3 0.8 %add_convert_fusion = bf16[20,4,2,512]{3,2,1,0:T(2,128)(2,1)} fusion(bf16[20,4,2,512]{3,2,1,0:T(2,128)(2,1)S(1)} %copy-done, f32[4,2,512]{2,1,0:T(2,128)S(1)} %multiply_add_fusion.8), kind=kLoop, calls=%fused_computation.50 | loop fusion | flops 245760 | bytes 344064 | tf_op jit(solution)/shard_map/convert_element_type | solution.py:187
  71.1 0.6 constant_dynamic-slice_fusion
  (99 shorter events, 10.5 us)
Async XLA Ops:
  1.4 1.1 %copy-start.1 = (f32[4,2,512]{2,1,0:T(2,128)S(1)}, f32[4,2,512]{2,1,0:T(2,128)}, u32[]{:S(2)}) copy-start(f32[4,2,512]{2,1,0:T(2,128)} %param.5) | copy-start | bytes 49156
  3.6 19.0 %all-to-all-start = ((bf16[8,2,24,512]{3,1,2,0:T(2,128)(2,1)}), bf16[8,2,24,512]{3,1,2,0:T(2,128)(2,1)S(1)}, u32[]{:S(2)}, u32[]{:S(2)}) async-start(bf16[8,2,24,512]{3,1,2,0:T(2,128)(2,1)} %bitcast.4), calls=%async_computation | async-start | bytes 786432 | tf_op jit(solution)/shard_map/all_to_all | solution.py:122
  10.9 0.7 copy-start.8
  12.2 0.6 copy-start.2
  12.2 0.6 copy-start.4
  12.2 0.6 copy-start.6
  31.5 7.9 %all-to-all-start.1 = ((f32[4,16,512]{2,1,0:T(8,128)}), f32[4,16,512]{2,1,0:T(8,128)S(1)}, u32[]{:S(2)}, u32[]{:S(2)}) async-start(f32[4,16,512]{2,1,0:T(8,128)} %broadcast_in_dim.69), calls=%async_computation.1 | async-start | bytes 262144 | tf_op jit(solution)/shard_map/all_to_all | solution.py:101
  43.7 0.7 copy-start.3
  43.7 0.7 copy-start.5
  43.7 0.7 copy-start.7
  58.4 0.7 copy-start.9
  59.9 10.4 %copy-start = (bf16[20,4,2,512]{3,2,1,0:T(2,128)(2,1)S(1)}, bf16[20,4,2,512]{3,2,1,0:T(2,128)(2,1)}, u32[]{:S(2)}) copy-start(bf16[20,4,2,512]{3,2,1,0:T(2,128)(2,1)} %param.4) | copy-start | bytes 491524
  59.9 10.1 %all-to-all-start.3 = ((f32[32,1,512]{2,1,0:T(1,128)}), f32[32,1,512]{2,1,0:T(1,128)S(1)}, u32[]{:S(2)}, u32[]{:S(2)}) async-start(f32[32,1,512]{2,1,0:T(1,128)} %broadcast_in_dim.75), calls=%async_computation.3 | async-start | bytes 131072 | tf_op jit(solution)/shard_map/all_to_all | solution.py:93

commit v9 on v7

--- a/solution.py
+++ b/solution.py
@@ -1,6 +1,8 @@
 import jax
 import jax.numpy as jnp
 from jax import lax
+from jax.experimental import pallas as pl
+from jax.experimental.pallas import tpu as pltpu
 from jax.sharding import PartitionSpec as P
 
 PASSES = 2
@@ -83,6 +85,44 @@
     return field
 
 
+def smooth_in_kernel(field):
+    rows, nlon = field.shape[-2], field.shape[-1]
+    lat, lon = field.ndim - 2, field.ndim - 1
+    row = lax.broadcasted_iota(jnp.int32, field.shape, lat)
+    keep_ahead = jnp.abs(pltpu.roll(row, 1, lat) - row) == 1
+    keep_behind = jnp.abs(pltpu.roll(row, rows - 1, lat) - row) == 1
+    for sweep_index in range(PASSES):
+        ahead = jnp.where(keep_ahead, pltpu.roll(field, 1, lat), 0.0)
+        behind = jnp.where(keep_behind, pltpu.roll(field, rows - 1, lat), 0.0)
+        field = field + diffusion * (ahead + behind - 2.0 * field)
+    for sweep_index in range(PASSES):
+        field = field + diffusion * (pltpu.roll(field, 1, lon) + pltpu.roll(field, nlon - 1, lon) - 2.0 * field)
+    return field
+
+
+def gradient_kernel(members_ref, forcing_ref, residual_ref, total_ref):
+    widened = members_ref[...]
+    residual = smooth_in_kernel(widened * forcing_ref[...][None])
+    residual_ref[...] = residual
+    total_ref[...] = jnp.sum(widened * smooth_in_kernel(residual), axis=0)
+
+
+def image_kernel(members_ref, weight_ref, total_ref, residual_ref, image_ref, part_ref):
+    widened = members_ref[...]
+    image = residual_ref[...] + smooth_in_kernel(widened * (weight_ref[...] * total_ref[...])[None])
+    image_ref[...] = image
+    part_ref[...] = jnp.sum(widened * smooth_in_kernel(image), axis=0)
+
+
+def in_vmem(kernel, outs, *args):
+    return pl.pallas_call(
+        kernel,
+        out_shape=tuple(jax.ShapeDtypeStruct(s, jnp.float32) for s in outs),
+        in_specs=[pl.BlockSpec(memory_space=pltpu.VMEM)] * len(args),
+        out_specs=tuple(pl.BlockSpec(memory_space=pltpu.VMEM) for _ in outs),
+    )(*args)
+
+
 def exchange(values, rows_for):
     devices = lax.axis_size("grid") * lax.axis_size("mem")
     nlon = rows_for.shape[-1]
@@ -139,10 +179,10 @@
     def by_target(field):
         return jnp.repeat(field.reshape(grid_size, rows, nlon), mem_size, axis=0)
 
-    residual = smooth_rows(widened * (weight * innov)[None])
-    total1 = mem_total(jnp.sum(widened * smooth_rows(residual), axis=0))
-    image = residual + smooth_rows(widened * (weight * total1)[None])
-    image_part = jnp.sum(widened * smooth_rows(image), axis=0)
+    field, plane = (count, nlat, nlon), (nlat, nlon)
+    residual, total1_part = in_vmem(gradient_kernel, (field, plane), widened, weight * innov)
+    total1 = mem_total(total1_part)
+    image, image_part = in_vmem(image_kernel, (field, plane), widened, weight, total1, residual)
 
     if copies > 1:
         rows_for = jnp.where(grid_index % copies == 0, by_target(total1), by_target(image_part))

time: 70.4 us -> 73.2 us (1.040)
  Pallas kernels: 0 us -> 8.18 us
  other arithmetic: 9.2 us -> 6.68 us
  local copies, waits for them, and re-layouts: 10.6 us -> 8.95 us
  waiting for transfers between devices: 22.3 us -> 21.1 us
    pallas_call x0 -> x2, Pallas kernels: none -> 8.18 us  [in_vmem(): pl.pallas_call(kernel, out_shape=tuple((jax.ShapeDtypeStruct(s, jnp.float...]
    slice x24 -> x0, local copies, waits for them, and re-layouts: 3.85 us -> none  [the longest x14 2.49 us: smooth_rows(): jnp.roll(field, -1, -1)]
    add x13 -> x1, other arithmetic: 3.79 us -> 0.03 us  [local_by_level(): innov = split[0] + split[1] + split[2]]
    all_to_all x1, waiting for transfers between devices: 4.55 us -> 3.36 us  [mem_total(): lax.all_to_all(jnp.broadcast_to(part, (mem_size,) + part.shape), 'mem', 0...]
    convert_element_type x2, local copies, waits for them, and re-layouts: 0.96 us -> 1.82 us  [local_by_level(): widened = got[:count].astype(jnp.float32)]
    reduce_sum x2, other arithmetic: 0.55 us -> 1.38 us  [squares(): return jnp.sum(jnp.where(own[None], field * field, 0.0), axis=(0, 1))]
    reduce_sum x2 -> x0, other arithmetic: 0.8 us -> none  [the longest x1 0.4 us: local_by_level(): total1 = mem_total(jnp.sum(widened * smooth_rows(residual), axis=0))]
    select_n x1, other arithmetic: 0.01 us -> 0.77 us  [local_by_level(): jnp.where(grid_index % copies == 0, by_target(total1), by_target(image_pa...]
  transfers between devices with their start and end apart: 3 -> 3, of which waited for: 3 -> 3; matrix products, arithmetic and copies ran while one was open for 1% -> 3% of each run, Pallas kernels for 0% -> 0%
where the time goes in v9:
time: 73.2 us; the launch traced here: 72.5 us
  waiting for transfers between devices  21.1 us (29%)
  starting transfers between devices  13.3 us (18%)
  blocking collectives  13.1 us (18%)
  local copies, waits for them, and re-layouts  8.95 us (12%)
  Pallas kernels  8.18 us (11%)
  other arithmetic  6.68 us (9%)
  between operations  0.91 us (1%)
    all_to_all x1, blocking collectives, exchange(): got = lax.all_to_all(parcel, ('grid', 'mem'), 0, 0, tiled=True)  13.1 us
    all_to_all x1, waiting for transfers between devices, local_by_level(): got = lax.all_to_all(packed, 'grid', 1, 2, tiled=True)[:, 0]  10.3 us
    pallas_call x2, Pallas kernels, in_vmem(): pl.pallas_call(kernel, out_shape=tuple((jax.ShapeDtypeStruct(s, jnp.float...  8.18 us
    all_to_all x1, waiting for transfers between devices, exchange(): got = lax.all_to_all(parcel, ('grid', 'mem'), 0, 0, tiled=True)  7.41 us
    all_to_all x1, starting transfers between devices, local_by_level(): got = lax.all_to_all(packed, 'grid', 1, 2, tiled=True)[:, 0]  7.28 us
    all_to_all x1, waiting for transfers between devices, mem_total(): lax.all_to_all(jnp.broadcast_to(part, (mem_size,) + part.shape), 'mem', 0...  3.36 us
    all_to_all x1, starting transfers between devices, mem_total(): lax.all_to_all(jnp.broadcast_to(part, (mem_size,) + part.shape), 'mem', 0...  3.33 us
    all_to_all x1, starting transfers between devices, exchange(): got = lax.all_to_all(parcel, ('grid', 'mem'), 0, 0, tiled=True)  2.7 us
  transfers between devices with their start and end apart: 3, of which 3 were waited for; matrix products, arithmetic and copies ran while one was open for 3% of the time, Pallas kernels for 0%

profile of v9, /device:TPU:0, one launch (start us, length us, event | category | flops | bytes accessed | tf_op | source)
XLA Modules:
  0.0 72.5 jit_solution(17427139386774725959)
XLA Ops:
  0.6 0.8 %fusion.17 = (bf16[2,512]{1,0:T(2,128)(2,1)S(1)}, f32[2,512]{1,0:T(2,128)S(1)}) fusion(s32[2,512]{1,0:T(2,128)} %param.6), kind=kLoop, calls=%fused_computation.82 | loop fusion | flops 2048 | bytes 10240 | tf_op jit(solution)/shard_map/convert_element_type | solution.py:155
  1.4 1.0 %constant_dynamic-update-slice_fusion.4 = bf16[24,4,2,512]{3,2,1,0:T(2,128)(2,1)S(1)} fusion(bf16[20,4,2,512]{3,2,1,0:T(2,128)(2,1)} %param.4), kind=kLoop, calls=%fused_computation.37 | loop fusion | bytes 327680
  2.7 0.9 %broadcast_in_dim.65 = bf16[24,4,2,2,512]{4,3,0,2,1:T(2,128)(2,1)} broadcast(bf16[24,4,2,512]{3,2,0,1:T(2,128)(2,1)S(1)} %copy.19), dimensions={0,1,3,4} | broadcast | bytes 589824 | tf_op jit(solution)/shard_map/broadcast_in_dim | solution.py:161
  3.6 7.3 %all-to-all-start = ((bf16[24,8,2,512]{3,2,0,1:T(2,128)(2,1)}), bf16[24,8,2,512]{3,2,0,1:T(2,128)(2,1)S(1)}, u32[]{:S(2)}, u32[]{:S(2)}) async-start(bf16[24,8,2,512]{3,2,0,1:T(2,128)(2,1)} %bitcast.3), calls=%async_computation | async-start | bytes 786432 | tf_op jit(solution)/shard_map/all_to_all | solution.py:162
  10.9 0.6 copy-done.6
  11.6 0.6 dynamic_slice.7
  12.3 10.3 %all-to-all-done = bf16[24,8,2,512]{3,2,0,1:T(2,128)(2,1)S(1)} async-done(((bf16[24,8,2,512]{3,2,0,1:T(2,128)(2,1)}), bf16[24,8,2,512]{3,2,0,1:T(2,128)(2,1)S(1)}, u32[]{:S(2)}, u32[]{:S(2)}) %all-to-all-start) | async-done | bytes 393248 | tf_op jit(solution)/shard_map/all_to_all | solution.py:162
  22.6 0.7 convert_multiply_fusion
  24.3 1.3 %reshape.342.members_ref = f32[20,16,512]{2,1,0:T(8,128)} reshape(f32[20,8,2,512]{3,2,1,0:T(2,128)S(1)} %copy.21) | data formatting | bytes 1310720 | tf_op jit(solution)/shard_map/convert_element_type | solution.py:167
  25.6 0.6 mul.164.forcing_ref
  26.2 4.0 %shard_map.59 = (f32[20,16,512]{2,1,0:T(8,128)}, f32[16,512]{1,0:T(8,128)}) custom-call(f32[20,16,512]{2,1,0:T(8,128)} %reshape.342.members_ref, f32[16,512]{1,0:T(8,128)} %mul.164.forcing_ref), custom_call_target="tpu_custom_call" | custom-call | tf_op jit(solution)/shard_map/pallas_call | solution.py:118
  30.2 1.4 %broadcast_in_dim.67 = f32[4,16,512]{2,1,0:T(8,128)} broadcast(f32[16,512]{1,0:T(8,128)} %get-tuple-element.7), dimensions={1,2} | broadcast | bytes 163840 | tf_op jit(solution)/shard_map/broadcast_in_dim | solution.py:141
  31.6 3.3 %all-to-all-start.1 = ((f32[4,16,512]{2,1,0:T(8,128)}), f32[4,16,512]{2,1,0:T(8,128)S(1)}, u32[]{:S(2)}, u32[]{:S(2)}) async-start(f32[4,16,512]{2,1,0:T(8,128)} %broadcast_in_dim.67), calls=%async_computation.1 | async-start | bytes 262144 | tf_op jit(solution)/shard_map/all_to_all | solution.py:141
  34.9 1.2 %select_reduce_fusion.2 = f32[512]{0:T(512)S(1)} fusion(f32[20,16,512]{2,1,0:T(8,128)} %get-tuple-element.6.residual_ref, pred[16,512]{1,0:T(8,128)(4,1)S(1)} %select_compare_fusion), kind=kLoop, calls=%fused_computation.3 | loop fusion | flops 491008 | bytes 665600 | tf_op jit(solution)/shard_map/reduce_sum | solution.py:174
  36.1 3.4 %all-to-all-done.1 = f32[4,16,512]{2,1,0:T(8,128)S(1)} async-done(((f32[4,16,512]{2,1,0:T(8,128)}), f32[4,16,512]{2,1,0:T(8,128)S(1)}, u32[]{:S(2)}, u32[]{:S(2)}) %all-to-all-start.1) | async-done | bytes 131104 | tf_op jit(solution)/shard_map/all_to_all | solution.py:141
  40.1 4.2 %shard_map.60 = (f32[20,16,512]{2,1,0:T(8,128)}, f32[16,512]{1,0:T(8,128)}) custom-call(f32[20,16,512]{2,1,0:T(8,128)} %reshape.342.members_ref, f32[16,512]{1,0:T(8,128)} %copy-done.4, f32[16,512]{1,0:T(8,128)} %copy-done.3, f32[20,16,512]{2,1,0:T(8,128)} %get-tuple-element.6.residual_ref), custom_call_target="tpu_custom_call" | custom-call | tf_op jit(solution)/shard_map/pallas_call | solution.py:118
  44.3 0.8 %broadcast_select_fusion = f32[16,512]{1,0:T(8,128)S(1)} fusion(f32[16,512]{1,0:T(8,128)} %copy-done.3, f32[16,512]{1,0:T(8,128)} %get-tuple-element.8, pred[]{:T(512)S(6)} %eq.35), kind=kLoop, calls=%fused_computation.32 | loop fusion | flops 8192 | bytes 98305 | tf_op jit(solution)/shard_map/jit(_where)/select_n | solution.py:188
  45.1 0.8 %fusion.4 = f32[512]{0:T(512)S(1)} fusion(f32[1,8,2,512]{3,2,1,0:T(2,128)S(1)} %reduce_sum.153, pred[8,2]{1,0:T(8,128)(4,1)S(1)} %fusion.8, s32[]{:T(128)S(6)} %select_n.97, s32[8,2]{1,0:T(8,128)S(1)} %get-tuple-element.25, s32[8,2]{1,0:T(8,128)S(1)} %get-tuple-element.26, f32[]{:T(128)} %bitcast.4, bf16[24,8,2,512]{3,2,0,1:T(2,128)(2,1)S(1)} %all-to-all-done), kind=kLoop, calls=%fused_computation.20 | loop fusion | flops 65024 | bytes 51352 | tf_op jit(solution)/shard_map/reduce_sum | solution.py:177
  46.2 13.1 %all_to_all.24 = f32[32,3,512]{2,1,0:T(4,128)S(1)} all-to-all(f32[32,3,512]{2,1,0:T(4,128)S(1)} %pad_maximum_fusion), channel_id=1, replica_groups=mesh['grid'=8,'mem'=4] {'grid','mem'}, dimensions={0} | all-to-all | bytes 393216 | tf_op jit(solution)/shard_map/all_to_all | solution.py:133
  60.0 0.7 broadcast_in_dim.73
  60.7 2.7 %all-to-all-start.3 = ((f32[32,1,512]{2,1,0:T(1,128)}), f32[32,1,512]{2,1,0:T(1,128)S(1)}, u32[]{:S(2)}, u32[]{:S(2)}) async-start(f32[32,1,512]{2,1,0:T(1,128)} %broadcast_in_dim.73), calls=%async_computation.3 | async-start | bytes 131072 | tf_op jit(solution)/shard_map/all_to_all | solution.py:133
  63.4 7.4 %all-to-all-done.3 = f32[32,1,512]{2,1,0:T(1,128)S(1)} async-done(((f32[32,1,512]{2,1,0:T(1,128)}), f32[32,1,512]{2,1,0:T(1,128)S(1)}, u32[]{:S(2)}, u32[]{:S(2)}) %all-to-all-start.3) | async-done | bytes 65568 | tf_op jit(solution)/shard_map/all_to_all | solution.py:133
  71.1 0.8 %add_convert_fusion = bf16[20,4,2,512]{3,2,1,0:T(2,128)(2,1)} fusion(bf16[20,4,2,512]{3,2,1,0:T(2,128)(2,1)S(1)} %copy-done.1, f32[4,2,512]{2,1,0:T(2,128)S(1)} %multiply_add_fusion), kind=kLoop, calls=%fused_computation.5 | loop fusion | flops 245760 | bytes 344064 | tf_op jit(solution)/shard_map/convert_element_type | solution.py:226
  71.9 0.6 constant_dynamic-slice_fusion
  (58 shorter events, 3.1 us)
Async XLA Ops:
  1.4 1.1 %copy-start.5 = (f32[4,2,512]{2,1,0:T(2,128)S(1)}, f32[4,2,512]{2,1,0:T(2,128)}, u32[]{:S(2)}) copy-start(f32[4,2,512]{2,1,0:T(2,128)} %param.5) | copy-start | bytes 49156
  3.6 19.0 %all-to-all-start = ((bf16[24,8,2,512]{3,2,0,1:T(2,128)(2,1)}), bf16[24,8,2,512]{3,2,0,1:T(2,128)(2,1)S(1)}, u32[]{:S(2)}, u32[]{:S(2)}) async-start(bf16[24,8,2,512]{3,2,0,1:T(2,128)(2,1)} %bitcast.3), calls=%async_computation | async-start | bytes 786432 | tf_op jit(solution)/shard_map/all_to_all | solution.py:162
  10.9 0.7 copy-start.6
  23.3 2.3 %copy-start.4 = (f32[16,512]{1,0:T(8,128)}, f32[16,512]{1,0:T(8,128)S(1)}, u32[]{:S(2)}) copy-start(f32[16,512]{1,0:T(8,128)S(1)} %mul.163.weight_ref) | copy-start | bytes 98308
  31.6 7.9 %all-to-all-start.1 = ((f32[4,16,512]{2,1,0:T(8,128)}), f32[4,16,512]{2,1,0:T(8,128)S(1)}, u32[]{:S(2)}, u32[]{:S(2)}) async-start(f32[4,16,512]{2,1,0:T(8,128)} %broadcast_in_dim.67), calls=%async_computation.1 | async-start | bytes 262144 | tf_op jit(solution)/shard_map/all_to_all | solution.py:141
  39.5 0.6 copy-start.3
  45.9 13.6 %copy-start.2 = (f32[20,16,512]{2,1,0:T(8,128)S(1)}, f32[20,16,512]{2,1,0:T(8,128)}, u32[]{:S(2)}) copy-start(f32[20,16,512]{2,1,0:T(8,128)} %get-tuple-element.9) | copy-start | bytes 1966084
  45.9 13.6 %copy-start = (f32[20,16,512]{2,1,0:T(8,128)S(1)}, f32[20,16,512]{2,1,0:T(8,128)}, u32[]{:S(2)}) copy-start(f32[20,16,512]{2,1,0:T(8,128)} %get-tuple-element.6.residual_ref) | copy-start | bytes 1966084
  60.7 10.4 %copy-start.1 = (bf16[20,4,2,512]{3,2,1,0:T(2,128)(2,1)S(1)}, bf16[20,4,2,512]{3,2,1,0:T(2,128)(2,1)}, u32[]{:S(2)}) copy-start(bf16[20,4,2,512]{3,2,1,0:T(2,128)(2,1)} %param.4) | copy-start | bytes 491524
  60.7 10.1 %all-to-all-start.3 = ((f32[32,1,512]{2,1,0:T(1,128)}), f32[32,1,512]{2,1,0:T(1,128)S(1)}, u32[]{:S(2)}, u32[]{:S(2)}) async-start(f32[32,1,512]{2,1,0:T(1,128)} %broadcast_in_dim.73), calls=%async_computation.3 | async-start | bytes 131072 | tf_op jit(solution)/shard_map/all_to_all | solution.py:133

commit v10 on v9

--- a/solution.py
+++ b/solution.py
@@ -100,18 +100,11 @@
     return field
 
 
-def gradient_kernel(members_ref, forcing_ref, residual_ref, total_ref):
+def gradient_kernel(members_ref, weight_ref, innov_ref, residual_ref, total_ref):
     widened = members_ref[...]
-    residual = smooth_in_kernel(widened * forcing_ref[...][None])
+    residual = smooth_in_kernel(widened * (weight_ref[...] * innov_ref[...])[None])
     residual_ref[...] = residual
     total_ref[...] = jnp.sum(widened * smooth_in_kernel(residual), axis=0)
-
-
-def image_kernel(members_ref, weight_ref, total_ref, residual_ref, image_ref, part_ref):
-    widened = members_ref[...]
-    image = residual_ref[...] + smooth_in_kernel(widened * (weight_ref[...] * total_ref[...])[None])
-    image_ref[...] = image
-    part_ref[...] = jnp.sum(widened * smooth_in_kernel(image), axis=0)
 
 
 def in_vmem(kernel, outs, *args):
@@ -158,13 +151,14 @@
     middle = lax.reduce_precision(rest, exponent_bits=8, mantissa_bits=7)
     low = rest - middle
     parts = jnp.stack([high, middle, low]).astype(jnp.bfloat16)
-    packed = jnp.repeat(jnp.concatenate([members, counts, parts], axis=0), copies, axis=1)
-    got = lax.all_to_all(packed, "grid", 1, 2, tiled=True)[:, 0]
-    split = got[count + 1 :].astype(jnp.float32)
+    packed = jnp.transpose(jnp.concatenate([members, counts, parts], axis=0), (1, 2, 0, 3))
+    got = lax.all_to_all(jnp.repeat(packed, copies, axis=0), "grid", 0, 0, tiled=True)
+    received = jnp.transpose(got, (2, 0, 1, 3)).reshape(count + 4, nlat, nlon).astype(jnp.float32)
+    split = received[count + 1 :]
     innov = (split[0] + split[1]) + split[2]
     precision = lax.dynamic_index_in_dim(obs_precision, level, 0, keepdims=False)
-    weight = got[count].astype(jnp.float32) * precision
-    widened = got[:count].astype(jnp.float32)
+    weight = received[count] * precision
+    widened = received[:count]
 
     span = nlat // copies
     own = (lax.broadcasted_iota(jnp.int32, (nlat, nlon), 0) // span) == grid_index % copies
@@ -179,10 +173,10 @@
     def by_target(field):
         return jnp.repeat(field.reshape(grid_size, rows, nlon), mem_size, axis=0)
 
-    field, plane = (count, nlat, nlon), (nlat, nlon)
-    residual, total1_part = in_vmem(gradient_kernel, (field, plane), widened, weight * innov)
+    residual, total1_part = in_vmem(gradient_kernel, ((count, nlat, nlon), (nlat, nlon)), widened, weight, innov)
     total1 = mem_total(total1_part)
-    image, image_part = in_vmem(image_kernel, (field, plane), widened, weight, total1, residual)
+    image = residual + smooth_rows(widened * (weight * total1)[None])
+    image_part = jnp.sum(widened * smooth_rows(image), axis=0)
 
     if copies > 1:
         rows_for = jnp.where(grid_index % copies == 0, by_target(total1), by_target(image_part))

time: 73.2 us -> 73.3 us (level)
  Pallas kernels: 8.18 us -> 4.05 us
  local copies, waits for them, and re-layouts: 8.95 us -> 12.5 us
  waiting for transfers between devices: 21.1 us -> 22.3 us
    pallas_call x2 -> x1, Pallas kernels: 8.18 us -> 4.05 us  [in_vmem(): pl.pallas_call(kernel, out_shape=tuple((jax.ShapeDtypeStruct(s, jnp.float...]
    slice x1 -> x15, local copies, waits for them, and re-layouts: 0.23 us -> 3.78 us  [the longest x3 1.87 us: local_by_level(): widened = received[:count]]
    convert_element_type x2 -> x0, local copies, waits for them, and re-layouts: 1.82 us -> none  [local_by_level(): widened = got[:count].astype(jnp.float32)]
    add x0 -> x6, other arithmetic: none -> 1.72 us  [the longest x4 1.07 us: smooth_rows(): field = field + diffusion * (north + south - 2.0 * field)]
    mul x2, other arithmetic: 1.28 us -> 0.07 us  [local_by_level(): image = residual + smooth_rows(widened * (weight * total1)[None])]
    all_to_all x1, waiting for transfers between devices: 3.36 us -> 4.46 us  [mem_total(): lax.all_to_all(jnp.broadcast_to(part, (mem_size,) + part.shape), 'mem', 0...]
    select_n x1 -> x0, other arithmetic: 0.77 us -> none  [local_by_level(): jnp.where(grid_index % copies == 0, by_target(total1), by_target(image_pa...]
    unnamed x16 -> x14, local copies, waits for them, and re-layouts: 2.31 us -> 2.9 us
  transfers between devices with their start and end apart: 3 -> 3, of which waited for: 3 -> 3; matrix products, arithmetic and copies ran while one was open for 3% -> 1% of each run, Pallas kernels for 0% -> 0%
where the time goes in v10:
time: 73.3 us; the launch traced here: 72.7 us
  waiting for transfers between devices  22.3 us (30%)
  starting transfers between devices  13.3 us (18%)
  blocking collectives  13.1 us (18%)
  local copies, waits for them, and re-layouts  12.5 us (17%)
  other arithmetic  6.19 us (8%)
  Pallas kernels  4.05 us (6%)
  between operations  1 us (1%)
    all_to_all x1, blocking collectives, exchange(): got = lax.all_to_all(parcel, ('grid', 'mem'), 0, 0, tiled=True)  13.1 us
    all_to_all x1, waiting for transfers between devices, local_by_level(): lax.all_to_all(jnp.repeat(packed, copies, axis=0), 'grid', 0, 0, tiled=True)  10.4 us
    all_to_all x1, waiting for transfers between devices, exchange(): got = lax.all_to_all(parcel, ('grid', 'mem'), 0, 0, tiled=True)  7.41 us
    all_to_all x1, starting transfers between devices, local_by_level(): lax.all_to_all(jnp.repeat(packed, copies, axis=0), 'grid', 0, 0, tiled=True)  7.28 us
    all_to_all x1, waiting for transfers between devices, mem_total(): lax.all_to_all(jnp.broadcast_to(part, (mem_size,) + part.shape), 'mem', 0...  4.46 us
    pallas_call x1, Pallas kernels, in_vmem(): pl.pallas_call(kernel, out_shape=tuple((jax.ShapeDtypeStruct(s, jnp.float...  4.05 us
    all_to_all x1, starting transfers between devices, mem_total(): lax.all_to_all(jnp.broadcast_to(part, (mem_size,) + part.shape), 'mem', 0...  3.33 us
    unnamed x14, local copies, waits for them, and re-layouts  2.9 us
  transfers between devices with their start and end apart: 3, of which 3 were waited for; matrix products, arithmetic and copies ran while one was open for 1% of the time, Pallas kernels for 0%

profile of v10, /device:TPU:0, one launch (start us, length us, event | category | flops | bytes accessed | tf_op | source)
XLA Modules:
  0.0 72.7 jit_solution(12313687641360594687)
XLA Ops:
  0.6 0.8 %fusion.44 = (bf16[2,512]{1,0:T(2,128)(2,1)S(1)}, f32[2,512]{1,0:T(2,128)S(1)}) fusion(s32[2,512]{1,0:T(2,128)} %param.6), kind=kLoop, calls=%fused_computation.113 | loop fusion | flops 2048 | bytes 10240 | tf_op jit(solution)/shard_map/convert_element_type | solution.py:148
  1.4 1.0 %constant_dynamic-update-slice_fusion.4 = bf16[24,4,2,512]{3,2,1,0:T(2,128)(2,1)S(1)} fusion(bf16[20,4,2,512]{3,2,1,0:T(2,128)(2,1)} %param.4), kind=kLoop, calls=%fused_computation.62 | loop fusion | bytes 327680
  2.7 0.9 %broadcast_in_dim.66 = bf16[4,2,2,24,512]{4,2,3,1,0:T(2,128)(2,1)} broadcast(bf16[4,2,24,512]{3,1,2,0:T(2,128)(2,1)S(1)} %copy.10), dimensions={0,2,3,4} | broadcast | bytes 589824 | tf_op jit(solution)/shard_map/broadcast_in_dim | solution.py:155
  3.6 7.3 %all-to-all-start = ((bf16[8,2,24,512]{3,1,2,0:T(2,128)(2,1)}), bf16[8,2,24,512]{3,1,2,0:T(2,128)(2,1)S(1)}, u32[]{:S(2)}, u32[]{:S(2)}) async-start(bf16[8,2,24,512]{3,1,2,0:T(2,128)(2,1)} %bitcast.4), calls=%async_computation | async-start | bytes 786432 | tf_op jit(solution)/shard_map/all_to_all | solution.py:155
  10.9 0.6 copy-done.5
  11.6 0.6 dynamic_slice.7
  12.2 10.4 %all-to-all-done = bf16[8,2,24,512]{3,1,2,0:T(2,128)(2,1)S(1)} async-done(((bf16[8,2,24,512]{3,1,2,0:T(2,128)(2,1)}), bf16[8,2,24,512]{3,1,2,0:T(2,128)(2,1)S(1)}, u32[]{:S(2)}, u32[]{:S(2)}) %all-to-all-start) | async-done | bytes 393248 | tf_op jit(solution)/shard_map/all_to_all | solution.py:155
  23.5 1.3 %slice.133.members_ref = f32[20,16,512]{2,1,0:T(8,128)} reshape(f32[20,8,2,512]{3,2,1,0:T(2,128)S(1)} %copy.11) | data formatting | bytes 1310720 | tf_op jit(solution)/shard_map/slice | solution.py:161
  24.7 0.7 slice_add_fusion
  25.4 0.6 mul.225.weight_ref
  26.1 0.6 add.172.innov_ref
  26.7 4.1 %shard_map.59 = (f32[20,16,512]{2,1,0:T(8,128)}, f32[16,512]{1,0:T(8,128)}) custom-call(f32[20,16,512]{2,1,0:T(8,128)} %slice.133.members_ref, f32[16,512]{1,0:T(8,128)} %mul.225.weight_ref, f32[16,512]{1,0:T(8,128)} %add.172.innov_ref), custom_call_target="tpu_custom_call" | custom-call | tf_op jit(solution)/shard_map/pallas_call | solution.py:111
  30.7 1.4 %broadcast_in_dim.68 = f32[4,16,512]{2,1,0:T(8,128)} broadcast(f32[16,512]{1,0:T(8,128)} %get-tuple-element.5), dimensions={1,2} | broadcast | bytes 163840 | tf_op jit(solution)/shard_map/broadcast_in_dim | solution.py:134
  32.2 3.3 %all-to-all-start.1 = ((f32[4,16,512]{2,1,0:T(8,128)}), f32[4,16,512]{2,1,0:T(8,128)S(1)}, u32[]{:S(2)}, u32[]{:S(2)}) async-start(f32[4,16,512]{2,1,0:T(8,128)} %broadcast_in_dim.68), calls=%async_computation.1 | async-start | bytes 262144 | tf_op jit(solution)/shard_map/all_to_all | solution.py:134
  35.6 4.5 %all-to-all-done.1 = f32[4,16,512]{2,1,0:T(8,128)S(1)} async-done(((f32[4,16,512]{2,1,0:T(8,128)}), f32[4,16,512]{2,1,0:T(8,128)S(1)}, u32[]{:S(2)}, u32[]{:S(2)}) %all-to-all-start.1) | async-done | bytes 131104 | tf_op jit(solution)/shard_map/all_to_all | solution.py:134
  42.1 0.8 %copy-done.1 = f32[20,16,512]{2,1,0:T(8,128)S(1)} copy-done((f32[20,16,512]{2,1,0:T(8,128)S(1)}, f32[20,16,512]{2,1,0:T(8,128)}, u32[]{:S(2)}) %copy-start.1) | copy-done | bytes 655384
  42.9 0.5 select_reduce_fusion.2
  45.3 0.4 fusion.14
  46.4 13.1 %all_to_all.20 = f32[32,3,512]{2,1,0:T(4,128)S(1)} all-to-all(f32[32,3,512]{2,1,0:T(4,128)S(1)} %pad_maximum_fusion), channel_id=1, replica_groups=mesh['grid'=8,'mem'=4] {'grid','mem'}, dimensions={0} | all-to-all | bytes 393216 | tf_op jit(solution)/shard_map/all_to_all | solution.py:126
  60.2 0.7 broadcast_in_dim.74
  60.9 2.7 %all-to-all-start.3 = ((f32[32,1,512]{2,1,0:T(1,128)}), f32[32,1,512]{2,1,0:T(1,128)S(1)}, u32[]{:S(2)}, u32[]{:S(2)}) async-start(f32[32,1,512]{2,1,0:T(1,128)} %broadcast_in_dim.74), calls=%async_computation.3 | async-start | bytes 131072 | tf_op jit(solution)/shard_map/all_to_all | solution.py:126
  63.6 7.4 %all-to-all-done.3 = f32[32,1,512]{2,1,0:T(1,128)S(1)} async-done(((f32[32,1,512]{2,1,0:T(1,128)}), f32[32,1,512]{2,1,0:T(1,128)S(1)}, u32[]{:S(2)}, u32[]{:S(2)}) %all-to-all-start.3) | async-done | bytes 65568 | tf_op jit(solution)/shard_map/all_to_all | solution.py:126
  71.3 0.8 %add_convert_fusion = bf16[20,4,2,512]{3,2,1,0:T(2,128)(2,1)} fusion(bf16[20,4,2,512]{3,2,1,0:T(2,128)(2,1)S(1)} %copy-done.2, f32[4,2,512]{2,1,0:T(2,128)S(1)} %multiply_add_fusion.4), kind=kLoop, calls=%fused_computation.28 | loop fusion | flops 245760 | bytes 344064 | tf_op jit(solution)/shard_map/convert_element_type | solution.py:220
  72.1 0.6 constant_dynamic-slice_fusion
  (70 shorter events, 6.6 us)
Async XLA Ops:
  1.4 1.1 %copy-start.4 = (f32[4,2,512]{2,1,0:T(2,128)S(1)}, f32[4,2,512]{2,1,0:T(2,128)}, u32[]{:S(2)}) copy-start(f32[4,2,512]{2,1,0:T(2,128)} %param.5) | copy-start | bytes 49156
  3.6 19.0 %all-to-all-start = ((bf16[8,2,24,512]{3,1,2,0:T(2,128)(2,1)}), bf16[8,2,24,512]{3,1,2,0:T(2,128)(2,1)S(1)}, u32[]{:S(2)}, u32[]{:S(2)}) async-start(bf16[8,2,24,512]{3,1,2,0:T(2,128)(2,1)} %bitcast.4), calls=%async_computation | async-start | bytes 786432 | tf_op jit(solution)/shard_map/all_to_all | solution.py:155
  10.9 0.7 copy-start.5
  26.7 13.4 %copy-start = (f32[20,16,512]{2,1,0:T(8,128)S(1)}, f32[20,16,512]{2,1,0:T(8,128)}, u32[]{:S(2)}) copy-start(f32[20,16,512]{2,1,0:T(8,128)} %slice.133.members_ref) | copy-start | bytes 1966084
  32.2 7.9 %all-to-all-start.1 = ((f32[4,16,512]{2,1,0:T(8,128)}), f32[4,16,512]{2,1,0:T(8,128)S(1)}, u32[]{:S(2)}, u32[]{:S(2)}) async-start(f32[4,16,512]{2,1,0:T(8,128)} %broadcast_in_dim.68), calls=%async_computation.1 | async-start | bytes 262144 | tf_op jit(solution)/shard_map/all_to_all | solution.py:134
  41.8 1.1 %copy-start.1 = (f32[20,16,512]{2,1,0:T(8,128)S(1)}, f32[20,16,512]{2,1,0:T(8,128)}, u32[]{:S(2)}) copy-start(f32[20,16,512]{2,1,0:T(8,128)} %get-tuple-element.4) | copy-start | bytes 1966084
  45.2 0.8 %copy-start.3 = (f32[16,512]{1,0:T(8,128)S(1)}, f32[16,512]{1,0:T(8,128)}, u32[]{:S(2)}) copy-start(f32[16,512]{1,0:T(8,128)} %mul.225.weight_ref) | copy-start | bytes 98308
  60.9 10.4 %copy-start.2 = (bf16[20,4,2,512]{3,2,1,0:T(2,128)(2,1)S(1)}, bf16[20,4,2,512]{3,2,1,0:T(2,128)(2,1)}, u32[]{:S(2)}) copy-start(bf16[20,4,2,512]{3,2,1,0:T(2,128)(2,1)} %param.4) | copy-start | bytes 491524
  60.9 10.1 %all-to-all-start.3 = ((f32[32,1,512]{2,1,0:T(1,128)}), f32[32,1,512]{2,1,0:T(1,128)S(1)}, u32[]{:S(2)}, u32[]{:S(2)}) async-start(f32[32,1,512]{2,1,0:T(1,128)} %broadcast_in_dim.74), calls=%async_computation.3 | async-start | bytes 131072 | tf_op jit(solution)/shard_map/all_to_all | solution.py:126

commit v11 on v7

--- a/solution.py
+++ b/solution.py
@@ -73,14 +73,16 @@
 
 
 def smooth_rows(field):
-    for sweep_index in range(PASSES):
-        edge = jnp.zeros_like(field[..., :1, :])
-        north = jnp.concatenate([edge, field[..., :-1, :]], axis=-2)
-        south = jnp.concatenate([field[..., 1:, :], edge], axis=-2)
-        field = field + diffusion * (north + south - 2.0 * field)
-    for sweep_index in range(PASSES):
-        field = field + diffusion * (jnp.roll(field, 1, -1) + jnp.roll(field, -1, -1) - 2.0 * field)
-    return field
+    nlat = field.shape[-2]
+    row = lax.broadcasted_iota(jnp.int32, (nlat, 1), 0)
+    centre = jnp.where((row == 0) | (row == nlat - 1), 0.3125, 0.375)
+    wide = jnp.pad(field, [(0, 0)] * (field.ndim - 2) + [(2, 2), (0, 0)])
+    near = lax.slice_in_dim(wide, 1, nlat + 1, axis=-2) + lax.slice_in_dim(wide, 3, nlat + 3, axis=-2)
+    far = lax.slice_in_dim(wide, 0, nlat, axis=-2) + lax.slice_in_dim(wide, 4, nlat + 4, axis=-2)
+    field = centre * field + 0.25 * near + 0.0625 * far
+    near = jnp.roll(field, 1, -1) + jnp.roll(field, -1, -1)
+    far = jnp.roll(field, 2, -1) + jnp.roll(field, -2, -1)
+    return 0.375 * field + 0.25 * near + 0.0625 * far
 
 
 def exchange(values, rows_for):

time: 70.4 us -> 68.5 us (0.973)
  local copies, waits for them, and re-layouts: 10.6 us -> 9.61 us
  other arithmetic: 9.2 us -> 8.47 us
    add x12 -> x4, other arithmetic: 3.43 us -> 1.32 us  [smooth_rows(): field = centre * field + 0.25 * near + 0.0625 * far]
    slice x24 -> x16, local copies, waits for them, and re-layouts: 3.85 us -> 2.87 us  [the longest x8 1.44 us: smooth_rows(): near = jnp.roll(field, 1, -1) + jnp.roll(field, -1, -1)]
where the time goes in v11:
time: 68.5 us; the launch traced here: 68 us
  waiting for transfers between devices  22.2 us (32%)
  starting transfers between devices  13.3 us (19%)
  blocking collectives  13.1 us (19%)
  local copies, waits for them, and re-layouts  9.61 us (14%)
  other arithmetic  8.47 us (12%)
  between operations  1.05 us (2%)
    all_to_all x1, blocking collectives, exchange(): got = lax.all_to_all(parcel, ('grid', 'mem'), 0, 0, tiled=True)  13.1 us
    all_to_all x1, waiting for transfers between devices, local_by_level(): got = lax.all_to_all(packed, 'grid', 1, 2, tiled=True)[:, 0]  10.3 us
    all_to_all x1, waiting for transfers between devices, exchange(): got = lax.all_to_all(parcel, ('grid', 'mem'), 0, 0, tiled=True)  7.41 us
    all_to_all x1, starting transfers between devices, local_by_level(): got = lax.all_to_all(packed, 'grid', 1, 2, tiled=True)[:, 0]  7.28 us
    all_to_all x1, waiting for transfers between devices, mem_total(): lax.all_to_all(jnp.broadcast_to(part, (mem_size,) + part.shape), 'mem', 0...  4.55 us
    all_to_all x1, starting transfers between devices, mem_total(): lax.all_to_all(jnp.broadcast_to(part, (mem_size,) + part.shape), 'mem', 0...  3.33 us
    all_to_all x1, starting transfers between devices, exchange(): got = lax.all_to_all(parcel, ('grid', 'mem'), 0, 0, tiled=True)  2.7 us
    unnamed x8, local copies, waits for them, and re-layouts  1.71 us
  transfers between devices with their start and end apart: 3, of which 3 were waited for; matrix products, arithmetic and copies ran while one was open for 1% of the time, Pallas kernels for 0%

profile of v11, /device:TPU:0, one launch (start us, length us, event | category | flops | bytes accessed | tf_op | source)
XLA Modules:
  0.0 68.0 jit_solution(14306967534525596840)
XLA Ops:
  0.6 0.8 %fusion.80 = (bf16[2,512]{1,0:T(2,128)(2,1)S(1)}, f32[2,512]{1,0:T(2,128)S(1)}) fusion(s32[2,512]{1,0:T(2,128)} %param.6), kind=kLoop, calls=%fused_computation.171 | loop fusion | flops 2048 | bytes 10240 | tf_op jit(solution)/shard_map/convert_element_type | solution.py:117
  1.4 1.0 %constant_dynamic-update-slice_fusion.4 = bf16[24,4,2,512]{3,2,1,0:T(2,128)(2,1)S(1)} fusion(bf16[20,4,2,512]{3,2,1,0:T(2,128)(2,1)} %param.4), kind=kLoop, calls=%fused_computation.109 | loop fusion | bytes 327680
  2.7 0.9 %broadcast_in_dim.87 = bf16[24,4,2,2,512]{4,3,0,2,1:T(2,128)(2,1)} broadcast(bf16[24,4,2,512]{3,2,0,1:T(2,128)(2,1)S(1)} %copy.18), dimensions={0,1,3,4} | broadcast | bytes 589824 | tf_op jit(solution)/shard_map/broadcast_in_dim | solution.py:123
  3.6 7.3 %all-to-all-start = ((bf16[24,8,2,512]{3,2,0,1:T(2,128)(2,1)}), bf16[24,8,2,512]{3,2,0,1:T(2,128)(2,1)S(1)}, u32[]{:S(2)}, u32[]{:S(2)}) async-start(bf16[24,8,2,512]{3,2,0,1:T(2,128)(2,1)} %bitcast.3), calls=%async_computation | async-start | bytes 786432 | tf_op jit(solution)/shard_map/all_to_all | solution.py:124
  11.0 0.6 copy-done.2
  11.6 0.6 dynamic_slice.7
  12.3 10.3 %all-to-all-done = bf16[24,8,2,512]{3,2,0,1:T(2,128)(2,1)S(1)} async-done(((bf16[24,8,2,512]{3,2,0,1:T(2,128)(2,1)}), bf16[24,8,2,512]{3,2,0,1:T(2,128)(2,1)S(1)}, u32[]{:S(2)}, u32[]{:S(2)}) %all-to-all-start) | async-done | bytes 393248 | tf_op jit(solution)/shard_map/all_to_all | solution.py:124
  22.6 0.7 %fusion.45 = f32[1,8,2,512]{3,2,0,1:T(2,128)S(1)} fusion(f32[3,8,2,512]{3,2,0,1:T(2,128)S(1)} %slice_convert_fusion, f32[]{:T(128)} %bitcast.4, bf16[24,8,2,512]{3,2,0,1:T(2,128)(2,1)S(1)} %all-to-all-done), kind=kLoop, calls=%fused_computation.84 | loop fusion | flops 40960 | bytes 147460 | tf_op jit(solution)/shard_map/mul | solution.py:144
  23.7 0.5 copy.20
  24.2 0.5 reshape.377
  25.8 0.7 %select_reduce_fusion.2 = (f32[512]{0:T(512)S(1)}, f32[20,16,512]{2,1,0:T(8,128)S(1)}) fusion(pred[16,512]{1,0:T(8,128)(4,1)S(1)} %select_compare_fusion, f32[20,16,2]{2,1,0:T(8,128)S(1)} %get-tuple-element.38, f32[20,16,510]{2,1,0:T(8,128)S(1)} %get-tuple-element.40, f32[20,16,510]{2,1,0:T(8,128)S(1)} %get-tuple-element.39, ...), kind=kLoop, calls=%fused_computation.72 | loop fusion | flops 3440128 | bytes 3942464 | tf_op jit(solution)/shard_map/reduce_sum | solution.py:136
  27.6 0.7 %fusion.32 = f32[16,512]{1,0:T(8,128)S(1)} fusion(f32[20,16,512]{2,1,0:T(8,128)S(1)} %reshape.377, f32[20,16,511]{2,1,0:T(8,128)S(1)} %get-tuple-element.30, f32[20,16,1]{2,1,0:T(8,128)S(1)} %get-tuple-element.32, f32[20,16,1]{2,1,0:T(8,128)S(1)} %get-tuple-element.31, f32[20,16,511]{2,1,0:T(8,128)S(1)} %get-tuple-element.29, ...), kind=kLoop, calls=%fused_computation.51 | loop fusion | flops 3268608 | bytes 3964992 | tf_op jit(solution)/shard_map/reduce_sum | solution.py:145
  28.4 0.7 broadcast_in_dim.89
  29.0 3.3 %all-to-all-start.1 = ((f32[4,16,512]{2,1,0:T(8,128)}), f32[4,16,512]{2,1,0:T(8,128)S(1)}, u32[]{:S(2)}, u32[]{:S(2)}) async-start(f32[4,16,512]{2,1,0:T(8,128)} %broadcast_in_dim.89), calls=%async_computation.1 | async-start | bytes 262144 | tf_op jit(solution)/shard_map/all_to_all | solution.py:103
  32.4 4.5 %all-to-all-done.1 = f32[4,16,512]{2,1,0:T(8,128)S(1)} async-done(((f32[4,16,512]{2,1,0:T(8,128)}), f32[4,16,512]{2,1,0:T(8,128)S(1)}, u32[]{:S(2)}, u32[]{:S(2)}) %all-to-all-start.1) | async-done | bytes 131104 | tf_op jit(solution)/shard_map/all_to_all | solution.py:103
  37.0 0.8 %fusion.50 = (f32[512]{0:T(512)S(1)}, f32[1,8,2,512]{3,2,0,1:T(2,128)S(1)}) fusion(f32[1,8,2,512]{3,2,1,0:T(2,128)S(1)} %reduce_sum.172, pred[8,2]{1,0:T(8,128)(4,1)S(1)} %fusion.54, s32[]{:T(128)S(6)} %select_n.116, s32[8,2]{1,0:T(8,128)S(1)} %get-tuple-element.55, s32[8,2]{1,0:T(8,128)S(1)} %get-tuple-element.56, f32[]{:T(128)} %bitcast.4, ...), kind=kLoop, calls=%fused_computation.92 | loop fusion | flops 65024 | bytes 84120 | tf_op jit(solution)/shard_map/reduce_sum | solution.py:139
  38.9 0.7 %fusion.37 = f32[20,16,512]{2,1,0:T(8,128)S(1)} fusion(f32[20,16,512]{2,1,0:T(8,128)S(1)} %get-tuple-element.8, f32[20,16,511]{2,1,0:T(8,128)S(1)} %get-tuple-element.22, f32[20,16,1]{2,1,0:T(8,128)S(1)} %get-tuple-element.24, f32[20,16,1]{2,1,0:T(8,128)S(1)} %get-tuple-element.23, f32[20,16,511]{2,1,0:T(8,128)S(1)} %get-tuple-element.21, ...), kind=kLoop, calls=%fused_computation.58 | loop fusion | flops 3112960 | bytes 4587584 | tf_op jit(solution)/shard_map/add | solution.py:146
  40.7 0.7 %fusion.43 = f32[16,512]{1,0:T(8,128)S(1)} fusion(f32[20,16,512]{2,1,0:T(8,128)S(1)} %reshape.377, f32[20,16,511]{2,1,0:T(8,128)S(1)} %get-tuple-element.14, f32[20,16,1]{2,1,0:T(8,128)S(1)} %get-tuple-element.16, f32[20,16,1]{2,1,0:T(8,128)S(1)} %get-tuple-element.15, f32[20,16,511]{2,1,0:T(8,128)S(1)} %get-tuple-element.13, ...), kind=kLoop, calls=%fused_computation.66 | loop fusion | flops 3268608 | bytes 3964992 | tf_op jit(solution)/shard_map/reduce_sum | solution.py:147
  41.7 13.1 %all_to_all.24 = f32[32,3,512]{2,1,0:T(4,128)S(1)} all-to-all(f32[32,3,512]{2,1,0:T(4,128)S(1)} %pad_maximum_fusion), channel_id=1, replica_groups=mesh['grid'=8,'mem'=4] {'grid','mem'}, dimensions={0} | all-to-all | bytes 393216 | tf_op jit(solution)/shard_map/all_to_all | solution.py:95
  55.6 0.7 broadcast_in_dim.95
  56.2 2.7 %all-to-all-start.3 = ((f32[32,1,512]{2,1,0:T(1,128)}), f32[32,1,512]{2,1,0:T(1,128)S(1)}, u32[]{:S(2)}, u32[]{:S(2)}) async-start(f32[32,1,512]{2,1,0:T(1,128)} %broadcast_in_dim.95), calls=%async_computation.3 | async-start | bytes 131072 | tf_op jit(solution)/shard_map/all_to_all | solution.py:95
  59.0 7.4 %all-to-all-done.3 = f32[32,1,512]{2,1,0:T(1,128)S(1)} async-done(((f32[32,1,512]{2,1,0:T(1,128)}), f32[32,1,512]{2,1,0:T(1,128)S(1)}, u32[]{:S(2)}, u32[]{:S(2)}) %all-to-all-start.3) | async-done | bytes 65568 | tf_op jit(solution)/shard_map/all_to_all | solution.py:95
  66.7 0.8 %add_convert_fusion = bf16[20,4,2,512]{3,2,1,0:T(2,128)(2,1)} fusion(bf16[20,4,2,512]{3,2,1,0:T(2,128)(2,1)S(1)} %copy-done, f32[4,2,512]{2,1,0:T(2,128)S(1)} %multiply_add_fusion), kind=kLoop, calls=%fused_computation.74 | loop fusion | flops 245760 | bytes 344064 | tf_op jit(solution)/shard_map/convert_element_type | solution.py:188
  67.5 0.6 constant_dynamic-slice_fusion
  (73 shorter events, 6.3 us)
Async XLA Ops:
  1.4 1.1 %copy-start.1 = (f32[4,2,512]{2,1,0:T(2,128)S(1)}, f32[4,2,512]{2,1,0:T(2,128)}, u32[]{:S(2)}) copy-start(f32[4,2,512]{2,1,0:T(2,128)} %param.5) | copy-start | bytes 49156
  3.6 19.0 %all-to-all-start = ((bf16[24,8,2,512]{3,2,0,1:T(2,128)(2,1)}), bf16[24,8,2,512]{3,2,0,1:T(2,128)(2,1)S(1)}, u32[]{:S(2)}, u32[]{:S(2)}) async-start(bf16[24,8,2,512]{3,2,0,1:T(2,128)(2,1)} %bitcast.3), calls=%async_computation | async-start | bytes 786432 | tf_op jit(solution)/shard_map/all_to_all | solution.py:124
  10.9 0.7 copy-start.2
  29.0 7.9 %all-to-all-start.1 = ((f32[4,16,512]{2,1,0:T(8,128)}), f32[4,16,512]{2,1,0:T(8,128)S(1)}, u32[]{:S(2)}, u32[]{:S(2)}) async-start(f32[4,16,512]{2,1,0:T(8,128)} %broadcast_in_dim.89), calls=%async_computation.1 | async-start | bytes 262144 | tf_op jit(solution)/shard_map/all_to_all | solution.py:103
  56.2 10.4 %copy-start = (bf16[20,4,2,512]{3,2,1,0:T(2,128)(2,1)S(1)}, bf16[20,4,2,512]{3,2,1,0:T(2,128)(2,1)}, u32[]{:S(2)}) copy-start(bf16[20,4,2,512]{3,2,1,0:T(2,128)(2,1)} %param.4) | copy-start | bytes 491524
  56.2 10.1 %all-to-all-start.3 = ((f32[32,1,512]{2,1,0:T(1,128)}), f32[32,1,512]{2,1,0:T(1,128)S(1)}, u32[]{:S(2)}, u32[]{:S(2)}) async-start(f32[32,1,512]{2,1,0:T(1,128)} %broadcast_in_dim.95), calls=%async_computation.3 | async-start | bytes 131072 | tf_op jit(solution)/shard_map/all_to_all | solution.py:95

commit v12 on v11

--- a/solution.py
+++ b/solution.py
@@ -80,8 +80,10 @@
     near = lax.slice_in_dim(wide, 1, nlat + 1, axis=-2) + lax.slice_in_dim(wide, 3, nlat + 3, axis=-2)
     far = lax.slice_in_dim(wide, 0, nlat, axis=-2) + lax.slice_in_dim(wide, 4, nlat + 4, axis=-2)
     field = centre * field + 0.25 * near + 0.0625 * far
-    near = jnp.roll(field, 1, -1) + jnp.roll(field, -1, -1)
-    far = jnp.roll(field, 2, -1) + jnp.roll(field, -2, -1)
+    nlon = field.shape[-1]
+    wide = jnp.concatenate([field[..., nlon - 2 :], field, field[..., :2]], axis=-1)
+    near = wide[..., 1 : nlon + 1] + wide[..., 3 : nlon + 3]
+    far = wide[..., :nlon] + wide[..., 4 : nlon + 4]
     return 0.375 * field + 0.25 * near + 0.0625 * far
 
 

time: 68.5 us -> 66.6 us (0.972)
  local copies, waits for them, and re-layouts: 9.61 us -> 7.15 us
    slice x16 -> x4, local copies, waits for them, and re-layouts: 2.87 us -> 0.41 us  [smooth_rows(): field[..., nlon - 2:]]
where the time goes in v12:
time: 66.6 us; the launch traced here: 66.1 us
  waiting for transfers between devices  22.3 us (33%)
  starting transfers between devices  13.3 us (20%)
  blocking collectives  13.1 us (20%)
  other arithmetic  9.09 us (14%)
  local copies, waits for them, and re-layouts  7.15 us (11%)
  between operations  0.97 us (1%)
    all_to_all x1, blocking collectives, exchange(): got = lax.all_to_all(parcel, ('grid', 'mem'), 0, 0, tiled=True)  13.1 us
    all_to_all x1, waiting for transfers between devices, local_by_level(): got = lax.all_to_all(packed, 'grid', 1, 2, tiled=True)[:, 0]  10.3 us
    all_to_all x1, waiting for transfers between devices, exchange(): got = lax.all_to_all(parcel, ('grid', 'mem'), 0, 0, tiled=True)  7.41 us
    all_to_all x1, starting transfers between devices, local_by_level(): got = lax.all_to_all(packed, 'grid', 1, 2, tiled=True)[:, 0]  7.28 us
    all_to_all x1, waiting for transfers between devices, mem_total(): lax.all_to_all(jnp.broadcast_to(part, (mem_size,) + part.shape), 'mem', 0...  4.55 us
    all_to_all x1, starting transfers between devices, mem_total(): lax.all_to_all(jnp.broadcast_to(part, (mem_size,) + part.shape), 'mem', 0...  3.33 us
    all_to_all x1, starting transfers between devices, exchange(): got = lax.all_to_all(parcel, ('grid', 'mem'), 0, 0, tiled=True)  2.7 us
    unnamed x8, local copies, waits for them, and re-layouts  1.71 us
  transfers between devices with their start and end apart: 3, of which 3 were waited for; matrix products, arithmetic and copies ran while one was open for 1% of the time, Pallas kernels for 0%

profile of v12, /device:TPU:0, one launch (start us, length us, event | category | flops | bytes accessed | tf_op | source)
XLA Modules:
  0.0 66.1 jit_solution(12909382750448187597)
XLA Ops:
  0.6 0.8 %fusion.84 = (bf16[2,512]{1,0:T(2,128)(2,1)S(1)}, f32[2,512]{1,0:T(2,128)S(1)}) fusion(s32[2,512]{1,0:T(2,128)} %param.6), kind=kLoop, calls=%fused_computation.191 | loop fusion | flops 2048 | bytes 10240 | tf_op jit(solution)/shard_map/convert_element_type | solution.py:119
  1.4 1.0 %constant_dynamic-update-slice_fusion.4 = bf16[24,4,2,512]{3,2,1,0:T(2,128)(2,1)S(1)} fusion(bf16[20,4,2,512]{3,2,1,0:T(2,128)(2,1)} %param.4), kind=kLoop, calls=%fused_computation.141 | loop fusion | bytes 327680
  2.7 0.9 %broadcast_in_dim.87 = bf16[24,4,2,2,512]{4,3,0,2,1:T(2,128)(2,1)} broadcast(bf16[24,4,2,512]{3,2,0,1:T(2,128)(2,1)S(1)} %copy.18), dimensions={0,1,3,4} | broadcast | bytes 589824 | tf_op jit(solution)/shard_map/broadcast_in_dim | solution.py:125
  3.6 7.3 %all-to-all-start = ((bf16[24,8,2,512]{3,2,0,1:T(2,128)(2,1)}), bf16[24,8,2,512]{3,2,0,1:T(2,128)(2,1)S(1)}, u32[]{:S(2)}, u32[]{:S(2)}) async-start(bf16[24,8,2,512]{3,2,0,1:T(2,128)(2,1)} %bitcast.3), calls=%async_computation | async-start | bytes 786432 | tf_op jit(solution)/shard_map/all_to_all | solution.py:126
  11.0 0.6 copy-done.2
  11.6 0.6 dynamic_slice.7
  12.3 10.3 %all-to-all-done = bf16[24,8,2,512]{3,2,0,1:T(2,128)(2,1)S(1)} async-done(((bf16[24,8,2,512]{3,2,0,1:T(2,128)(2,1)}), bf16[24,8,2,512]{3,2,0,1:T(2,128)(2,1)S(1)}, u32[]{:S(2)}, u32[]{:S(2)}) %all-to-all-start) | async-done | bytes 393248 | tf_op jit(solution)/shard_map/all_to_all | solution.py:126
  22.9 0.5 copy.20
  23.5 0.5 reshape.377
  24.0 0.7 %fusion.61 = f32[1,8,2,512]{3,2,0,1:T(2,128)S(1)} fusion(f32[3,8,2,512]{3,2,0,1:T(2,128)S(1)} %slice_convert_fusion, f32[]{:T(128)} %bitcast.4, bf16[24,8,2,512]{3,2,0,1:T(2,128)(2,1)S(1)} %all-to-all-done), kind=kLoop, calls=%fused_computation.116 | loop fusion | flops 40960 | bytes 147460 | tf_op jit(solution)/shard_map/mul | solution.py:146
  25.2 0.9 %select_reduce_fusion.2 = (f32[512]{0:T(512)S(1)}, f32[20,16,512]{2,1,0:T(8,128)S(1)}) fusion(pred[16,512]{1,0:T(8,128)(4,1)S(1)} %select_compare_fusion, f32[20,16,2]{2,1,0:T(8,128)S(1)} %get-tuple-element.16, f32[20,16,512]{2,1,0:T(8,128)S(1)} %fusion.32, f32[20,16,2]{2,1,0:T(8,128)S(1)} %get-tuple-element.15), kind=kLoop, calls=%fused_computation.104 | loop fusion | flops 2293248 | bytes 1326080 | tf_op jit(solution)/shard_map/reduce_sum | solution.py:138
  26.5 0.9 %fusion.21 = f32[16,512]{1,0:T(8,128)S(1)} fusion(f32[20,16,512]{2,1,0:T(8,128)S(1)} %reshape.377, f32[20,16,512]{2,1,0:T(8,128)S(1)} %fusion.38, f32[20,16,2]{2,1,0:T(8,128)S(1)} %get-tuple-element.14, f32[20,16,2]{2,1,0:T(8,128)S(1)} %get-tuple-element.13), kind=kLoop, calls=%fused_computation.53 | loop fusion | flops 2121728 | bytes 1348608 | tf_op jit(solution)/shard_map/reduce_sum | solution.py:147
  27.4 0.7 %broadcast_in_dim.89 = f32[4,16,512]{2,1,0:T(8,128)} broadcast(f32[16,512]{1,0:T(8,128)S(1)} %fusion.21), dimensions={1,2} | broadcast | bytes 163840 | tf_op jit(solution)/shard_map/broadcast_in_dim | solution.py:105
  28.1 3.3 %all-to-all-start.1 = ((f32[4,16,512]{2,1,0:T(8,128)}), f32[4,16,512]{2,1,0:T(8,128)S(1)}, u32[]{:S(2)}, u32[]{:S(2)}) async-start(f32[4,16,512]{2,1,0:T(8,128)} %broadcast_in_dim.89), calls=%async_computation.1 | async-start | bytes 262144 | tf_op jit(solution)/shard_map/all_to_all | solution.py:105
  31.4 4.5 %all-to-all-done.1 = f32[4,16,512]{2,1,0:T(8,128)S(1)} async-done(((f32[4,16,512]{2,1,0:T(8,128)}), f32[4,16,512]{2,1,0:T(8,128)S(1)}, u32[]{:S(2)}, u32[]{:S(2)}) %all-to-all-start.1) | async-done | bytes 131104 | tf_op jit(solution)/shard_map/all_to_all | solution.py:105
  36.0 0.8 %fusion.66 = (f32[512]{0:T(512)S(1)}, f32[1,8,2,512]{3,2,0,1:T(2,128)S(1)}) fusion(f32[1,8,2,512]{3,2,1,0:T(2,128)S(1)} %reduce_sum.172, pred[8,2]{1,0:T(8,128)(4,1)S(1)} %fusion.70, s32[]{:T(128)S(6)} %select_n.116, s32[8,2]{1,0:T(8,128)S(1)} %get-tuple-element.31, s32[8,2]{1,0:T(8,128)S(1)} %get-tuple-element.32, f32[]{:T(128)} %bitcast.4, ...), kind=kLoop, calls=%fused_computation.124 | loop fusion | flops 65024 | bytes 84120 | tf_op jit(solution)/shard_map/reduce_sum | solution.py:141
  37.3 0.9 %fusion.13 = f32[20,16,512]{2,1,0:T(8,128)S(1)} fusion(f32[20,16,512]{2,1,0:T(8,128)S(1)} %get-tuple-element.8, f32[20,16,512]{2,1,0:T(8,128)S(1)} %fusion.44, f32[20,16,2]{2,1,0:T(8,128)S(1)} %get-tuple-element.12, f32[20,16,2]{2,1,0:T(8,128)S(1)} %get-tuple-element.11), kind=kLoop, calls=%fused_computation.45 | loop fusion | flops 1966080 | bytes 1971200 | tf_op jit(solution)/shard_map/add | solution.py:148
  38.7 0.9 %fusion.6 = f32[16,512]{1,0:T(8,128)S(1)} fusion(f32[20,16,512]{2,1,0:T(8,128)S(1)} %reshape.377, f32[20,16,512]{2,1,0:T(8,128)S(1)} %fusion.50, f32[20,16,2]{2,1,0:T(8,128)S(1)} %get-tuple-element.10, f32[20,16,2]{2,1,0:T(8,128)S(1)} %get-tuple-element.9), kind=kLoop, calls=%fused_computation.38 | loop fusion | flops 2121728 | bytes 1348608 | tf_op jit(solution)/shard_map/reduce_sum | solution.py:149
  39.8 13.1 %all_to_all.24 = f32[32,3,512]{2,1,0:T(4,128)S(1)} all-to-all(f32[32,3,512]{2,1,0:T(4,128)S(1)} %pad_maximum_fusion.8), channel_id=1, replica_groups=mesh['grid'=8,'mem'=4] {'grid','mem'}, dimensions={0} | all-to-all | bytes 393216 | tf_op jit(solution)/shard_map/all_to_all | solution.py:97
  53.7 0.7 %broadcast_in_dim.95 = f32[32,1,512]{2,1,0:T(1,128)} broadcast(f32[512]{0:T(512)S(1)} %pad_maximum_fusion.10), dimensions={2} | broadcast | bytes 67584 | tf_op jit(solution)/shard_map/broadcast_in_dim | solution.py:95
  54.3 2.7 %all-to-all-start.3 = ((f32[32,1,512]{2,1,0:T(1,128)}), f32[32,1,512]{2,1,0:T(1,128)S(1)}, u32[]{:S(2)}, u32[]{:S(2)}) async-start(f32[32,1,512]{2,1,0:T(1,128)} %broadcast_in_dim.95), calls=%async_computation.3 | async-start | bytes 131072 | tf_op jit(solution)/shard_map/all_to_all | solution.py:97
  57.0 7.4 %all-to-all-done.3 = f32[32,1,512]{2,1,0:T(1,128)S(1)} async-done(((f32[32,1,512]{2,1,0:T(1,128)}), f32[32,1,512]{2,1,0:T(1,128)S(1)}, u32[]{:S(2)}, u32[]{:S(2)}) %all-to-all-start.3) | async-done | bytes 65568 | tf_op jit(solution)/shard_map/all_to_all | solution.py:97
  64.7 0.8 %add_convert_fusion = bf16[20,4,2,512]{3,2,1,0:T(2,128)(2,1)} fusion(bf16[20,4,2,512]{3,2,1,0:T(2,128)(2,1)S(1)} %copy-done, f32[4,2,512]{2,1,0:T(2,128)S(1)} %multiply_add_fusion), kind=kLoop, calls=%fused_computation.106 | loop fusion | flops 245760 | bytes 344064 | tf_op jit(solution)/shard_map/convert_element_type | solution.py:190
  65.5 0.6 constant_dynamic-slice_fusion
  (61 shorter events, 3.9 us)
Async XLA Ops:
  1.4 1.1 %copy-start.1 = (f32[4,2,512]{2,1,0:T(2,128)S(1)}, f32[4,2,512]{2,1,0:T(2,128)}, u32[]{:S(2)}) copy-start(f32[4,2,512]{2,1,0:T(2,128)} %param.5) | copy-start | bytes 49156
  3.6 19.0 %all-to-all-start = ((bf16[24,8,2,512]{3,2,0,1:T(2,128)(2,1)}), bf16[24,8,2,512]{3,2,0,1:T(2,128)(2,1)S(1)}, u32[]{:S(2)}, u32[]{:S(2)}) async-start(bf16[24,8,2,512]{3,2,0,1:T(2,128)(2,1)} %bitcast.3), calls=%async_computation | async-start | bytes 786432 | tf_op jit(solution)/shard_map/all_to_all | solution.py:126
  10.9 0.7 copy-start.2
  28.1 7.9 %all-to-all-start.1 = ((f32[4,16,512]{2,1,0:T(8,128)}), f32[4,16,512]{2,1,0:T(8,128)S(1)}, u32[]{:S(2)}, u32[]{:S(2)}) async-start(f32[4,16,512]{2,1,0:T(8,128)} %broadcast_in_dim.89), calls=%async_computation.1 | async-start | bytes 262144 | tf_op jit(solution)/shard_map/all_to_all | solution.py:105
  54.3 10.4 %copy-start = (bf16[20,4,2,512]{3,2,1,0:T(2,128)(2,1)S(1)}, bf16[20,4,2,512]{3,2,1,0:T(2,128)(2,1)}, u32[]{:S(2)}) copy-start(bf16[20,4,2,512]{3,2,1,0:T(2,128)(2,1)} %param.4) | copy-start | bytes 491524
  54.3 10.1 %all-to-all-start.3 = ((f32[32,1,512]{2,1,0:T(1,128)}), f32[32,1,512]{2,1,0:T(1,128)S(1)}, u32[]{:S(2)}, u32[]{:S(2)}) async-start(f32[32,1,512]{2,1,0:T(1,128)} %broadcast_in_dim.95), calls=%async_computation.3 | async-start | bytes 131072 | tf_op jit(solution)/shard_map/all_to_all | solution.py:97

commit v13 on v12

--- a/solution.py
+++ b/solution.py
@@ -2,6 +2,7 @@
 import jax.numpy as jnp
 from jax import lax
 from jax.sharding import PartitionSpec as P
+
 
 PASSES = 2
 ITERS = 2
@@ -24,11 +25,11 @@
 
 
 def smooth(field):
-    for sweep_index in range(PASSES):
+    for _ in range(PASSES):
         extended = padded(field, (("grid", 2),), 1)
         centre = extended[:, :, 1:-1]
         field = centre + diffusion * (extended[:, :, :-2] + extended[:, :, 2:] - 2.0 * centre)
-    for sweep_index in range(PASSES):
+    for _ in range(PASSES):
         field = field + diffusion * (jnp.roll(field, 1, 3) + jnp.roll(field, -1, 3) - 2.0 * field)
     return field
 
@@ -106,7 +107,11 @@
     return jnp.sum(got, axis=0)
 
 
-def local_by_level(members, innovation, observed_count, obs_precision):
+def local_by_level(*args):
+    return level_body(*args)
+
+
+def level_body(members, innovation, observed_count, obs_precision):
     grid_size = lax.axis_size("grid")
     mem_size = lax.axis_size("mem")
     count, levels, rows, nlon = members.shape
@@ -152,7 +157,8 @@
         rows_for = jnp.where(grid_index % copies == 0, by_target(total1), by_target(image_part))
     else:
         rows_for = jnp.concatenate([by_target(total1), by_target(image_part)], axis=1)
-    sums1, got1 = exchange([squares(residual), weighted(total1)], rows_for)
+    norm_part = squares(lax.optimization_barrier(residual))
+    sums1, got1 = exchange([norm_part, weighted(total1)], rows_for)
     norm_now = sums1[0]
     curvature1 = sums1[1]
     step1 = norm_now / (norm_now + curvature1)

time: 66.6 us -> 66.6 us (level)
    add x2 -> x3, other arithmetic: 0.9 us -> 1.78 us  [the longest x1 0.88 us: level_body(): image = residual + smooth_rows(widened * (weight * total1)[None])]
    reduce_sum x2, other arithmetic: 1.09 us -> 0.31 us  [squares(): return jnp.sum(jnp.where(own[None], field * field, 0.0), axis=(0, 1))]
where the time goes in v13:
time: 66.6 us; the launch traced here: 66.1 us
  waiting for transfers between devices  22.1 us (33%)
  starting transfers between devices  13.3 us (20%)
  blocking collectives  13.1 us (20%)
  other arithmetic  9.18 us (14%)
  local copies, waits for them, and re-layouts  7.15 us (11%)
  between operations  0.98 us (1%)
    all_to_all x1, blocking collectives, exchange(): got = lax.all_to_all(parcel, ('grid', 'mem'), 0, 0, tiled=True)  13.1 us
    all_to_all x1, waiting for transfers between devices, level_body(): got = lax.all_to_all(packed, 'grid', 1, 2, tiled=True)[:, 0]  10.3 us
    all_to_all x1, waiting for transfers between devices, exchange(): got = lax.all_to_all(parcel, ('grid', 'mem'), 0, 0, tiled=True)  7.41 us
    all_to_all x1, starting transfers between devices, level_body(): got = lax.all_to_all(packed, 'grid', 1, 2, tiled=True)[:, 0]  7.28 us
    all_to_all x1, waiting for transfers between devices, mem_total(): lax.all_to_all(jnp.broadcast_to(part, (mem_size,) + part.shape), 'mem', 0...  4.43 us
    all_to_all x1, starting transfers between devices, mem_total(): lax.all_to_all(jnp.broadcast_to(part, (mem_size,) + part.shape), 'mem', 0...  3.33 us
    all_to_all x1, starting transfers between devices, exchange(): got = lax.all_to_all(parcel, ('grid', 'mem'), 0, 0, tiled=True)  2.7 us
    unnamed x8, local copies, waits for them, and re-layouts  1.71 us
  transfers between devices with their start and end apart: 3, of which 3 were waited for; matrix products, arithmetic and copies ran while one was open for 1% of the time, Pallas kernels for 0%

profile of v13, /device:TPU:0, one launch (start us, length us, event | category | flops | bytes accessed | tf_op | source)
XLA Modules:
  0.0 66.1 jit_solution(5266524942264287430)
XLA Ops:
  0.6 0.8 %fusion.83 = (bf16[2,512]{1,0:T(2,128)(2,1)S(1)}, f32[2,512]{1,0:T(2,128)S(1)}) fusion(s32[2,512]{1,0:T(2,128)} %param.6), kind=kLoop, calls=%fused_computation.191 | loop fusion | flops 2048 | bytes 10240 | tf_op jit(solution)/shard_map/convert_element_type | solution.py:124
  1.4 1.0 %constant_dynamic-update-slice_fusion.4 = bf16[24,4,2,512]{3,2,1,0:T(2,128)(2,1)S(1)} fusion(bf16[20,4,2,512]{3,2,1,0:T(2,128)(2,1)} %param.4), kind=kLoop, calls=%fused_computation.141 | loop fusion | bytes 327680
  2.7 0.9 %broadcast_in_dim.87 = bf16[24,4,2,2,512]{4,3,0,2,1:T(2,128)(2,1)} broadcast(bf16[24,4,2,512]{3,2,0,1:T(2,128)(2,1)S(1)} %copy.18), dimensions={0,1,3,4} | broadcast | bytes 589824 | tf_op jit(solution)/shard_map/broadcast_in_dim | solution.py:130
  3.6 7.3 %all-to-all-start = ((bf16[24,8,2,512]{3,2,0,1:T(2,128)(2,1)}), bf16[24,8,2,512]{3,2,0,1:T(2,128)(2,1)S(1)}, u32[]{:S(2)}, u32[]{:S(2)}) async-start(bf16[24,8,2,512]{3,2,0,1:T(2,128)(2,1)} %bitcast.3), calls=%async_computation | async-start | bytes 786432 | tf_op jit(solution)/shard_map/all_to_all | solution.py:131
  11.0 0.6 copy-done.2
  11.6 0.6 dynamic_slice.7
  12.3 10.3 %all-to-all-done = bf16[24,8,2,512]{3,2,0,1:T(2,128)(2,1)S(1)} async-done(((bf16[24,8,2,512]{3,2,0,1:T(2,128)(2,1)}), bf16[24,8,2,512]{3,2,0,1:T(2,128)(2,1)S(1)}, u32[]{:S(2)}, u32[]{:S(2)}) %all-to-all-start) | async-done | bytes 393248 | tf_op jit(solution)/shard_map/all_to_all | solution.py:131
  22.9 0.5 copy.20
  23.5 0.5 reshape.377
  24.0 0.7 %fusion.61 = f32[1,8,2,512]{3,2,0,1:T(2,128)S(1)} fusion(f32[3,8,2,512]{3,2,0,1:T(2,128)S(1)} %slice_convert_fusion, f32[]{:T(128)} %bitcast.4, bf16[24,8,2,512]{3,2,0,1:T(2,128)(2,1)S(1)} %all-to-all-done), kind=kLoop, calls=%fused_computation.116 | loop fusion | flops 40960 | bytes 147460 | tf_op jit(solution)/shard_map/mul | solution.py:151
  25.2 0.9 %fusion.27 = f32[20,16,512]{2,1,0:T(8,128)S(1)} fusion(f32[20,16,512]{2,1,0:T(8,128)S(1)} %fusion.32, f32[20,16,2]{2,1,0:T(8,128)S(1)} %get-tuple-element.14, f32[20,16,2]{2,1,0:T(8,128)S(1)} %get-tuple-element.13), kind=kLoop, calls=%fused_computation.59 | loop fusion | flops 1802240 | bytes 1315840 | tf_op jit(solution)/shard_map/add | solution.py:88
  26.5 0.9 %fusion.21 = f32[16,512]{1,0:T(8,128)S(1)} fusion(f32[20,16,512]{2,1,0:T(8,128)S(1)} %reshape.377, f32[20,16,512]{2,1,0:T(8,128)S(1)} %fusion.38, f32[20,16,2]{2,1,0:T(8,128)S(1)} %get-tuple-element.12, f32[20,16,2]{2,1,0:T(8,128)S(1)} %get-tuple-element.11), kind=kLoop, calls=%fused_computation.53 | loop fusion | flops 2121728 | bytes 1348608 | tf_op jit(solution)/shard_map/reduce_sum | solution.py:152
  27.4 0.7 %broadcast_in_dim.89 = f32[4,16,512]{2,1,0:T(8,128)} broadcast(f32[16,512]{1,0:T(8,128)S(1)} %fusion.21), dimensions={1,2} | broadcast | bytes 163840 | tf_op jit(solution)/shard_map/broadcast_in_dim | solution.py:106
  28.1 3.3 %all-to-all-start.1 = ((f32[4,16,512]{2,1,0:T(8,128)}), f32[4,16,512]{2,1,0:T(8,128)S(1)}, u32[]{:S(2)}, u32[]{:S(2)}) async-start(f32[4,16,512]{2,1,0:T(8,128)} %broadcast_in_dim.89), calls=%async_computation.1 | async-start | bytes 262144 | tf_op jit(solution)/shard_map/all_to_all | solution.py:106
  31.5 4.4 %all-to-all-done.1 = f32[4,16,512]{2,1,0:T(8,128)S(1)} async-done(((f32[4,16,512]{2,1,0:T(8,128)}), f32[4,16,512]{2,1,0:T(8,128)S(1)}, u32[]{:S(2)}, u32[]{:S(2)}) %all-to-all-start.1) | async-done | bytes 131104 | tf_op jit(solution)/shard_map/all_to_all | solution.py:106
  36.0 0.8 %fusion.66 = (f32[512]{0:T(512)S(1)}, f32[1,8,2,512]{3,2,0,1:T(2,128)S(1)}) fusion(f32[1,8,2,512]{3,2,1,0:T(2,128)S(1)} %reduce_sum.172, pred[8,2]{1,0:T(8,128)(4,1)S(1)} %fusion.70, s32[]{:T(128)S(6)} %select_n.116, s32[8,2]{1,0:T(8,128)S(1)} %get-tuple-element.27, s32[8,2]{1,0:T(8,128)S(1)} %get-tuple-element.28, f32[]{:T(128)} %bitcast.4, ...), kind=kLoop, calls=%fused_computation.124 | loop fusion | flops 65024 | bytes 84120 | tf_op jit(solution)/shard_map/reduce_sum | solution.py:146
  37.3 0.9 %fusion.13 = f32[20,16,512]{2,1,0:T(8,128)S(1)} fusion(f32[20,16,512]{2,1,0:T(8,128)S(1)} %fusion.27, f32[20,16,512]{2,1,0:T(8,128)S(1)} %fusion.44, f32[20,16,2]{2,1,0:T(8,128)S(1)} %get-tuple-element.10, f32[20,16,2]{2,1,0:T(8,128)S(1)} %get-tuple-element.9), kind=kLoop, calls=%fused_computation.45 | loop fusion | flops 1966080 | bytes 1971200 | tf_op jit(solution)/shard_map/add | solution.py:153
  38.6 0.9 %fusion.6 = f32[16,512]{1,0:T(8,128)S(1)} fusion(f32[20,16,512]{2,1,0:T(8,128)S(1)} %reshape.377, f32[20,16,512]{2,1,0:T(8,128)S(1)} %fusion.50, f32[20,16,2]{2,1,0:T(8,128)S(1)} %get-tuple-element.8, f32[20,16,2]{2,1,0:T(8,128)S(1)} %get-tuple-element.7), kind=kLoop, calls=%fused_computation.38 | loop fusion | flops 2121728 | bytes 1348608 | tf_op jit(solution)/shard_map/reduce_sum | solution.py:154
  39.8 13.1 %all_to_all.24 = f32[32,3,512]{2,1,0:T(4,128)S(1)} all-to-all(f32[32,3,512]{2,1,0:T(4,128)S(1)} %pad_maximum_fusion.8), channel_id=1, replica_groups=mesh['grid'=8,'mem'=4] {'grid','mem'}, dimensions={0} | all-to-all | bytes 393216 | tf_op jit(solution)/shard_map/all_to_all | solution.py:98
  53.6 0.7 %broadcast_in_dim.95 = f32[32,1,512]{2,1,0:T(1,128)} broadcast(f32[512]{0:T(512)S(1)} %pad_maximum_fusion.10), dimensions={2} | broadcast | bytes 67584 | tf_op jit(solution)/shard_map/broadcast_in_dim | solution.py:96
  54.3 2.7 %all-to-all-start.3 = ((f32[32,1,512]{2,1,0:T(1,128)}), f32[32,1,512]{2,1,0:T(1,128)S(1)}, u32[]{:S(2)}, u32[]{:S(2)}) async-start(f32[32,1,512]{2,1,0:T(1,128)} %broadcast_in_dim.95), calls=%async_computation.3 | async-start | bytes 131072 | tf_op jit(solution)/shard_map/all_to_all | solution.py:98
  57.0 7.4 %all-to-all-done.3 = f32[32,1,512]{2,1,0:T(1,128)S(1)} async-done(((f32[32,1,512]{2,1,0:T(1,128)}), f32[32,1,512]{2,1,0:T(1,128)S(1)}, u32[]{:S(2)}, u32[]{:S(2)}) %all-to-all-start.3) | async-done | bytes 65568 | tf_op jit(solution)/shard_map/all_to_all | solution.py:98
  64.7 0.8 %add_convert_fusion = bf16[20,4,2,512]{3,2,1,0:T(2,128)(2,1)} fusion(bf16[20,4,2,512]{3,2,1,0:T(2,128)(2,1)S(1)} %copy-done, f32[4,2,512]{2,1,0:T(2,128)S(1)} %multiply_add_fusion), kind=kLoop, calls=%fused_computation.106 | loop fusion | flops 245760 | bytes 344064 | tf_op jit(solution)/shard_map/convert_element_type | solution.py:196
  65.5 0.6 constant_dynamic-slice_fusion
  (62 shorter events, 4.0 us)
Async XLA Ops:
  1.4 1.1 %copy-start.1 = (f32[4,2,512]{2,1,0:T(2,128)S(1)}, f32[4,2,512]{2,1,0:T(2,128)}, u32[]{:S(2)}) copy-start(f32[4,2,512]{2,1,0:T(2,128)} %param.5) | copy-start | bytes 49156
  3.6 19.0 %all-to-all-start = ((bf16[24,8,2,512]{3,2,0,1:T(2,128)(2,1)}), bf16[24,8,2,512]{3,2,0,1:T(2,128)(2,1)S(1)}, u32[]{:S(2)}, u32[]{:S(2)}) async-start(bf16[24,8,2,512]{3,2,0,1:T(2,128)(2,1)} %bitcast.3), calls=%async_computation | async-start | bytes 786432 | tf_op jit(solution)/shard_map/all_to_all | solution.py:131
  10.9 0.7 copy-start.2
  28.1 7.9 %all-to-all-start.1 = ((f32[4,16,512]{2,1,0:T(8,128)}), f32[4,16,512]{2,1,0:T(8,128)S(1)}, u32[]{:S(2)}, u32[]{:S(2)}) async-start(f32[4,16,512]{2,1,0:T(8,128)} %broadcast_in_dim.89), calls=%async_computation.1 | async-start | bytes 262144 | tf_op jit(solution)/shard_map/all_to_all | solution.py:106
  54.3 10.4 %copy-start = (bf16[20,4,2,512]{3,2,1,0:T(2,128)(2,1)S(1)}, bf16[20,4,2,512]{3,2,1,0:T(2,128)(2,1)}, u32[]{:S(2)}) copy-start(bf16[20,4,2,512]{3,2,1,0:T(2,128)(2,1)} %param.4) | copy-start | bytes 491524
  54.3 10.1 %all-to-all-start.3 = ((f32[32,1,512]{2,1,0:T(1,128)}), f32[32,1,512]{2,1,0:T(1,128)S(1)}, u32[]{:S(2)}, u32[]{:S(2)}) async-start(f32[32,1,512]{2,1,0:T(1,128)} %broadcast_in_dim.95), calls=%async_computation.3 | async-start | bytes 131072 | tf_op jit(solution)/shard_map/all_to_all | solution.py:98

commit v14 on v12

--- a/solution.py
+++ b/solution.py
@@ -186,7 +186,11 @@
     whole = step1 * total1_rows + step2 * total2_rows
 
     share = levels // mem_size
-    mine_out = lax.dynamic_slice_in_dim(whole, mem_index * share, share, 0)
+    if share == 1:
+        pick = lax.broadcasted_iota(jnp.int32, (levels, 1, 1), 0) == mem_index
+        mine_out = jnp.sum(jnp.where(pick, whole, 0.0), axis=0, keepdims=True)
+    else:
+        mine_out = lax.dynamic_slice_in_dim(whole, mem_index * share, share, 0)
     recentred = (members.astype(jnp.float32) + whole[None]).astype(jnp.bfloat16)
     return (recentred, mine_out)
 

time: 66.6 us -> 66.6 us (level)
    reduce_sum x0 -> x1, other arithmetic: none -> 0.69 us  [local_by_level(): mine_out = jnp.sum(jnp.where(pick, whole, 0.0), axis=0, keepdims=True)]
where the time goes in v14:
time: 66.6 us; the launch traced here: 66.2 us
  waiting for transfers between devices  22.2 us (33%)
  starting transfers between devices  13.3 us (20%)
  blocking collectives  13.1 us (20%)
  other arithmetic  9.75 us (15%)
  local copies, waits for them, and re-layouts  6.56 us (10%)
  between operations  0.97 us (1%)
    all_to_all x1, blocking collectives, exchange(): got = lax.all_to_all(parcel, ('grid', 'mem'), 0, 0, tiled=True)  13.1 us
    all_to_all x1, waiting for transfers between devices, local_by_level(): got = lax.all_to_all(packed, 'grid', 1, 2, tiled=True)[:, 0]  10.3 us
    all_to_all x1, waiting for transfers between devices, exchange(): got = lax.all_to_all(parcel, ('grid', 'mem'), 0, 0, tiled=True)  7.4 us
    all_to_all x1, starting transfers between devices, local_by_level(): got = lax.all_to_all(packed, 'grid', 1, 2, tiled=True)[:, 0]  7.28 us
    all_to_all x1, waiting for transfers between devices, mem_total(): lax.all_to_all(jnp.broadcast_to(part, (mem_size,) + part.shape), 'mem', 0...  4.55 us
    all_to_all x1, starting transfers between devices, mem_total(): lax.all_to_all(jnp.broadcast_to(part, (mem_size,) + part.shape), 'mem', 0...  3.33 us
    all_to_all x1, starting transfers between devices, exchange(): got = lax.all_to_all(parcel, ('grid', 'mem'), 0, 0, tiled=True)  2.7 us
    unnamed x8, local copies, waits for them, and re-layouts  1.71 us
  transfers between devices with their start and end apart: 3, of which 3 were waited for; matrix products, arithmetic and copies ran while one was open for 1% of the time, Pallas kernels for 0%

profile of v14, /device:TPU:0, one launch (start us, length us, event | category | flops | bytes accessed | tf_op | source)
XLA Modules:
  0.0 66.2 jit_solution(10300284008369793385)
XLA Ops:
  0.6 0.8 %fusion.84 = (bf16[2,512]{1,0:T(2,128)(2,1)S(1)}, f32[2,512]{1,0:T(2,128)S(1)}) fusion(s32[2,512]{1,0:T(2,128)} %param.6), kind=kLoop, calls=%fused_computation.192 | loop fusion | flops 2048 | bytes 10240 | tf_op jit(solution)/shard_map/convert_element_type | solution.py:119
  1.4 1.0 %constant_dynamic-update-slice_fusion.4 = bf16[24,4,2,512]{3,2,1,0:T(2,128)(2,1)S(1)} fusion(bf16[20,4,2,512]{3,2,1,0:T(2,128)(2,1)} %param.4), kind=kLoop, calls=%fused_computation.142 | loop fusion | bytes 327680
  2.7 0.9 %broadcast_in_dim.102 = bf16[24,4,2,2,512]{4,3,0,2,1:T(2,128)(2,1)} broadcast(bf16[24,4,2,512]{3,2,0,1:T(2,128)(2,1)S(1)} %copy.18), dimensions={0,1,3,4} | broadcast | bytes 589824 | tf_op jit(solution)/shard_map/broadcast_in_dim | solution.py:125
  3.6 7.3 %all-to-all-start = ((bf16[24,8,2,512]{3,2,0,1:T(2,128)(2,1)}), bf16[24,8,2,512]{3,2,0,1:T(2,128)(2,1)S(1)}, u32[]{:S(2)}, u32[]{:S(2)}) async-start(bf16[24,8,2,512]{3,2,0,1:T(2,128)(2,1)} %bitcast.3), calls=%async_computation | async-start | bytes 786432 | tf_op jit(solution)/shard_map/all_to_all | solution.py:126
  11.0 0.6 copy-done.2
  11.6 0.6 dynamic_slice.4
  12.3 10.3 %all-to-all-done = bf16[24,8,2,512]{3,2,0,1:T(2,128)(2,1)S(1)} async-done(((bf16[24,8,2,512]{3,2,0,1:T(2,128)(2,1)}), bf16[24,8,2,512]{3,2,0,1:T(2,128)(2,1)S(1)}, u32[]{:S(2)}, u32[]{:S(2)}) %all-to-all-start) | async-done | bytes 393248 | tf_op jit(solution)/shard_map/all_to_all | solution.py:126
  22.9 0.5 copy.20
  23.5 0.5 reshape.382
  24.0 0.7 %fusion.61 = f32[1,8,2,512]{3,2,0,1:T(2,128)S(1)} fusion(f32[3,8,2,512]{3,2,0,1:T(2,128)S(1)} %slice_convert_fusion, f32[]{:T(128)} %bitcast.4, bf16[24,8,2,512]{3,2,0,1:T(2,128)(2,1)S(1)} %all-to-all-done), kind=kLoop, calls=%fused_computation.116 | loop fusion | flops 40960 | bytes 147460 | tf_op jit(solution)/shard_map/mul | solution.py:146
  25.2 0.9 %select_reduce_fusion.2 = (f32[512]{0:T(512)S(1)}, f32[20,16,512]{2,1,0:T(8,128)S(1)}) fusion(pred[16,512]{1,0:T(8,128)(4,1)S(1)} %select_compare_fusion, f32[20,16,2]{2,1,0:T(8,128)S(1)} %get-tuple-element.18, f32[20,16,512]{2,1,0:T(8,128)S(1)} %fusion.32, f32[20,16,2]{2,1,0:T(8,128)S(1)} %get-tuple-element.17), kind=kLoop, calls=%fused_computation.104 | loop fusion | flops 2293248 | bytes 1326080 | tf_op jit(solution)/shard_map/reduce_sum | solution.py:138
  26.5 0.9 %fusion.21 = f32[16,512]{1,0:T(8,128)S(1)} fusion(f32[20,16,512]{2,1,0:T(8,128)S(1)} %reshape.382, f32[20,16,512]{2,1,0:T(8,128)S(1)} %fusion.38, f32[20,16,2]{2,1,0:T(8,128)S(1)} %get-tuple-element.16, f32[20,16,2]{2,1,0:T(8,128)S(1)} %get-tuple-element.15), kind=kLoop, calls=%fused_computation.53 | loop fusion | flops 2121728 | bytes 1348608 | tf_op jit(solution)/shard_map/reduce_sum | solution.py:147
  27.4 0.7 %broadcast_in_dim.104 = f32[4,16,512]{2,1,0:T(8,128)} broadcast(f32[16,512]{1,0:T(8,128)S(1)} %fusion.21), dimensions={1,2} | broadcast | bytes 163840 | tf_op jit(solution)/shard_map/broadcast_in_dim | solution.py:105
  28.1 3.3 %all-to-all-start.1 = ((f32[4,16,512]{2,1,0:T(8,128)}), f32[4,16,512]{2,1,0:T(8,128)S(1)}, u32[]{:S(2)}, u32[]{:S(2)}) async-start(f32[4,16,512]{2,1,0:T(8,128)} %broadcast_in_dim.104), calls=%async_computation.1 | async-start | bytes 262144 | tf_op jit(solution)/shard_map/all_to_all | solution.py:105
  31.4 4.5 %all-to-all-done.1 = f32[4,16,512]{2,1,0:T(8,128)S(1)} async-done(((f32[4,16,512]{2,1,0:T(8,128)}), f32[4,16,512]{2,1,0:T(8,128)S(1)}, u32[]{:S(2)}, u32[]{:S(2)}) %all-to-all-start.1) | async-done | bytes 131104 | tf_op jit(solution)/shard_map/all_to_all | solution.py:105
  36.0 0.8 %fusion.66 = (f32[512]{0:T(512)S(1)}, f32[1,8,2,512]{3,2,0,1:T(2,128)S(1)}) fusion(f32[1,8,2,512]{3,2,1,0:T(2,128)S(1)} %reduce_sum.181, pred[8,2]{1,0:T(8,128)(4,1)S(1)} %fusion.70, s32[]{:T(128)S(6)} %select_n.117, s32[8,2]{1,0:T(8,128)S(1)} %get-tuple-element.33, s32[8,2]{1,0:T(8,128)S(1)} %get-tuple-element.34, f32[]{:T(128)} %bitcast.4, ...), kind=kLoop, calls=%fused_computation.124 | loop fusion | flops 65024 | bytes 84120 | tf_op jit(solution)/shard_map/reduce_sum | solution.py:141
  37.3 0.9 %fusion.13 = f32[20,16,512]{2,1,0:T(8,128)S(1)} fusion(f32[20,16,512]{2,1,0:T(8,128)S(1)} %get-tuple-element.10, f32[20,16,512]{2,1,0:T(8,128)S(1)} %fusion.44, f32[20,16,2]{2,1,0:T(8,128)S(1)} %get-tuple-element.14, f32[20,16,2]{2,1,0:T(8,128)S(1)} %get-tuple-element.13), kind=kLoop, calls=%fused_computation.45 | loop fusion | flops 1966080 | bytes 1971200 | tf_op jit(solution)/shard_map/add | solution.py:148
  38.7 0.9 %fusion.6 = f32[16,512]{1,0:T(8,128)S(1)} fusion(f32[20,16,512]{2,1,0:T(8,128)S(1)} %reshape.382, f32[20,16,512]{2,1,0:T(8,128)S(1)} %fusion.50, f32[20,16,2]{2,1,0:T(8,128)S(1)} %get-tuple-element.12, f32[20,16,2]{2,1,0:T(8,128)S(1)} %get-tuple-element.11), kind=kLoop, calls=%fused_computation.38 | loop fusion | flops 2121728 | bytes 1348608 | tf_op jit(solution)/shard_map/reduce_sum | solution.py:149
  39.8 13.1 %all_to_all.24 = f32[32,3,512]{2,1,0:T(4,128)S(1)} all-to-all(f32[32,3,512]{2,1,0:T(4,128)S(1)} %pad_maximum_fusion.8), channel_id=1, replica_groups=mesh['grid'=8,'mem'=4] {'grid','mem'}, dimensions={0} | all-to-all | bytes 393216 | tf_op jit(solution)/shard_map/all_to_all | solution.py:97
  53.7 0.7 %broadcast_in_dim.110 = f32[32,1,512]{2,1,0:T(1,128)} broadcast(f32[512]{0:T(512)S(1)} %pad_maximum_fusion.10), dimensions={2} | broadcast | bytes 67584 | tf_op jit(solution)/shard_map/broadcast_in_dim | solution.py:95
  54.3 2.7 %all-to-all-start.3 = ((f32[32,1,512]{2,1,0:T(1,128)}), f32[32,1,512]{2,1,0:T(1,128)S(1)}, u32[]{:S(2)}, u32[]{:S(2)}) async-start(f32[32,1,512]{2,1,0:T(1,128)} %broadcast_in_dim.110), calls=%async_computation.3 | async-start | bytes 131072 | tf_op jit(solution)/shard_map/all_to_all | solution.py:97
  57.1 7.4 %all-to-all-done.3 = f32[32,1,512]{2,1,0:T(1,128)S(1)} async-done(((f32[32,1,512]{2,1,0:T(1,128)}), f32[32,1,512]{2,1,0:T(1,128)S(1)}, u32[]{:S(2)}, u32[]{:S(2)}) %all-to-all-start.3) | async-done | bytes 65568 | tf_op jit(solution)/shard_map/all_to_all | solution.py:97
  64.7 0.7 %select_reduce_fusion.3 = (f32[2,512]{1,0:T(2,128)}, f32[4,2,512]{2,1,0:T(2,128)S(1)}) fusion(pred[4]{0:T(512)(128)(4,1)S(1)} %iota_compare_fusion, f32[4,2,512]{2,1,0:T(2,128)S(1)} %get-tuple-element.8, f32[512]{0:T(512)S(1)} %get-tuple-element.30, f32[512]{0:T(512)S(1)} %get-tuple-element.29, f32[4,2,4,2,512]{4,3,2,1,0:T(2,128)S(1)} %bitcast.109, ...), kind=kLoop, calls=%fused_computation.131 | loop fusion | flops 27648 | bytes 59396 | tf_op jit(solution)/shard_map/reduce_sum | solution.py:191
  65.4 0.8 %add_convert_fusion = bf16[20,4,2,512]{3,2,1,0:T(2,128)(2,1)} fusion(bf16[20,4,2,512]{3,2,1,0:T(2,128)(2,1)S(1)} %copy-done, f32[4,2,512]{2,1,0:T(2,128)S(1)} %get-tuple-element.7), kind=kLoop, calls=%fused_computation.106 | loop fusion | flops 245760 | bytes 344064 | tf_op jit(solution)/shard_map/convert_element_type | solution.py:194
  (61 shorter events, 3.8 us)
Async XLA Ops:
  1.4 1.1 %copy-start.1 = (f32[4,2,512]{2,1,0:T(2,128)S(1)}, f32[4,2,512]{2,1,0:T(2,128)}, u32[]{:S(2)}) copy-start(f32[4,2,512]{2,1,0:T(2,128)} %param.5) | copy-start | bytes 49156
  3.6 19.0 %all-to-all-start = ((bf16[24,8,2,512]{3,2,0,1:T(2,128)(2,1)}), bf16[24,8,2,512]{3,2,0,1:T(2,128)(2,1)S(1)}, u32[]{:S(2)}, u32[]{:S(2)}) async-start(bf16[24,8,2,512]{3,2,0,1:T(2,128)(2,1)} %bitcast.3), calls=%async_computation | async-start | bytes 786432 | tf_op jit(solution)/shard_map/all_to_all | solution.py:126
  10.9 0.7 copy-start.2
  28.1 7.9 %all-to-all-start.1 = ((f32[4,16,512]{2,1,0:T(8,128)}), f32[4,16,512]{2,1,0:T(8,128)S(1)}, u32[]{:S(2)}, u32[]{:S(2)}) async-start(f32[4,16,512]{2,1,0:T(8,128)} %broadcast_in_dim.104), calls=%async_computation.1 | async-start | bytes 262144 | tf_op jit(solution)/shard_map/all_to_all | solution.py:105
  54.3 11.1 %copy-start = (bf16[20,4,2,512]{3,2,1,0:T(2,128)(2,1)S(1)}, bf16[20,4,2,512]{3,2,1,0:T(2,128)(2,1)}, u32[]{:S(2)}) copy-start(bf16[20,4,2,512]{3,2,1,0:T(2,128)(2,1)} %param.4) | copy-start | bytes 491524
  54.3 10.1 %all-to-all-start.3 = ((f32[32,1,512]{2,1,0:T(1,128)}), f32[32,1,512]{2,1,0:T(1,128)S(1)}, u32[]{:S(2)}, u32[]{:S(2)}) async-start(f32[32,1,512]{2,1,0:T(1,128)} %broadcast_in_dim.110), calls=%async_computation.3 | async-start | bytes 131072 | tf_op jit(solution)/shard_map/all_to_all | solution.py:97

commit v15 on v12

--- a/solution.py
+++ b/solution.py
@@ -87,17 +87,18 @@
     return 0.375 * field + 0.25 * near + 0.0625 * far
 
 
-def exchange(values, rows_for):
+def exchange(values, rows_for, width=128):
     devices = lax.axis_size("grid") * lax.axis_size("mem")
     nlon = rows_for.shape[-1]
-    lanes = [jnp.sum(v.reshape(-1, 128), axis=0) for v in values]
-    lanes.append(jnp.zeros((nlon - 128 * len(values),), jnp.float32))
-    head = jnp.broadcast_to(jnp.concatenate(lanes), (devices, 1, nlon))
-    parcel = jnp.concatenate([head, rows_for], axis=1)
+    rows = rows_for.shape[1]
+    lanes = [jnp.sum(v.reshape(-1, width), axis=0) for v in values]
+    head = jnp.broadcast_to(jnp.concatenate(lanes), (devices, width * len(values)))
+    parcel = jnp.concatenate([head, rows_for.reshape(devices, rows * nlon)], axis=1)
     got = lax.all_to_all(parcel, ("grid", "mem"), 0, 0, tiled=True)
-    lanes = jnp.sum(got[:, 0].reshape(devices, nlon // 128, 128), axis=0)
-    sums = jnp.dot(lanes, jnp.ones((128, 128), jnp.float32), precision=lax.Precision.HIGHEST)
-    return [jnp.tile(sums[i : i + 1], (1, nlon // 128)) for i in range(len(values))], got[:, 1:]
+    parts = jnp.sum(got[:, : width * len(values)].reshape(devices, len(values), width), axis=0)
+    sums = jnp.dot(parts, jnp.ones((width, 128), jnp.float32), precision=lax.Precision.HIGHEST)
+    received = got[:, width * len(values) :].reshape(devices, rows, nlon)
+    return [jnp.tile(sums[i : i + 1], (1, nlon // 128)) for i in range(len(values))], received
 
 
 def mem_total(part):
@@ -176,6 +177,7 @@
             jnp.where(first, jnp.sum(weight_rows * moved_rows * total1_rows, axis=(0, 1)), 0.0),
         ],
         jnp.zeros((grid_size * mem_size, 0, nlon), jnp.float32),
+        width=32,
     )
     norm_next = sums[0]
     beta = norm_next / norm_now

time: 66.6 us -> 64.6 us (0.970)
  blocking collectives: 13.1 us -> 11.2 us
    all_to_all x1, blocking collectives: 13.1 us -> 11.2 us  [exchange(): got = lax.all_to_all(parcel, ('grid', 'mem'), 0, 0, tiled=True)]
    unnamed x8 -> x10, local copies, waits for them, and re-layouts: 1.71 us -> 1.75 us
where the time goes in v15:
time: 64.6 us; the launch traced here: 64.2 us
  waiting for transfers between devices  21.9 us (34%)
  starting transfers between devices  13.1 us (20%)
  blocking collectives  11.2 us (17%)
  other arithmetic  8.98 us (14%)
  local copies, waits for them, and re-layouts  7.67 us (12%)
  between operations  1 us (2%)
    all_to_all x1, blocking collectives, exchange(): got = lax.all_to_all(parcel, ('grid', 'mem'), 0, 0, tiled=True)  11.2 us
    all_to_all x1, waiting for transfers between devices, local_by_level(): got = lax.all_to_all(packed, 'grid', 1, 2, tiled=True)[:, 0]  10.3 us
    all_to_all x1, starting transfers between devices, local_by_level(): got = lax.all_to_all(packed, 'grid', 1, 2, tiled=True)[:, 0]  7.28 us
    all_to_all x1, waiting for transfers between devices, exchange(): got = lax.all_to_all(parcel, ('grid', 'mem'), 0, 0, tiled=True)  7.1 us
    all_to_all x1, waiting for transfers between devices, mem_total(): lax.all_to_all(jnp.broadcast_to(part, (mem_size,) + part.shape), 'mem', 0...  4.55 us
    all_to_all x1, starting transfers between devices, mem_total(): lax.all_to_all(jnp.broadcast_to(part, (mem_size,) + part.shape), 'mem', 0...  3.33 us
    all_to_all x1, starting transfers between devices, exchange(): got = lax.all_to_all(parcel, ('grid', 'mem'), 0, 0, tiled=True)  2.54 us
    unnamed x10, local copies, waits for them, and re-layouts  1.75 us
  transfers between devices with their start and end apart: 3, of which 3 were waited for; matrix products, arithmetic and copies ran while one was open for 1% of the time, Pallas kernels for 0%

profile of v15, /device:TPU:0, one launch (start us, length us, event | category | flops | bytes accessed | tf_op | source)
XLA Modules:
  0.0 64.2 jit_solution(2874894953227911471)
XLA Ops:
  0.6 0.8 %fusion.83 = (bf16[2,512]{1,0:T(2,128)(2,1)S(1)}, f32[2,512]{1,0:T(2,128)S(1)}) fusion(s32[2,512]{1,0:T(2,128)} %param.6), kind=kLoop, calls=%fused_computation.189 | loop fusion | flops 2048 | bytes 10240 | tf_op jit(solution)/shard_map/convert_element_type | solution.py:120
  1.4 1.0 %constant_dynamic-update-slice_fusion.4 = bf16[24,4,2,512]{3,2,1,0:T(2,128)(2,1)S(1)} fusion(bf16[20,4,2,512]{3,2,1,0:T(2,128)(2,1)} %param.4), kind=kLoop, calls=%fused_computation.140 | loop fusion | bytes 327680
  2.7 0.9 %broadcast_in_dim.90 = bf16[24,4,2,2,512]{4,3,0,2,1:T(2,128)(2,1)} broadcast(bf16[24,4,2,512]{3,2,0,1:T(2,128)(2,1)S(1)} %copy.18), dimensions={0,1,3,4} | broadcast | bytes 589824 | tf_op jit(solution)/shard_map/broadcast_in_dim | solution.py:126
  3.6 7.3 %all-to-all-start = ((bf16[24,8,2,512]{3,2,0,1:T(2,128)(2,1)}), bf16[24,8,2,512]{3,2,0,1:T(2,128)(2,1)S(1)}, u32[]{:S(2)}, u32[]{:S(2)}) async-start(bf16[24,8,2,512]{3,2,0,1:T(2,128)(2,1)} %bitcast.3), calls=%async_computation | async-start | bytes 786432 | tf_op jit(solution)/shard_map/all_to_all | solution.py:127
  11.0 0.6 %copy-done.2 = f32[4]{0:T(128)S(1)} copy-done((f32[4]{0:T(128)S(1)}, f32[4]{0:T(128)}, u32[]{:S(2)}) %copy-start.2) | copy-done | bytes 40
  11.6 0.6 dynamic_slice.7
  12.3 10.3 %all-to-all-done = bf16[24,8,2,512]{3,2,0,1:T(2,128)(2,1)S(1)} async-done(((bf16[24,8,2,512]{3,2,0,1:T(2,128)(2,1)}), bf16[24,8,2,512]{3,2,0,1:T(2,128)(2,1)S(1)}, u32[]{:S(2)}, u32[]{:S(2)}) %all-to-all-start) | async-done | bytes 393248 | tf_op jit(solution)/shard_map/all_to_all | solution.py:127
  22.9 0.5 copy.20
  23.5 0.5 reshape.384
  24.0 0.7 %fusion.61 = f32[1,8,2,512]{3,2,0,1:T(2,128)S(1)} fusion(f32[3,8,2,512]{3,2,0,1:T(2,128)S(1)} %slice_convert_fusion, f32[]{:T(128)} %bitcast.4, bf16[24,8,2,512]{3,2,0,1:T(2,128)(2,1)S(1)} %all-to-all-done), kind=kLoop, calls=%fused_computation.117 | loop fusion | flops 40960 | bytes 147460 | tf_op jit(solution)/shard_map/mul | solution.py:147
  25.2 0.9 %select_reduce_fusion.2 = (f32[512]{0:T(512)S(1)}, f32[20,16,512]{2,1,0:T(8,128)S(1)}) fusion(pred[16,512]{1,0:T(8,128)(4,1)S(1)} %select_compare_fusion, f32[20,16,2]{2,1,0:T(8,128)S(1)} %get-tuple-element.16, f32[20,16,512]{2,1,0:T(8,128)S(1)} %fusion.32, f32[20,16,2]{2,1,0:T(8,128)S(1)} %get-tuple-element.15), kind=kLoop, calls=%fused_computation.104 | loop fusion | flops 2293248 | bytes 1326080 | tf_op jit(solution)/shard_map/reduce_sum | solution.py:139
  26.5 0.9 %fusion.21 = f32[16,512]{1,0:T(8,128)S(1)} fusion(f32[20,16,512]{2,1,0:T(8,128)S(1)} %reshape.384, f32[20,16,512]{2,1,0:T(8,128)S(1)} %fusion.38, f32[20,16,2]{2,1,0:T(8,128)S(1)} %get-tuple-element.14, f32[20,16,2]{2,1,0:T(8,128)S(1)} %get-tuple-element.13), kind=kLoop, calls=%fused_computation.53 | loop fusion | flops 2121728 | bytes 1348608 | tf_op jit(solution)/shard_map/reduce_sum | solution.py:148
  27.4 0.7 %broadcast_in_dim.92 = f32[4,16,512]{2,1,0:T(8,128)} broadcast(f32[16,512]{1,0:T(8,128)S(1)} %fusion.21), dimensions={1,2} | broadcast | bytes 163840 | tf_op jit(solution)/shard_map/broadcast_in_dim | solution.py:106
  28.1 3.3 %all-to-all-start.1 = ((f32[4,16,512]{2,1,0:T(8,128)}), f32[4,16,512]{2,1,0:T(8,128)S(1)}, u32[]{:S(2)}, u32[]{:S(2)}) async-start(f32[4,16,512]{2,1,0:T(8,128)} %broadcast_in_dim.92), calls=%async_computation.1 | async-start | bytes 262144 | tf_op jit(solution)/shard_map/all_to_all | solution.py:106
  31.4 4.5 %all-to-all-done.1 = f32[4,16,512]{2,1,0:T(8,128)S(1)} async-done(((f32[4,16,512]{2,1,0:T(8,128)}), f32[4,16,512]{2,1,0:T(8,128)S(1)}, u32[]{:S(2)}, u32[]{:S(2)}) %all-to-all-start.1) | async-done | bytes 131104 | tf_op jit(solution)/shard_map/all_to_all | solution.py:106
  36.0 0.8 %fusion.64 = (f32[512]{0:T(512)S(1)}, f32[1,8,2,512]{3,2,0,1:T(2,128)S(1)}) fusion(f32[1,8,2,512]{3,2,1,0:T(2,128)S(1)} %reduce_sum.172, pred[8,2]{1,0:T(8,128)(4,1)S(1)} %fusion.70, s32[]{:T(128)S(6)} %select_n.117, s32[8,2]{1,0:T(8,128)S(1)} %get-tuple-element.31, s32[8,2]{1,0:T(8,128)S(1)} %get-tuple-element.32, f32[]{:T(128)} %bitcast.4, ...), kind=kLoop, calls=%fused_computation.123 | loop fusion | flops 65024 | bytes 84120 | tf_op jit(solution)/shard_map/reduce_sum | solution.py:142
  37.3 0.9 %fusion.13 = f32[20,16,512]{2,1,0:T(8,128)S(1)} fusion(f32[20,16,512]{2,1,0:T(8,128)S(1)} %get-tuple-element.8, f32[20,16,512]{2,1,0:T(8,128)S(1)} %fusion.44, f32[20,16,2]{2,1,0:T(8,128)S(1)} %get-tuple-element.12, f32[20,16,2]{2,1,0:T(8,128)S(1)} %get-tuple-element.11), kind=kLoop, calls=%fused_computation.45 | loop fusion | flops 1966080 | bytes 1971200 | tf_op jit(solution)/shard_map/add | solution.py:149
  38.7 0.9 %fusion.6 = f32[16,512]{1,0:T(8,128)S(1)} fusion(f32[20,16,512]{2,1,0:T(8,128)S(1)} %reshape.384, f32[20,16,512]{2,1,0:T(8,128)S(1)} %fusion.50, f32[20,16,2]{2,1,0:T(8,128)S(1)} %get-tuple-element.10, f32[20,16,2]{2,1,0:T(8,128)S(1)} %get-tuple-element.9), kind=kLoop, calls=%fused_computation.38 | loop fusion | flops 2121728 | bytes 1348608 | tf_op jit(solution)/shard_map/reduce_sum | solution.py:150
  39.8 11.2 %all_to_all.32 = f32[32,1,1280]{2,1,0:T(1,128)S(1)} all-to-all(f32[32,1,1280]{2,1,0:T(1,128)S(1)} %all_to_all.24), channel_id=1, replica_groups=mesh['grid'=8,'mem'=4] {'grid','mem'}, dimensions={0} | all-to-all | bytes 327680 | tf_op jit(solution)/shard_map/all_to_all | solution.py:97
  52.2 0.6 broadcast_in_dim.98
  52.8 2.5 %all-to-all-start.3 = ((f32[32,1,128]{2,1,0:T(1,128)}), f32[32,1,128]{2,1,0:T(1,128)S(1)}, u32[]{:S(2)}, u32[]{:S(2)}) async-start(f32[32,1,128]{2,1,0:T(1,128)} %broadcast_in_dim.98), calls=%async_computation.3 | async-start | bytes 32768 | tf_op jit(solution)/shard_map/all_to_all | solution.py:97
  55.3 7.1 %all-to-all-done.3 = f32[32,1,128]{2,1,0:T(1,128)S(1)} async-done(((f32[32,1,128]{2,1,0:T(1,128)}), f32[32,1,128]{2,1,0:T(1,128)S(1)}, u32[]{:S(2)}, u32[]{:S(2)}) %all-to-all-start.3) | async-done | bytes 16416 | tf_op jit(solution)/shard_map/all_to_all | solution.py:97
  62.8 0.8 %add_convert_fusion = bf16[20,4,2,512]{3,2,1,0:T(2,128)(2,1)} fusion(bf16[20,4,2,512]{3,2,1,0:T(2,128)(2,1)S(1)} %copy-done, f32[4,2,512]{2,1,0:T(2,128)S(1)} %multiply_add_fusion), kind=kLoop, calls=%fused_computation.106 | loop fusion | flops 245760 | bytes 344064 | tf_op jit(solution)/shard_map/convert_element_type | solution.py:192
  63.6 0.6 constant_dynamic-slice_fusion
  (70 shorter events, 4.3 us)
Async XLA Ops:
  1.4 1.1 %copy-start.1 = (f32[4,2,512]{2,1,0:T(2,128)S(1)}, f32[4,2,512]{2,1,0:T(2,128)}, u32[]{:S(2)}) copy-start(f32[4,2,512]{2,1,0:T(2,128)} %param.5) | copy-start | bytes 49156
  3.6 19.0 %all-to-all-start = ((bf16[24,8,2,512]{3,2,0,1:T(2,128)(2,1)}), bf16[24,8,2,512]{3,2,0,1:T(2,128)(2,1)S(1)}, u32[]{:S(2)}, u32[]{:S(2)}) async-start(bf16[24,8,2,512]{3,2,0,1:T(2,128)(2,1)} %bitcast.3), calls=%async_computation | async-start | bytes 786432 | tf_op jit(solution)/shard_map/all_to_all | solution.py:127
  10.9 0.7 %copy-start.2 = (f32[4]{0:T(128)S(1)}, f32[4]{0:T(128)}, u32[]{:S(2)}) copy-start(f32[4]{0:T(128)} %param.7) | copy-start | bytes 52
  28.1 7.9 %all-to-all-start.1 = ((f32[4,16,512]{2,1,0:T(8,128)}), f32[4,16,512]{2,1,0:T(8,128)S(1)}, u32[]{:S(2)}, u32[]{:S(2)}) async-start(f32[4,16,512]{2,1,0:T(8,128)} %broadcast_in_dim.92), calls=%async_computation.1 | async-start | bytes 262144 | tf_op jit(solution)/shard_map/all_to_all | solution.py:106
  51.6 11.2 %copy-start = (bf16[20,4,2,512]{3,2,1,0:T(2,128)(2,1)S(1)}, bf16[20,4,2,512]{3,2,1,0:T(2,128)(2,1)}, u32[]{:S(2)}) copy-start(bf16[20,4,2,512]{3,2,1,0:T(2,128)(2,1)} %param.4) | copy-start | bytes 491524
  52.8 9.7 %all-to-all-start.3 = ((f32[32,1,128]{2,1,0:T(1,128)}), f32[32,1,128]{2,1,0:T(1,128)S(1)}, u32[]{:S(2)}, u32[]{:S(2)}) async-start(f32[32,1,128]{2,1,0:T(1,128)} %broadcast_in_dim.98), calls=%async_computation.3 | async-start | bytes 32768 | tf_op jit(solution)/shard_map/all_to_all | solution.py:97

commit v16 on v15

--- a/solution.py
+++ b/solution.py
@@ -177,7 +177,7 @@
             jnp.where(first, jnp.sum(weight_rows * moved_rows * total1_rows, axis=(0, 1)), 0.0),
         ],
         jnp.zeros((grid_size * mem_size, 0, nlon), jnp.float32),
-        width=32,
+        width=128,
     )
     norm_next = sums[0]
     beta = norm_next / norm_now

time: 64.6 us -> 64.7 us (level)
  no operation moved by 1% of the time
where the time goes in v16:
time: 64.7 us; the launch traced here: 64.2 us
  waiting for transfers between devices  22.3 us (34%)
  starting transfers between devices  13.3 us (21%)
  blocking collectives  11.2 us (17%)
  other arithmetic  8.94 us (14%)
  local copies, waits for them, and re-layouts  7.32 us (11%)
  between operations  0.98 us (2%)
    all_to_all x1, blocking collectives, exchange(): got = lax.all_to_all(parcel, ('grid', 'mem'), 0, 0, tiled=True)  11.2 us
    all_to_all x1, waiting for transfers between devices, local_by_level(): got = lax.all_to_all(packed, 'grid', 1, 2, tiled=True)[:, 0]  10.3 us
    all_to_all x1, waiting for transfers between devices, exchange(): got = lax.all_to_all(parcel, ('grid', 'mem'), 0, 0, tiled=True)  7.41 us
    all_to_all x1, starting transfers between devices, local_by_level(): got = lax.all_to_all(packed, 'grid', 1, 2, tiled=True)[:, 0]  7.28 us
    all_to_all x1, waiting for transfers between devices, mem_total(): lax.all_to_all(jnp.broadcast_to(part, (mem_size,) + part.shape), 'mem', 0...  4.55 us
    all_to_all x1, starting transfers between devices, mem_total(): lax.all_to_all(jnp.broadcast_to(part, (mem_size,) + part.shape), 'mem', 0...  3.33 us
    all_to_all x1, starting transfers between devices, exchange(): got = lax.all_to_all(parcel, ('grid', 'mem'), 0, 0, tiled=True)  2.7 us
    unnamed x10, local copies, waits for them, and re-layouts  1.75 us
  transfers between devices with their start and end apart: 3, of which 3 were waited for; matrix products, arithmetic and copies ran while one was open for 1% of the time, Pallas kernels for 0%

profile of v16, /device:TPU:0, one launch (start us, length us, event | category | flops | bytes accessed | tf_op | source)
XLA Modules:
  0.0 64.2 jit_solution(4726506380289218035)
XLA Ops:
  0.6 0.8 %fusion.84 = (bf16[2,512]{1,0:T(2,128)(2,1)S(1)}, f32[2,512]{1,0:T(2,128)S(1)}) fusion(s32[2,512]{1,0:T(2,128)} %param.6), kind=kLoop, calls=%fused_computation.192 | loop fusion | flops 2048 | bytes 10240 | tf_op jit(solution)/shard_map/convert_element_type | solution.py:120
  1.4 1.0 %constant_dynamic-update-slice_fusion.4 = bf16[24,4,2,512]{3,2,1,0:T(2,128)(2,1)S(1)} fusion(bf16[20,4,2,512]{3,2,1,0:T(2,128)(2,1)} %param.4), kind=kLoop, calls=%fused_computation.142 | loop fusion | bytes 327680
  2.7 0.9 %broadcast_in_dim.84 = bf16[24,4,2,2,512]{4,3,0,2,1:T(2,128)(2,1)} broadcast(bf16[24,4,2,512]{3,2,0,1:T(2,128)(2,1)S(1)} %copy.18), dimensions={0,1,3,4} | broadcast | bytes 589824 | tf_op jit(solution)/shard_map/broadcast_in_dim | solution.py:126
  3.6 7.3 %all-to-all-start = ((bf16[24,8,2,512]{3,2,0,1:T(2,128)(2,1)}), bf16[24,8,2,512]{3,2,0,1:T(2,128)(2,1)S(1)}, u32[]{:S(2)}, u32[]{:S(2)}) async-start(bf16[24,8,2,512]{3,2,0,1:T(2,128)(2,1)} %bitcast.3), calls=%async_computation | async-start | bytes 786432 | tf_op jit(solution)/shard_map/all_to_all | solution.py:127
  11.0 0.6 %copy-done.2 = f32[4]{0:T(128)S(1)} copy-done((f32[4]{0:T(128)S(1)}, f32[4]{0:T(128)}, u32[]{:S(2)}) %copy-start.2) | copy-done | bytes 40
  11.6 0.6 dynamic_slice.7
  12.3 10.3 %all-to-all-done = bf16[24,8,2,512]{3,2,0,1:T(2,128)(2,1)S(1)} async-done(((bf16[24,8,2,512]{3,2,0,1:T(2,128)(2,1)}), bf16[24,8,2,512]{3,2,0,1:T(2,128)(2,1)S(1)}, u32[]{:S(2)}, u32[]{:S(2)}) %all-to-all-start) | async-done | bytes 393248 | tf_op jit(solution)/shard_map/all_to_all | solution.py:127
  22.9 0.5 copy.20
  23.5 0.5 reshape.384
  24.0 0.7 %fusion.61 = f32[1,8,2,512]{3,2,0,1:T(2,128)S(1)} fusion(f32[3,8,2,512]{3,2,0,1:T(2,128)S(1)} %slice_convert_fusion, f32[]{:T(128)} %bitcast.4, bf16[24,8,2,512]{3,2,0,1:T(2,128)(2,1)S(1)} %all-to-all-done), kind=kLoop, calls=%fused_computation.117 | loop fusion | flops 40960 | bytes 147460 | tf_op jit(solution)/shard_map/mul | solution.py:147
  25.2 0.9 %select_reduce_fusion.2 = (f32[512]{0:T(512)S(1)}, f32[20,16,512]{2,1,0:T(8,128)S(1)}) fusion(pred[16,512]{1,0:T(8,128)(4,1)S(1)} %select_compare_fusion, f32[20,16,2]{2,1,0:T(8,128)S(1)} %get-tuple-element.16, f32[20,16,512]{2,1,0:T(8,128)S(1)} %fusion.32, f32[20,16,2]{2,1,0:T(8,128)S(1)} %get-tuple-element.15), kind=kLoop, calls=%fused_computation.104 | loop fusion | flops 2293248 | bytes 1326080 | tf_op jit(solution)/shard_map/reduce_sum | solution.py:139
  26.5 0.9 %fusion.21 = f32[16,512]{1,0:T(8,128)S(1)} fusion(f32[20,16,512]{2,1,0:T(8,128)S(1)} %reshape.384, f32[20,16,512]{2,1,0:T(8,128)S(1)} %fusion.38, f32[20,16,2]{2,1,0:T(8,128)S(1)} %get-tuple-element.14, f32[20,16,2]{2,1,0:T(8,128)S(1)} %get-tuple-element.13), kind=kLoop, calls=%fused_computation.53 | loop fusion | flops 2121728 | bytes 1348608 | tf_op jit(solution)/shard_map/reduce_sum | solution.py:148
  27.4 0.7 %broadcast_in_dim.86 = f32[4,16,512]{2,1,0:T(8,128)} broadcast(f32[16,512]{1,0:T(8,128)S(1)} %fusion.21), dimensions={1,2} | broadcast | bytes 163840 | tf_op jit(solution)/shard_map/broadcast_in_dim | solution.py:106
  28.1 3.3 %all-to-all-start.1 = ((f32[4,16,512]{2,1,0:T(8,128)}), f32[4,16,512]{2,1,0:T(8,128)S(1)}, u32[]{:S(2)}, u32[]{:S(2)}) async-start(f32[4,16,512]{2,1,0:T(8,128)} %broadcast_in_dim.86), calls=%async_computation.1 | async-start | bytes 262144 | tf_op jit(solution)/shard_map/all_to_all | solution.py:106
  31.4 4.5 %all-to-all-done.1 = f32[4,16,512]{2,1,0:T(8,128)S(1)} async-done(((f32[4,16,512]{2,1,0:T(8,128)}), f32[4,16,512]{2,1,0:T(8,128)S(1)}, u32[]{:S(2)}, u32[]{:S(2)}) %all-to-all-start.1) | async-done | bytes 131104 | tf_op jit(solution)/shard_map/all_to_all | solution.py:106
  36.0 0.8 %fusion.66 = (f32[512]{0:T(512)S(1)}, f32[1,8,2,512]{3,2,0,1:T(2,128)S(1)}) fusion(f32[1,8,2,512]{3,2,1,0:T(2,128)S(1)} %reduce_sum.172, pred[8,2]{1,0:T(8,128)(4,1)S(1)} %fusion.70, s32[]{:T(128)S(6)} %select_n.117, s32[8,2]{1,0:T(8,128)S(1)} %get-tuple-element.31, s32[8,2]{1,0:T(8,128)S(1)} %get-tuple-element.32, f32[]{:T(128)} %bitcast.4, ...), kind=kLoop, calls=%fused_computation.125 | loop fusion | flops 65024 | bytes 84120 | tf_op jit(solution)/shard_map/reduce_sum | solution.py:142
  37.3 0.9 %fusion.13 = f32[20,16,512]{2,1,0:T(8,128)S(1)} fusion(f32[20,16,512]{2,1,0:T(8,128)S(1)} %get-tuple-element.8, f32[20,16,512]{2,1,0:T(8,128)S(1)} %fusion.44, f32[20,16,2]{2,1,0:T(8,128)S(1)} %get-tuple-element.12, f32[20,16,2]{2,1,0:T(8,128)S(1)} %get-tuple-element.11), kind=kLoop, calls=%fused_computation.45 | loop fusion | flops 1966080 | bytes 1971200 | tf_op jit(solution)/shard_map/add | solution.py:149
  38.7 0.9 %fusion.6 = f32[16,512]{1,0:T(8,128)S(1)} fusion(f32[20,16,512]{2,1,0:T(8,128)S(1)} %reshape.384, f32[20,16,512]{2,1,0:T(8,128)S(1)} %fusion.50, f32[20,16,2]{2,1,0:T(8,128)S(1)} %get-tuple-element.10, f32[20,16,2]{2,1,0:T(8,128)S(1)} %get-tuple-element.9), kind=kLoop, calls=%fused_computation.38 | loop fusion | flops 2121728 | bytes 1348608 | tf_op jit(solution)/shard_map/reduce_sum | solution.py:150
  39.8 11.2 %all_to_all.32 = f32[32,1,1280]{2,1,0:T(1,128)S(1)} all-to-all(f32[32,1,1280]{2,1,0:T(1,128)S(1)} %all_to_all.24), channel_id=1, replica_groups=mesh['grid'=8,'mem'=4] {'grid','mem'}, dimensions={0} | all-to-all | bytes 327680 | tf_op jit(solution)/shard_map/all_to_all | solution.py:97
  51.8 0.7 %broadcast_in_dim.91 = f32[32,1,512]{2,1,0:T(1,128)} broadcast(f32[512]{0:T(512)S(1)} %pad_maximum_fusion.10), dimensions={2} | broadcast | bytes 67584 | tf_op jit(solution)/shard_map/broadcast_in_dim | solution.py:95
  52.4 2.7 %all-to-all-start.3 = ((f32[32,1,512]{2,1,0:T(1,128)}), f32[32,1,512]{2,1,0:T(1,128)S(1)}, u32[]{:S(2)}, u32[]{:S(2)}) async-start(f32[32,1,512]{2,1,0:T(1,128)} %broadcast_in_dim.91), calls=%async_computation.3 | async-start | bytes 131072 | tf_op jit(solution)/shard_map/all_to_all | solution.py:97
  55.1 7.4 %all-to-all-done.3 = f32[32,1,512]{2,1,0:T(1,128)S(1)} async-done(((f32[32,1,512]{2,1,0:T(1,128)}), f32[32,1,512]{2,1,0:T(1,128)S(1)}, u32[]{:S(2)}, u32[]{:S(2)}) %all-to-all-start.3) | async-done | bytes 65568 | tf_op jit(solution)/shard_map/all_to_all | solution.py:97
  62.8 0.8 %add_convert_fusion = bf16[20,4,2,512]{3,2,1,0:T(2,128)(2,1)} fusion(bf16[20,4,2,512]{3,2,1,0:T(2,128)(2,1)S(1)} %copy-done, f32[4,2,512]{2,1,0:T(2,128)S(1)} %multiply_add_fusion), kind=kLoop, calls=%fused_computation.106 | loop fusion | flops 245760 | bytes 344064 | tf_op jit(solution)/shard_map/convert_element_type | solution.py:192
  63.6 0.6 constant_dynamic-slice_fusion
  (63 shorter events, 3.9 us)
Async XLA Ops:
  1.4 1.1 %copy-start.1 = (f32[4,2,512]{2,1,0:T(2,128)S(1)}, f32[4,2,512]{2,1,0:T(2,128)}, u32[]{:S(2)}) copy-start(f32[4,2,512]{2,1,0:T(2,128)} %param.5) | copy-start | bytes 49156
  3.6 19.0 %all-to-all-start = ((bf16[24,8,2,512]{3,2,0,1:T(2,128)(2,1)}), bf16[24,8,2,512]{3,2,0,1:T(2,128)(2,1)S(1)}, u32[]{:S(2)}, u32[]{:S(2)}) async-start(bf16[24,8,2,512]{3,2,0,1:T(2,128)(2,1)} %bitcast.3), calls=%async_computation | async-start | bytes 786432 | tf_op jit(solution)/shard_map/all_to_all | solution.py:127
  10.9 0.7 %copy-start.2 = (f32[4]{0:T(128)S(1)}, f32[4]{0:T(128)}, u32[]{:S(2)}) copy-start(f32[4]{0:T(128)} %param.7) | copy-start | bytes 52
  28.1 7.9 %all-to-all-start.1 = ((f32[4,16,512]{2,1,0:T(8,128)}), f32[4,16,512]{2,1,0:T(8,128)S(1)}, u32[]{:S(2)}, u32[]{:S(2)}) async-start(f32[4,16,512]{2,1,0:T(8,128)} %broadcast_in_dim.86), calls=%async_computation.1 | async-start | bytes 262144 | tf_op jit(solution)/shard_map/all_to_all | solution.py:106
  52.4 10.4 %copy-start = (bf16[20,4,2,512]{3,2,1,0:T(2,128)(2,1)S(1)}, bf16[20,4,2,512]{3,2,1,0:T(2,128)(2,1)}, u32[]{:S(2)}) copy-start(bf16[20,4,2,512]{3,2,1,0:T(2,128)(2,1)} %param.4) | copy-start | bytes 491524
  52.4 10.1 %all-to-all-start.3 = ((f32[32,1,512]{2,1,0:T(1,128)}), f32[32,1,512]{2,1,0:T(1,128)S(1)}, u32[]{:S(2)}, u32[]{:S(2)}) async-start(f32[32,1,512]{2,1,0:T(1,128)} %broadcast_in_dim.91), calls=%async_computation.3 | async-start | bytes 131072 | tf_op jit(solution)/shard_map/all_to_all | solution.py:97

commit v17 on v16

--- a/solution.py
+++ b/solution.py
@@ -2,6 +2,7 @@
 import jax.numpy as jnp
 from jax import lax
 from jax.sharding import PartitionSpec as P
+
 
 PASSES = 2
 ITERS = 2
@@ -24,11 +25,11 @@
 
 
 def smooth(field):
-    for sweep_index in range(PASSES):
+    for _ in range(PASSES):
         extended = padded(field, (("grid", 2),), 1)
         centre = extended[:, :, 1:-1]
         field = centre + diffusion * (extended[:, :, :-2] + extended[:, :, 2:] - 2.0 * centre)
-    for sweep_index in range(PASSES):
+    for _ in range(PASSES):
         field = field + diffusion * (jnp.roll(field, 1, 3) + jnp.roll(field, -1, 3) - 2.0 * field)
     return field
 
@@ -107,7 +108,11 @@
     return jnp.sum(got, axis=0)
 
 
-def local_by_level(members, innovation, observed_count, obs_precision):
+def local_by_level(*args):
+    return level_body(*args)
+
+
+def level_body(members, innovation, observed_count, obs_precision):
     grid_size = lax.axis_size("grid")
     mem_size = lax.axis_size("mem")
     count, levels, rows, nlon = members.shape
@@ -153,7 +158,8 @@
         rows_for = jnp.where(grid_index % copies == 0, by_target(total1), by_target(image_part))
     else:
         rows_for = jnp.concatenate([by_target(total1), by_target(image_part)], axis=1)
-    sums1, got1 = exchange([squares(residual), weighted(total1)], rows_for)
+    norm_part = squares(lax.optimization_barrier(residual))
+    sums1, got1 = exchange([norm_part, weighted(total1)], rows_for)
     norm_now = sums1[0]
     curvature1 = sums1[1]
     step1 = norm_now / (norm_now + curvature1)
@@ -188,7 +194,11 @@
     whole = step1 * total1_rows + step2 * total2_rows
 
     share = levels // mem_size
-    mine_out = lax.dynamic_slice_in_dim(whole, mem_index * share, share, 0)
+    if share == 1:
+        pick = lax.broadcasted_iota(jnp.int32, (levels, 1, 1), 0) == mem_index
+        mine_out = jnp.sum(jnp.where(pick, whole, 0.0), axis=0, keepdims=True)
+    else:
+        mine_out = lax.dynamic_slice_in_dim(whole, mem_index * share, share, 0)
     recentred = (members.astype(jnp.float32) + whole[None]).astype(jnp.bfloat16)
     return (recentred, mine_out)
 

time: 64.7 us -> 64.7 us (level)
  other arithmetic: 8.94 us -> 9.7 us
    add x2, other arithmetic: 0.9 us -> 1.75 us  [the longest x1 0.88 us: level_body(): image = residual + smooth_rows(widened * (weight * total1)[None])]
    reduce_sum x2, other arithmetic: 1.09 us -> 0.31 us  [squares(): return jnp.sum(jnp.where(own[None], field * field, 0.0), axis=(0, 1))]
    reduce_sum x4 -> x5, other arithmetic: 1.89 us -> 2.58 us  [the longest x1 0.88 us: level_body(): total1 = mem_total(jnp.sum(widened * smooth_rows(residual), axis=0))]
where the time goes in v17:
time: 64.7 us; the launch traced here: 64.3 us
  waiting for transfers between devices  22.1 us (34%)
  starting transfers between devices  13.3 us (21%)
  blocking collectives  11.2 us (17%)
  other arithmetic  9.7 us (15%)
  local copies, waits for them, and re-layouts  6.72 us (10%)
  between operations  0.99 us (2%)
    all_to_all x1, blocking collectives, exchange(): got = lax.all_to_all(parcel, ('grid', 'mem'), 0, 0, tiled=True)  11.2 us
    all_to_all x1, waiting for transfers between devices, level_body(): got = lax.all_to_all(packed, 'grid', 1, 2, tiled=True)[:, 0]  10.3 us
    all_to_all x1, waiting for transfers between devices, exchange(): got = lax.all_to_all(parcel, ('grid', 'mem'), 0, 0, tiled=True)  7.4 us
    all_to_all x1, starting transfers between devices, level_body(): got = lax.all_to_all(packed, 'grid', 1, 2, tiled=True)[:, 0]  7.28 us
    all_to_all x1, waiting for transfers between devices, mem_total(): lax.all_to_all(jnp.broadcast_to(part, (mem_size,) + part.shape), 'mem', 0...  4.43 us
    all_to_all x1, starting transfers between devices, mem_total(): lax.all_to_all(jnp.broadcast_to(part, (mem_size,) + part.shape), 'mem', 0...  3.33 us
    all_to_all x1, starting transfers between devices, exchange(): got = lax.all_to_all(parcel, ('grid', 'mem'), 0, 0, tiled=True)  2.7 us
    unnamed x10, local copies, waits for them, and re-layouts  1.75 us
  transfers between devices with their start and end apart: 3, of which 3 were waited for; matrix products, arithmetic and copies ran while one was open for 1% of the time, Pallas kernels for 0%

profile of v17, /device:TPU:0, one launch (start us, length us, event | category | flops | bytes accessed | tf_op | source)
XLA Modules:
  0.0 64.3 jit_solution(892293521453520065)
XLA Ops:
  0.6 0.8 %fusion.83 = (bf16[2,512]{1,0:T(2,128)(2,1)S(1)}, f32[2,512]{1,0:T(2,128)S(1)}) fusion(s32[2,512]{1,0:T(2,128)} %param.6), kind=kLoop, calls=%fused_computation.193 | loop fusion | flops 2048 | bytes 10240 | tf_op jit(solution)/shard_map/convert_element_type | solution.py:125
  1.4 1.0 %constant_dynamic-update-slice_fusion.4 = bf16[24,4,2,512]{3,2,1,0:T(2,128)(2,1)S(1)} fusion(bf16[20,4,2,512]{3,2,1,0:T(2,128)(2,1)} %param.4), kind=kLoop, calls=%fused_computation.143 | loop fusion | bytes 327680
  2.7 0.9 %broadcast_in_dim.99 = bf16[24,4,2,2,512]{4,3,0,2,1:T(2,128)(2,1)} broadcast(bf16[24,4,2,512]{3,2,0,1:T(2,128)(2,1)S(1)} %copy.18), dimensions={0,1,3,4} | broadcast | bytes 589824 | tf_op jit(solution)/shard_map/broadcast_in_dim | solution.py:131
  3.6 7.3 %all-to-all-start = ((bf16[24,8,2,512]{3,2,0,1:T(2,128)(2,1)}), bf16[24,8,2,512]{3,2,0,1:T(2,128)(2,1)S(1)}, u32[]{:S(2)}, u32[]{:S(2)}) async-start(bf16[24,8,2,512]{3,2,0,1:T(2,128)(2,1)} %bitcast.3), calls=%async_computation | async-start | bytes 786432 | tf_op jit(solution)/shard_map/all_to_all | solution.py:132
  11.0 0.6 %copy-done.2 = f32[4]{0:T(128)S(1)} copy-done((f32[4]{0:T(128)S(1)}, f32[4]{0:T(128)}, u32[]{:S(2)}) %copy-start.2) | copy-done | bytes 40
  11.6 0.6 dynamic_slice.4
  12.3 10.3 %all-to-all-done = bf16[24,8,2,512]{3,2,0,1:T(2,128)(2,1)S(1)} async-done(((bf16[24,8,2,512]{3,2,0,1:T(2,128)(2,1)}), bf16[24,8,2,512]{3,2,0,1:T(2,128)(2,1)S(1)}, u32[]{:S(2)}, u32[]{:S(2)}) %all-to-all-start) | async-done | bytes 393248 | tf_op jit(solution)/shard_map/all_to_all | solution.py:132
  22.9 0.5 copy.20
  23.5 0.5 reshape.389
  24.0 0.7 %fusion.61 = f32[1,8,2,512]{3,2,0,1:T(2,128)S(1)} fusion(f32[3,8,2,512]{3,2,0,1:T(2,128)S(1)} %slice_convert_fusion, f32[]{:T(128)} %bitcast.4, bf16[24,8,2,512]{3,2,0,1:T(2,128)(2,1)S(1)} %all-to-all-done), kind=kLoop, calls=%fused_computation.117 | loop fusion | flops 40960 | bytes 147460 | tf_op jit(solution)/shard_map/mul | solution.py:152
  25.2 0.9 %fusion.27 = f32[20,16,512]{2,1,0:T(8,128)S(1)} fusion(f32[20,16,512]{2,1,0:T(8,128)S(1)} %fusion.32, f32[20,16,2]{2,1,0:T(8,128)S(1)} %get-tuple-element.16, f32[20,16,2]{2,1,0:T(8,128)S(1)} %get-tuple-element.15), kind=kLoop, calls=%fused_computation.59 | loop fusion | flops 1802240 | bytes 1315840 | tf_op jit(solution)/shard_map/add | solution.py:88
  26.5 0.9 %fusion.21 = f32[16,512]{1,0:T(8,128)S(1)} fusion(f32[20,16,512]{2,1,0:T(8,128)S(1)} %reshape.389, f32[20,16,512]{2,1,0:T(8,128)S(1)} %fusion.38, f32[20,16,2]{2,1,0:T(8,128)S(1)} %get-tuple-element.14, f32[20,16,2]{2,1,0:T(8,128)S(1)} %get-tuple-element.13), kind=kLoop, calls=%fused_computation.53 | loop fusion | flops 2121728 | bytes 1348608 | tf_op jit(solution)/shard_map/reduce_sum | solution.py:153
  27.4 0.7 %broadcast_in_dim.101 = f32[4,16,512]{2,1,0:T(8,128)} broadcast(f32[16,512]{1,0:T(8,128)S(1)} %fusion.21), dimensions={1,2} | broadcast | bytes 163840 | tf_op jit(solution)/shard_map/broadcast_in_dim | solution.py:107
  28.1 3.3 %all-to-all-start.1 = ((f32[4,16,512]{2,1,0:T(8,128)}), f32[4,16,512]{2,1,0:T(8,128)S(1)}, u32[]{:S(2)}, u32[]{:S(2)}) async-start(f32[4,16,512]{2,1,0:T(8,128)} %broadcast_in_dim.101), calls=%async_computation.1 | async-start | bytes 262144 | tf_op jit(solution)/shard_map/all_to_all | solution.py:107
  31.5 4.4 %all-to-all-done.1 = f32[4,16,512]{2,1,0:T(8,128)S(1)} async-done(((f32[4,16,512]{2,1,0:T(8,128)}), f32[4,16,512]{2,1,0:T(8,128)S(1)}, u32[]{:S(2)}, u32[]{:S(2)}) %all-to-all-start.1) | async-done | bytes 131104 | tf_op jit(solution)/shard_map/all_to_all | solution.py:107
  36.0 0.8 %fusion.66 = (f32[512]{0:T(512)S(1)}, f32[1,8,2,512]{3,2,0,1:T(2,128)S(1)}) fusion(f32[1,8,2,512]{3,2,1,0:T(2,128)S(1)} %reduce_sum.181, pred[8,2]{1,0:T(8,128)(4,1)S(1)} %fusion.70, s32[]{:T(128)S(6)} %select_n.118, s32[8,2]{1,0:T(8,128)S(1)} %get-tuple-element.29, s32[8,2]{1,0:T(8,128)S(1)} %get-tuple-element.30, f32[]{:T(128)} %bitcast.4, ...), kind=kLoop, calls=%fused_computation.125 | loop fusion | flops 65024 | bytes 84120 | tf_op jit(solution)/shard_map/reduce_sum | solution.py:147
  37.3 0.9 %fusion.13 = f32[20,16,512]{2,1,0:T(8,128)S(1)} fusion(f32[20,16,512]{2,1,0:T(8,128)S(1)} %fusion.27, f32[20,16,512]{2,1,0:T(8,128)S(1)} %fusion.44, f32[20,16,2]{2,1,0:T(8,128)S(1)} %get-tuple-element.12, f32[20,16,2]{2,1,0:T(8,128)S(1)} %get-tuple-element.11), kind=kLoop, calls=%fused_computation.45 | loop fusion | flops 1966080 | bytes 1971200 | tf_op jit(solution)/shard_map/add | solution.py:154
  38.6 0.9 %fusion.6 = f32[16,512]{1,0:T(8,128)S(1)} fusion(f32[20,16,512]{2,1,0:T(8,128)S(1)} %reshape.389, f32[20,16,512]{2,1,0:T(8,128)S(1)} %fusion.50, f32[20,16,2]{2,1,0:T(8,128)S(1)} %get-tuple-element.10, f32[20,16,2]{2,1,0:T(8,128)S(1)} %get-tuple-element.9), kind=kLoop, calls=%fused_computation.38 | loop fusion | flops 2121728 | bytes 1348608 | tf_op jit(solution)/shard_map/reduce_sum | solution.py:155
  39.8 11.2 %all_to_all.32 = f32[32,1,1280]{2,1,0:T(1,128)S(1)} all-to-all(f32[32,1,1280]{2,1,0:T(1,128)S(1)} %all_to_all.24), channel_id=1, replica_groups=mesh['grid'=8,'mem'=4] {'grid','mem'}, dimensions={0} | all-to-all | bytes 327680 | tf_op jit(solution)/shard_map/all_to_all | solution.py:98
  51.7 0.7 %broadcast_in_dim.106 = f32[32,1,512]{2,1,0:T(1,128)} broadcast(f32[512]{0:T(512)S(1)} %pad_maximum_fusion.10), dimensions={2} | broadcast | bytes 67584 | tf_op jit(solution)/shard_map/broadcast_in_dim | solution.py:96
  52.4 2.7 %all-to-all-start.3 = ((f32[32,1,512]{2,1,0:T(1,128)}), f32[32,1,512]{2,1,0:T(1,128)S(1)}, u32[]{:S(2)}, u32[]{:S(2)}) async-start(f32[32,1,512]{2,1,0:T(1,128)} %broadcast_in_dim.106), calls=%async_computation.3 | async-start | bytes 131072 | tf_op jit(solution)/shard_map/all_to_all | solution.py:98
  55.1 7.4 %all-to-all-done.3 = f32[32,1,512]{2,1,0:T(1,128)S(1)} async-done(((f32[32,1,512]{2,1,0:T(1,128)}), f32[32,1,512]{2,1,0:T(1,128)S(1)}, u32[]{:S(2)}, u32[]{:S(2)}) %all-to-all-start.3) | async-done | bytes 65568 | tf_op jit(solution)/shard_map/all_to_all | solution.py:98
  62.8 0.7 %select_reduce_fusion.3 = (f32[2,512]{1,0:T(2,128)}, f32[4,2,512]{2,1,0:T(2,128)S(1)}) fusion(pred[4]{0:T(512)(128)(4,1)S(1)} %iota_compare_fusion, f32[4,2,512]{2,1,0:T(2,128)S(1)} %get-tuple-element.8, f32[512]{0:T(512)S(1)} %get-tuple-element.26, f32[512]{0:T(512)S(1)} %get-tuple-element.25, f32[4,2,4,2,512]{4,3,2,1,0:T(2,128)S(1)} %reshape_reshape.3, ...), kind=kLoop, calls=%fused_computation.132 | loop fusion | flops 27648 | bytes 59396 | tf_op jit(solution)/shard_map/reduce_sum | solution.py:199
  63.5 0.8 %add_convert_fusion = bf16[20,4,2,512]{3,2,1,0:T(2,128)(2,1)} fusion(bf16[20,4,2,512]{3,2,1,0:T(2,128)(2,1)S(1)} %copy-done, f32[4,2,512]{2,1,0:T(2,128)S(1)} %get-tuple-element.7), kind=kLoop, calls=%fused_computation.106 | loop fusion | flops 245760 | bytes 344064 | tf_op jit(solution)/shard_map/convert_element_type | solution.py:202
  (64 shorter events, 4.0 us)
Async XLA Ops:
  1.4 1.1 %copy-start.1 = (f32[4,2,512]{2,1,0:T(2,128)S(1)}, f32[4,2,512]{2,1,0:T(2,128)}, u32[]{:S(2)}) copy-start(f32[4,2,512]{2,1,0:T(2,128)} %param.5) | copy-start | bytes 49156
  3.6 19.0 %all-to-all-start = ((bf16[24,8,2,512]{3,2,0,1:T(2,128)(2,1)}), bf16[24,8,2,512]{3,2,0,1:T(2,128)(2,1)S(1)}, u32[]{:S(2)}, u32[]{:S(2)}) async-start(bf16[24,8,2,512]{3,2,0,1:T(2,128)(2,1)} %bitcast.3), calls=%async_computation | async-start | bytes 786432 | tf_op jit(solution)/shard_map/all_to_all | solution.py:132
  10.9 0.7 %copy-start.2 = (f32[4]{0:T(128)S(1)}, f32[4]{0:T(128)}, u32[]{:S(2)}) copy-start(f32[4]{0:T(128)} %param.7) | copy-start | bytes 52
  28.1 7.9 %all-to-all-start.1 = ((f32[4,16,512]{2,1,0:T(8,128)}), f32[4,16,512]{2,1,0:T(8,128)S(1)}, u32[]{:S(2)}, u32[]{:S(2)}) async-start(f32[4,16,512]{2,1,0:T(8,128)} %broadcast_in_dim.101), calls=%async_computation.1 | async-start | bytes 262144 | tf_op jit(solution)/shard_map/all_to_all | solution.py:107
  52.4 11.1 %copy-start = (bf16[20,4,2,512]{3,2,1,0:T(2,128)(2,1)S(1)}, bf16[20,4,2,512]{3,2,1,0:T(2,128)(2,1)}, u32[]{:S(2)}) copy-start(bf16[20,4,2,512]{3,2,1,0:T(2,128)(2,1)} %param.4) | copy-start | bytes 491524
  52.4 10.1 %all-to-all-start.3 = ((f32[32,1,512]{2,1,0:T(1,128)}), f32[32,1,512]{2,1,0:T(1,128)S(1)}, u32[]{:S(2)}, u32[]{:S(2)}) async-start(f32[32,1,512]{2,1,0:T(1,128)} %broadcast_in_dim.106), calls=%async_computation.3 | async-start | bytes 131072 | tf_op jit(solution)/shard_map/all_to_all | solution.py:98

commit v18 on v16

--- a/solution.py
+++ b/solution.py
@@ -129,7 +129,7 @@
     innov = (split[0] + split[1]) + split[2]
     precision = lax.dynamic_index_in_dim(obs_precision, level, 0, keepdims=False)
     weight = got[count].astype(jnp.float32) * precision
-    widened = got[:count].astype(jnp.float32)
+    widened = lax.optimization_barrier(got[:count]).astype(jnp.float32)
 
     span = nlat // copies
     own = (lax.broadcasted_iota(jnp.int32, (nlat, nlon), 0) // span) == grid_index % copies

time: 64.7 us -> 64.1 us (level)
    convert_element_type x2 -> x0, local copies, waits for them, and re-layouts: 0.96 us -> none  [local_by_level(): widened = got[:count].astype(jnp.float32)]
where the time goes in v18:
time: 64.1 us; the launch traced here: 63.6 us
  waiting for transfers between devices  22.3 us (35%)
  starting transfers between devices  13.3 us (21%)
  blocking collectives  11.2 us (17%)
  other arithmetic  8.89 us (14%)
  local copies, waits for them, and re-layouts  6.8 us (11%)
  between operations  0.98 us (2%)
    all_to_all x1, blocking collectives, exchange(): got = lax.all_to_all(parcel, ('grid', 'mem'), 0, 0, tiled=True)  11.2 us
    all_to_all x1, waiting for transfers between devices, local_by_level(): got = lax.all_to_all(packed, 'grid', 1, 2, tiled=True)[:, 0]  10.3 us
    all_to_all x1, waiting for transfers between devices, exchange(): got = lax.all_to_all(parcel, ('grid', 'mem'), 0, 0, tiled=True)  7.41 us
    all_to_all x1, starting transfers between devices, local_by_level(): got = lax.all_to_all(packed, 'grid', 1, 2, tiled=True)[:, 0]  7.28 us
    all_to_all x1, waiting for transfers between devices, mem_total(): lax.all_to_all(jnp.broadcast_to(part, (mem_size,) + part.shape), 'mem', 0...  4.55 us
    all_to_all x1, starting transfers between devices, mem_total(): lax.all_to_all(jnp.broadcast_to(part, (mem_size,) + part.shape), 'mem', 0...  3.33 us
    all_to_all x1, starting transfers between devices, exchange(): got = lax.all_to_all(parcel, ('grid', 'mem'), 0, 0, tiled=True)  2.7 us
    unnamed x10, local copies, waits for them, and re-layouts  1.75 us
  transfers between devices with their start and end apart: 3, of which 3 were waited for; matrix products, arithmetic and copies ran while one was open for 1% of the time, Pallas kernels for 0%

profile of v18, /device:TPU:0, one launch (start us, length us, event | category | flops | bytes accessed | tf_op | source)
XLA Modules:
  0.0 63.6 jit_solution(8869877844181429534)
XLA Ops:
  0.6 0.8 %fusion.82 = (bf16[2,512]{1,0:T(2,128)(2,1)S(1)}, f32[2,512]{1,0:T(2,128)S(1)}) fusion(s32[2,512]{1,0:T(2,128)} %param.6), kind=kLoop, calls=%fused_computation.191 | loop fusion | flops 2048 | bytes 10240 | tf_op jit(solution)/shard_map/convert_element_type | solution.py:120
  1.4 1.0 %constant_dynamic-update-slice_fusion.4 = bf16[24,4,2,512]{3,2,1,0:T(2,128)(2,1)S(1)} fusion(bf16[20,4,2,512]{3,2,1,0:T(2,128)(2,1)} %param.4), kind=kLoop, calls=%fused_computation.141 | loop fusion | bytes 327680
  2.7 0.9 %broadcast_in_dim.84 = bf16[24,4,2,2,512]{4,3,0,2,1:T(2,128)(2,1)} broadcast(bf16[24,4,2,512]{3,2,0,1:T(2,128)(2,1)S(1)} %copy.13), dimensions={0,1,3,4} | broadcast | bytes 589824 | tf_op jit(solution)/shard_map/broadcast_in_dim | solution.py:126
  3.6 7.3 %all-to-all-start = ((bf16[24,8,2,512]{3,2,0,1:T(2,128)(2,1)}), bf16[24,8,2,512]{3,2,0,1:T(2,128)(2,1)S(1)}, u32[]{:S(2)}, u32[]{:S(2)}) async-start(bf16[24,8,2,512]{3,2,0,1:T(2,128)(2,1)} %bitcast.3), calls=%async_computation | async-start | bytes 786432 | tf_op jit(solution)/shard_map/all_to_all | solution.py:127
  11.0 0.6 %copy-done.2 = f32[4]{0:T(128)S(1)} copy-done((f32[4]{0:T(128)S(1)}, f32[4]{0:T(128)}, u32[]{:S(2)}) %copy-start.2) | copy-done | bytes 40
  11.6 0.6 dynamic_slice.7
  12.3 10.3 %all-to-all-done = bf16[24,8,2,512]{3,2,0,1:T(2,128)(2,1)S(1)} async-done(((bf16[24,8,2,512]{3,2,0,1:T(2,128)(2,1)}), bf16[24,8,2,512]{3,2,0,1:T(2,128)(2,1)S(1)}, u32[]{:S(2)}, u32[]{:S(2)}) %all-to-all-start) | async-done | bytes 393248 | tf_op jit(solution)/shard_map/all_to_all | solution.py:127
  23.3 0.7 %fusion.59 = f32[1,8,2,512]{3,2,0,1:T(2,128)S(1)} fusion(f32[3,8,2,512]{3,2,0,1:T(2,128)S(1)} %slice_convert_fusion, f32[]{:T(128)} %bitcast.4, bf16[24,8,2,512]{3,2,0,1:T(2,128)(2,1)S(1)} %all-to-all-done), kind=kLoop, calls=%fused_computation.116 | loop fusion | flops 40960 | bytes 147460 | tf_op jit(solution)/shard_map/mul | solution.py:147
  24.1 0.3 fusion.28
  24.6 0.9 %select_reduce_fusion.2 = (f32[512]{0:T(512)S(1)}, f32[20,16,512]{2,1,0:T(8,128)S(1)}) fusion(pred[16,512]{1,0:T(8,128)(4,1)S(1)} %select_compare_fusion, f32[20,16,2]{2,1,0:T(8,128)S(1)} %get-tuple-element.16, f32[20,16,512]{2,1,0:T(8,128)S(1)} %fusion.28, f32[20,16,2]{2,1,0:T(8,128)S(1)} %get-tuple-element.15), kind=kLoop, calls=%fused_computation.104 | loop fusion | flops 2293248 | bytes 1326080 | tf_op jit(solution)/shard_map/reduce_sum | solution.py:139
  25.9 0.9 %fusion.57 = f32[16,512]{1,0:T(8,128)S(1)} fusion(f32[20,16,2]{2,1,0:T(8,128)S(1)} %get-tuple-element.14, f32[20,16,512]{2,1,0:T(8,128)S(1)} %fusion.34, f32[20,16,2]{2,1,0:T(8,128)S(1)} %get-tuple-element.13, bf16[20,16,512]{2,1,0:T(8,128)(2,1)S(1)} %slice.194), kind=kLoop, calls=%fused_computation.105 | loop fusion | flops 2285568 | bytes 1020928 | tf_op jit(solution)/shard_map/reduce_sum | solution.py:148
  26.8 0.7 %broadcast_in_dim.86 = f32[4,16,512]{2,1,0:T(8,128)} broadcast(f32[16,512]{1,0:T(8,128)S(1)} %fusion.57), dimensions={1,2} | broadcast | bytes 163840 | tf_op jit(solution)/shard_map/broadcast_in_dim | solution.py:106
  27.5 3.3 %all-to-all-start.1 = ((f32[4,16,512]{2,1,0:T(8,128)}), f32[4,16,512]{2,1,0:T(8,128)S(1)}, u32[]{:S(2)}, u32[]{:S(2)}) async-start(f32[4,16,512]{2,1,0:T(8,128)} %broadcast_in_dim.86), calls=%async_computation.1 | async-start | bytes 262144 | tf_op jit(solution)/shard_map/all_to_all | solution.py:106
  30.8 4.5 %all-to-all-done.1 = f32[4,16,512]{2,1,0:T(8,128)S(1)} async-done(((f32[4,16,512]{2,1,0:T(8,128)}), f32[4,16,512]{2,1,0:T(8,128)S(1)}, u32[]{:S(2)}, u32[]{:S(2)}) %all-to-all-start.1) | async-done | bytes 131104 | tf_op jit(solution)/shard_map/all_to_all | solution.py:106
  35.4 0.8 %fusion.64 = (f32[512]{0:T(512)S(1)}, f32[1,8,2,512]{3,2,0,1:T(2,128)S(1)}) fusion(f32[1,8,2,512]{3,2,1,0:T(2,128)S(1)} %reduce_sum.172, pred[8,2]{1,0:T(8,128)(4,1)S(1)} %fusion.68, s32[]{:T(128)S(6)} %select_n.117, s32[8,2]{1,0:T(8,128)S(1)} %get-tuple-element.31, s32[8,2]{1,0:T(8,128)S(1)} %get-tuple-element.32, f32[]{:T(128)} %bitcast.4, ...), kind=kLoop, calls=%fused_computation.124 | loop fusion | flops 65024 | bytes 84120 | tf_op jit(solution)/shard_map/reduce_sum | solution.py:142
  36.3 0.3 fusion.40
  36.7 0.9 %fusion.11 = f32[20,16,512]{2,1,0:T(8,128)S(1)} fusion(f32[20,16,512]{2,1,0:T(8,128)S(1)} %get-tuple-element.8, f32[20,16,512]{2,1,0:T(8,128)S(1)} %fusion.40, f32[20,16,2]{2,1,0:T(8,128)S(1)} %get-tuple-element.12, f32[20,16,2]{2,1,0:T(8,128)S(1)} %get-tuple-element.11), kind=kLoop, calls=%fused_computation.47 | loop fusion | flops 1966080 | bytes 1971200 | tf_op jit(solution)/shard_map/add | solution.py:149
  38.1 0.9 %fusion.58 = f32[16,512]{1,0:T(8,128)S(1)} fusion(f32[20,16,2]{2,1,0:T(8,128)S(1)} %get-tuple-element.10, f32[20,16,512]{2,1,0:T(8,128)S(1)} %fusion.46, f32[20,16,2]{2,1,0:T(8,128)S(1)} %get-tuple-element.9, bf16[20,16,512]{2,1,0:T(8,128)(2,1)S(1)} %slice.194), kind=kLoop, calls=%fused_computation.106 | loop fusion | flops 2285568 | bytes 1020928 | tf_op jit(solution)/shard_map/reduce_sum | solution.py:150
  39.3 11.2 %all_to_all.32 = f32[32,1,1280]{2,1,0:T(1,128)S(1)} all-to-all(f32[32,1,1280]{2,1,0:T(1,128)S(1)} %all_to_all.24), channel_id=1, replica_groups=mesh['grid'=8,'mem'=4] {'grid','mem'}, dimensions={0} | all-to-all | bytes 327680 | tf_op jit(solution)/shard_map/all_to_all | solution.py:97
  51.2 0.7 %broadcast_in_dim.91 = f32[32,1,512]{2,1,0:T(1,128)} broadcast(f32[512]{0:T(512)S(1)} %pad_maximum_fusion.10), dimensions={2} | broadcast | bytes 67584 | tf_op jit(solution)/shard_map/broadcast_in_dim | solution.py:95
  51.8 2.7 %all-to-all-start.3 = ((f32[32,1,512]{2,1,0:T(1,128)}), f32[32,1,512]{2,1,0:T(1,128)S(1)}, u32[]{:S(2)}, u32[]{:S(2)}) async-start(f32[32,1,512]{2,1,0:T(1,128)} %broadcast_in_dim.91), calls=%async_computation.3 | async-start | bytes 131072 | tf_op jit(solution)/shard_map/all_to_all | solution.py:97
  54.6 7.4 %all-to-all-done.3 = f32[32,1,512]{2,1,0:T(1,128)S(1)} async-done(((f32[32,1,512]{2,1,0:T(1,128)}), f32[32,1,512]{2,1,0:T(1,128)S(1)}, u32[]{:S(2)}, u32[]{:S(2)}) %all-to-all-start.3) | async-done | bytes 65568 | tf_op jit(solution)/shard_map/all_to_all | solution.py:97
  62.2 0.8 %add_convert_fusion = bf16[20,4,2,512]{3,2,1,0:T(2,128)(2,1)} fusion(bf16[20,4,2,512]{3,2,1,0:T(2,128)(2,1)S(1)} %copy-done, f32[4,2,512]{2,1,0:T(2,128)S(1)} %multiply_add_fusion), kind=kLoop, calls=%fused_computation.107 | loop fusion | flops 245760 | bytes 344064 | tf_op jit(solution)/shard_map/convert_element_type | solution.py:192
  63.0 0.6 constant_dynamic-slice_fusion
  (62 shorter events, 3.6 us)
Async XLA Ops:
  1.4 1.1 %copy-start.1 = (f32[4,2,512]{2,1,0:T(2,128)S(1)}, f32[4,2,512]{2,1,0:T(2,128)}, u32[]{:S(2)}) copy-start(f32[4,2,512]{2,1,0:T(2,128)} %param.5) | copy-start | bytes 49156
  3.6 19.0 %all-to-all-start = ((bf16[24,8,2,512]{3,2,0,1:T(2,128)(2,1)}), bf16[24,8,2,512]{3,2,0,1:T(2,128)(2,1)S(1)}, u32[]{:S(2)}, u32[]{:S(2)}) async-start(bf16[24,8,2,512]{3,2,0,1:T(2,128)(2,1)} %bitcast.3), calls=%async_computation | async-start | bytes 786432 | tf_op jit(solution)/shard_map/all_to_all | solution.py:127
  10.9 0.7 %copy-start.2 = (f32[4]{0:T(128)S(1)}, f32[4]{0:T(128)}, u32[]{:S(2)}) copy-start(f32[4]{0:T(128)} %param.7) | copy-start | bytes 52
  27.5 7.9 %all-to-all-start.1 = ((f32[4,16,512]{2,1,0:T(8,128)}), f32[4,16,512]{2,1,0:T(8,128)S(1)}, u32[]{:S(2)}, u32[]{:S(2)}) async-start(f32[4,16,512]{2,1,0:T(8,128)} %broadcast_in_dim.86), calls=%async_computation.1 | async-start | bytes 262144 | tf_op jit(solution)/shard_map/all_to_all | solution.py:106
  51.8 10.4 %copy-start = (bf16[20,4,2,512]{3,2,1,0:T(2,128)(2,1)S(1)}, bf16[20,4,2,512]{3,2,1,0:T(2,128)(2,1)}, u32[]{:S(2)}) copy-start(bf16[20,4,2,512]{3,2,1,0:T(2,128)(2,1)} %param.4) | copy-start | bytes 491524
  51.8 10.1 %all-to-all-start.3 = ((f32[32,1,512]{2,1,0:T(1,128)}), f32[32,1,512]{2,1,0:T(1,128)S(1)}, u32[]{:S(2)}, u32[]{:S(2)}) async-start(f32[32,1,512]{2,1,0:T(1,128)} %broadcast_in_dim.91), calls=%async_computation.3 | async-start | bytes 131072 | tf_op jit(solution)/shard_map/all_to_all | solution.py:97

commit v19 on v18

--- a/solution.py
+++ b/solution.py
@@ -125,10 +125,10 @@
     parts = jnp.stack([high, middle, low]).astype(jnp.bfloat16)
     packed = jnp.repeat(jnp.concatenate([members, counts, parts], axis=0), copies, axis=1)
     got = lax.all_to_all(packed, "grid", 1, 2, tiled=True)[:, 0]
-    split = got[count + 1 :].astype(jnp.float32)
-    innov = (split[0] + split[1]) + split[2]
+    extra = lax.optimization_barrier(got[count:]).astype(jnp.float32)
+    innov = (extra[1] + extra[2]) + extra[3]
     precision = lax.dynamic_index_in_dim(obs_precision, level, 0, keepdims=False)
-    weight = got[count].astype(jnp.float32) * precision
+    weight = extra[0] * precision
     widened = lax.optimization_barrier(got[:count]).astype(jnp.float32)
 
     span = nlat // copies

time: 64.1 us -> 64.7 us (level)
    mul x1 -> x2, other arithmetic: 0.07 us -> 0.73 us  [local_by_level(): image = residual + smooth_rows(widened * (weight * total1)[None])]
where the time goes in v19:
time: 64.7 us; the launch traced here: 64.2 us
  waiting for transfers between devices  22.3 us (34%)
  starting transfers between devices  13.3 us (21%)
  blocking collectives  11.2 us (17%)
  other arithmetic  9.46 us (15%)
  local copies, waits for them, and re-layouts  6.8 us (11%)
  between operations  0.94 us (1%)
    all_to_all x1, blocking collectives, exchange(): got = lax.all_to_all(parcel, ('grid', 'mem'), 0, 0, tiled=True)  11.2 us
    all_to_all x1, waiting for transfers between devices, local_by_level(): got = lax.all_to_all(packed, 'grid', 1, 2, tiled=True)[:, 0]  10.3 us
    all_to_all x1, waiting for transfers between devices, exchange(): got = lax.all_to_all(parcel, ('grid', 'mem'), 0, 0, tiled=True)  7.41 us
    all_to_all x1, starting transfers between devices, local_by_level(): got = lax.all_to_all(packed, 'grid', 1, 2, tiled=True)[:, 0]  7.28 us
    all_to_all x1, waiting for transfers between devices, mem_total(): lax.all_to_all(jnp.broadcast_to(part, (mem_size,) + part.shape), 'mem', 0...  4.55 us
    all_to_all x1, starting transfers between devices, mem_total(): lax.all_to_all(jnp.broadcast_to(part, (mem_size,) + part.shape), 'mem', 0...  3.33 us
    all_to_all x1, starting transfers between devices, exchange(): got = lax.all_to_all(parcel, ('grid', 'mem'), 0, 0, tiled=True)  2.7 us
    unnamed x10, local copies, waits for them, and re-layouts  1.75 us
  transfers between devices with their start and end apart: 3, of which 3 were waited for; matrix products, arithmetic and copies ran while one was open for 1% of the time, Pallas kernels for 0%

profile of v19, /device:TPU:0, one launch (start us, length us, event | category | flops | bytes accessed | tf_op | source)
XLA Modules:
  0.0 64.2 jit_solution(7729434437109772087)
XLA Ops:
  0.6 0.8 %fusion.83 = (bf16[2,512]{1,0:T(2,128)(2,1)S(1)}, f32[2,512]{1,0:T(2,128)S(1)}) fusion(s32[2,512]{1,0:T(2,128)} %param.6), kind=kLoop, calls=%fused_computation.188 | loop fusion | flops 2048 | bytes 10240 | tf_op jit(solution)/shard_map/convert_element_type | solution.py:120
  1.4 1.0 %constant_dynamic-update-slice_fusion.4 = bf16[24,4,2,512]{3,2,1,0:T(2,128)(2,1)S(1)} fusion(bf16[20,4,2,512]{3,2,1,0:T(2,128)(2,1)} %param.4), kind=kLoop, calls=%fused_computation.144 | loop fusion | bytes 327680
  2.7 0.9 %broadcast_in_dim.84 = bf16[24,4,2,2,512]{4,3,0,2,1:T(2,128)(2,1)} broadcast(bf16[24,4,2,512]{3,2,0,1:T(2,128)(2,1)S(1)} %copy.14), dimensions={0,1,3,4} | broadcast | bytes 589824 | tf_op jit(solution)/shard_map/broadcast_in_dim | solution.py:126
  3.6 7.3 %all-to-all-start = ((bf16[24,8,2,512]{3,2,0,1:T(2,128)(2,1)}), bf16[24,8,2,512]{3,2,0,1:T(2,128)(2,1)S(1)}, u32[]{:S(2)}, u32[]{:S(2)}) async-start(bf16[24,8,2,512]{3,2,0,1:T(2,128)(2,1)} %bitcast.3), calls=%async_computation | async-start | bytes 786432 | tf_op jit(solution)/shard_map/all_to_all | solution.py:127
  10.9 0.6 %copy-done.2 = f32[4]{0:T(128)S(1)} copy-done((f32[4]{0:T(128)S(1)}, f32[4]{0:T(128)}, u32[]{:S(2)}) %copy-start.2) | copy-done | bytes 40
  11.6 0.6 dynamic_slice.7
  12.2 10.3 %all-to-all-done = bf16[24,8,2,512]{3,2,0,1:T(2,128)(2,1)S(1)} async-done(((bf16[24,8,2,512]{3,2,0,1:T(2,128)(2,1)}), bf16[24,8,2,512]{3,2,0,1:T(2,128)(2,1)S(1)}, u32[]{:S(2)}, u32[]{:S(2)}) %all-to-all-start) | async-done | bytes 393248 | tf_op jit(solution)/shard_map/all_to_all | solution.py:127
  23.4 0.7 %fusion.62 = f32[16,512]{1,0:T(8,128)S(1)} fusion(f32[4,16,512]{2,1,0:T(8,128)S(1)} %copy_convert_fusion, f32[]{:T(128)} %bitcast.5), kind=kLoop, calls=%fused_computation.118 | loop fusion | flops 32768 | bytes 163844 | tf_op jit(solution)/shard_map/mul | solution.py:147
  24.6 0.9 %select_reduce_fusion.2 = (f32[512]{0:T(512)S(1)}, f32[20,16,512]{2,1,0:T(8,128)S(1)}) fusion(pred[16,512]{1,0:T(8,128)(4,1)S(1)} %select_compare_fusion, f32[20,16,2]{2,1,0:T(8,128)S(1)} %get-tuple-element.16, f32[20,16,512]{2,1,0:T(8,128)S(1)} %fusion.28, f32[20,16,2]{2,1,0:T(8,128)S(1)} %get-tuple-element.15), kind=kLoop, calls=%fused_computation.104 | loop fusion | flops 2293248 | bytes 1326080 | tf_op jit(solution)/shard_map/reduce_sum | solution.py:139
  25.9 0.9 %fusion.57 = f32[16,512]{1,0:T(8,128)S(1)} fusion(f32[20,16,2]{2,1,0:T(8,128)S(1)} %get-tuple-element.14, f32[20,16,512]{2,1,0:T(8,128)S(1)} %fusion.34, f32[20,16,2]{2,1,0:T(8,128)S(1)} %get-tuple-element.13, bf16[20,16,512]{2,1,0:T(8,128)(2,1)S(1)} %slice.192), kind=kLoop, calls=%fused_computation.105 | loop fusion | flops 2285568 | bytes 1020928 | tf_op jit(solution)/shard_map/reduce_sum | solution.py:148
  26.8 0.7 %broadcast_in_dim.86 = f32[4,16,512]{2,1,0:T(8,128)} broadcast(f32[16,512]{1,0:T(8,128)S(1)} %fusion.57), dimensions={1,2} | broadcast | bytes 163840 | tf_op jit(solution)/shard_map/broadcast_in_dim | solution.py:106
  27.5 3.3 %all-to-all-start.1 = ((f32[4,16,512]{2,1,0:T(8,128)}), f32[4,16,512]{2,1,0:T(8,128)S(1)}, u32[]{:S(2)}, u32[]{:S(2)}) async-start(f32[4,16,512]{2,1,0:T(8,128)} %broadcast_in_dim.86), calls=%async_computation.1 | async-start | bytes 262144 | tf_op jit(solution)/shard_map/all_to_all | solution.py:106
  30.8 4.5 %all-to-all-done.1 = f32[4,16,512]{2,1,0:T(8,128)S(1)} async-done(((f32[4,16,512]{2,1,0:T(8,128)}), f32[4,16,512]{2,1,0:T(8,128)S(1)}, u32[]{:S(2)}, u32[]{:S(2)}) %all-to-all-start.1) | async-done | bytes 131104 | tf_op jit(solution)/shard_map/all_to_all | solution.py:106
  35.4 0.7 %fusion.63 = f32[16,512]{1,0:T(8,128)S(1)} fusion(f32[16,512]{1,0:T(8,128)S(1)} %reduce_sum.171, f32[4,16,512]{2,1,0:T(8,128)S(1)} %copy_convert_fusion, f32[]{:T(128)} %bitcast.5), kind=kLoop, calls=%fused_computation.122 | loop fusion | flops 16384 | bytes 98308 | tf_op jit(solution)/shard_map/mul | solution.py:149
  36.1 0.3 fusion.40
  36.6 0.9 %fusion.11 = f32[20,16,512]{2,1,0:T(8,128)S(1)} fusion(f32[20,16,512]{2,1,0:T(8,128)S(1)} %get-tuple-element.8, f32[20,16,512]{2,1,0:T(8,128)S(1)} %fusion.40, f32[20,16,2]{2,1,0:T(8,128)S(1)} %get-tuple-element.12, f32[20,16,2]{2,1,0:T(8,128)S(1)} %get-tuple-element.11), kind=kLoop, calls=%fused_computation.47 | loop fusion | flops 1966080 | bytes 1971200 | tf_op jit(solution)/shard_map/add | solution.py:149
  37.9 0.9 %fusion.58 = f32[16,512]{1,0:T(8,128)S(1)} fusion(f32[20,16,2]{2,1,0:T(8,128)S(1)} %get-tuple-element.10, f32[20,16,512]{2,1,0:T(8,128)S(1)} %fusion.46, f32[20,16,2]{2,1,0:T(8,128)S(1)} %get-tuple-element.9, bf16[20,16,512]{2,1,0:T(8,128)(2,1)S(1)} %slice.192), kind=kLoop, calls=%fused_computation.106 | loop fusion | flops 2285568 | bytes 1020928 | tf_op jit(solution)/shard_map/reduce_sum | solution.py:150
  38.8 0.7 %fusion.60 = (f32[512]{0:T(512)S(1)}, f32[16,512]{1,0:T(8,128)S(1)}) fusion(f32[16,512]{1,0:T(8,128)S(1)} %reduce_sum.171, f32[4,16,512]{2,1,0:T(8,128)S(1)} %copy_convert_fusion, f32[]{:T(128)} %bitcast.5, s32[]{:T(128)S(6)} %select_n.107, s32[16]{0:T(128)S(1)} %get-tuple-element.29, s32[16]{0:T(128)S(1)} %get-tuple-element.30, ...), kind=kLoop, calls=%fused_computation.114 | loop fusion | flops 65024 | bytes 133273 | tf_op jit(solution)/shard_map/reduce_sum | solution.py:142
  39.8 11.2 %all_to_all.32 = f32[32,1,1280]{2,1,0:T(1,128)S(1)} all-to-all(f32[32,1,1280]{2,1,0:T(1,128)S(1)} %all_to_all.24), channel_id=1, replica_groups=mesh['grid'=8,'mem'=4] {'grid','mem'}, dimensions={0} | all-to-all | bytes 327680 | tf_op jit(solution)/shard_map/all_to_all | solution.py:97
  51.8 0.7 %broadcast_in_dim.91 = f32[32,1,512]{2,1,0:T(1,128)} broadcast(f32[512]{0:T(512)S(1)} %pad_maximum_fusion.10), dimensions={2} | broadcast | bytes 67584 | tf_op jit(solution)/shard_map/broadcast_in_dim | solution.py:95
  52.4 2.7 %all-to-all-start.3 = ((f32[32,1,512]{2,1,0:T(1,128)}), f32[32,1,512]{2,1,0:T(1,128)S(1)}, u32[]{:S(2)}, u32[]{:S(2)}) async-start(f32[32,1,512]{2,1,0:T(1,128)} %broadcast_in_dim.91), calls=%async_computation.3 | async-start | bytes 131072 | tf_op jit(solution)/shard_map/all_to_all | solution.py:97
  55.1 7.4 %all-to-all-done.3 = f32[32,1,512]{2,1,0:T(1,128)S(1)} async-done(((f32[32,1,512]{2,1,0:T(1,128)}), f32[32,1,512]{2,1,0:T(1,128)S(1)}, u32[]{:S(2)}, u32[]{:S(2)}) %all-to-all-start.3) | async-done | bytes 65568 | tf_op jit(solution)/shard_map/all_to_all | solution.py:97
  62.8 0.8 %add_convert_fusion = bf16[20,4,2,512]{3,2,1,0:T(2,128)(2,1)} fusion(bf16[20,4,2,512]{3,2,1,0:T(2,128)(2,1)S(1)} %copy-done, f32[4,2,512]{2,1,0:T(2,128)S(1)} %multiply_add_fusion), kind=kLoop, calls=%fused_computation.107 | loop fusion | flops 245760 | bytes 344064 | tf_op jit(solution)/shard_map/convert_element_type | solution.py:192
  63.6 0.6 constant_dynamic-slice_fusion
  (58 shorter events, 3.9 us)
Async XLA Ops:
  1.4 1.1 %copy-start.1 = (f32[4,2,512]{2,1,0:T(2,128)S(1)}, f32[4,2,512]{2,1,0:T(2,128)}, u32[]{:S(2)}) copy-start(f32[4,2,512]{2,1,0:T(2,128)} %param.5) | copy-start | bytes 49156
  3.6 19.0 %all-to-all-start = ((bf16[24,8,2,512]{3,2,0,1:T(2,128)(2,1)}), bf16[24,8,2,512]{3,2,0,1:T(2,128)(2,1)S(1)}, u32[]{:S(2)}, u32[]{:S(2)}) async-start(bf16[24,8,2,512]{3,2,0,1:T(2,128)(2,1)} %bitcast.3), calls=%async_computation | async-start | bytes 786432 | tf_op jit(solution)/shard_map/all_to_all | solution.py:127
  10.9 0.7 %copy-start.2 = (f32[4]{0:T(128)S(1)}, f32[4]{0:T(128)}, u32[]{:S(2)}) copy-start(f32[4]{0:T(128)} %param.7) | copy-start | bytes 52
  27.5 7.9 %all-to-all-start.1 = ((f32[4,16,512]{2,1,0:T(8,128)}), f32[4,16,512]{2,1,0:T(8,128)S(1)}, u32[]{:S(2)}, u32[]{:S(2)}) async-start(f32[4,16,512]{2,1,0:T(8,128)} %broadcast_in_dim.86), calls=%async_computation.1 | async-start | bytes 262144 | tf_op jit(solution)/shard_map/all_to_all | solution.py:106
  52.4 10.4 %copy-start = (bf16[20,4,2,512]{3,2,1,0:T(2,128)(2,1)S(1)}, bf16[20,4,2,512]{3,2,1,0:T(2,128)(2,1)}, u32[]{:S(2)}) copy-start(bf16[20,4,2,512]{3,2,1,0:T(2,128)(2,1)} %param.4) | copy-start | bytes 491524
  52.4 10.1 %all-to-all-start.3 = ((f32[32,1,512]{2,1,0:T(1,128)}), f32[32,1,512]{2,1,0:T(1,128)S(1)}, u32[]{:S(2)}, u32[]{:S(2)}) async-start(f32[32,1,512]{2,1,0:T(1,128)} %broadcast_in_dim.91), calls=%async_computation.3 | async-start | bytes 131072 | tf_op jit(solution)/shard_map/all_to_all | solution.py:97

commit v20 on v18

--- a/solution.py
+++ b/solution.py
@@ -135,8 +135,14 @@
     own = (lax.broadcasted_iota(jnp.int32, (nlat, nlon), 0) // span) == grid_index % copies
     first = mem_index == 0
 
+    half = grid_index % copies
+
+    def own_rows(field):
+        return lax.dynamic_slice_in_dim(field, half * span, span, axis=1)
+
     def squares(field):
-        return jnp.sum(jnp.where(own[None], field * field, 0.0), axis=(0, 1))
+        mine = own_rows(field)
+        return jnp.sum(mine * mine, axis=(0, 1))
 
     def weighted(total):
         return jnp.where(first, jnp.sum(jnp.where(own, weight * total * total, 0.0), axis=0), 0.0)
@@ -172,7 +178,7 @@
     sums, _ = exchange(
         [
             squares(residual_next),
-            jnp.sum(jnp.where(own[None], residual_next * residual, 0.0), axis=(0, 1)),
+            jnp.sum(own_rows(residual_next) * own_rows(residual), axis=(0, 1)),
             jnp.where(first, jnp.sum(weight_rows * moved_rows * moved_rows, axis=(0, 1)), 0.0),
             jnp.where(first, jnp.sum(weight_rows * moved_rows * total1_rows, axis=(0, 1)), 0.0),
         ],

time: 64.1 us -> 64 us (level)
    reduce_sum x2, other arithmetic: 1.09 us -> 0.15 us  [squares(): return jnp.sum(mine * mine, axis=(0, 1))]
    add x0 -> x1, other arithmetic: none -> 0.87 us  [smooth_rows(): return 0.375 * field + 0.25 * near + 0.0625 * far]
where the time goes in v20:
time: 64 us; the launch traced here: 63.5 us
  waiting for transfers between devices  22.3 us (35%)
  starting transfers between devices  13.3 us (21%)
  blocking collectives  11.2 us (18%)
  other arithmetic  8.73 us (14%)
  local copies, waits for them, and re-layouts  6.8 us (11%)
  between operations  0.95 us (1%)
    all_to_all x1, blocking collectives, exchange(): got = lax.all_to_all(parcel, ('grid', 'mem'), 0, 0, tiled=True)  11.2 us
    all_to_all x1, waiting for transfers between devices, local_by_level(): got = lax.all_to_all(packed, 'grid', 1, 2, tiled=True)[:, 0]  10.4 us
    all_to_all x1, waiting for transfers between devices, exchange(): got = lax.all_to_all(parcel, ('grid', 'mem'), 0, 0, tiled=True)  7.41 us
    all_to_all x1, starting transfers between devices, local_by_level(): got = lax.all_to_all(packed, 'grid', 1, 2, tiled=True)[:, 0]  7.28 us
    all_to_all x1, waiting for transfers between devices, mem_total(): lax.all_to_all(jnp.broadcast_to(part, (mem_size,) + part.shape), 'mem', 0...  4.49 us
    all_to_all x1, starting transfers between devices, mem_total(): lax.all_to_all(jnp.broadcast_to(part, (mem_size,) + part.shape), 'mem', 0...  3.33 us
    all_to_all x1, starting transfers between devices, exchange(): got = lax.all_to_all(parcel, ('grid', 'mem'), 0, 0, tiled=True)  2.7 us
    unnamed x10, local copies, waits for them, and re-layouts  1.75 us
  transfers between devices with their start and end apart: 3, of which 3 were waited for; matrix products, arithmetic and copies ran while one was open for 1% of the time, Pallas kernels for 0%

profile of v20, /device:TPU:0, one launch (start us, length us, event | category | flops | bytes accessed | tf_op | source)
XLA Modules:
  0.0 63.5 jit_solution(10398712394496717118)
XLA Ops:
  0.6 0.8 %fusion.82 = (bf16[2,512]{1,0:T(2,128)(2,1)S(1)}, f32[2,512]{1,0:T(2,128)S(1)}) fusion(s32[2,512]{1,0:T(2,128)} %param.6), kind=kLoop, calls=%fused_computation.186 | loop fusion | flops 2048 | bytes 10240 | tf_op jit(solution)/shard_map/convert_element_type | solution.py:120
  1.4 1.0 %constant_dynamic-update-slice_fusion.4 = bf16[24,4,2,512]{3,2,1,0:T(2,128)(2,1)S(1)} fusion(bf16[20,4,2,512]{3,2,1,0:T(2,128)(2,1)} %param.4), kind=kLoop, calls=%fused_computation.141 | loop fusion | bytes 327680
  2.7 0.9 %broadcast_in_dim.60 = bf16[24,4,2,2,512]{4,3,0,2,1:T(2,128)(2,1)} broadcast(bf16[24,4,2,512]{3,2,0,1:T(2,128)(2,1)S(1)} %copy.13), dimensions={0,1,3,4} | broadcast | bytes 589824 | tf_op jit(solution)/shard_map/broadcast_in_dim | solution.py:126
  3.6 7.3 %all-to-all-start = ((bf16[24,8,2,512]{3,2,0,1:T(2,128)(2,1)}), bf16[24,8,2,512]{3,2,0,1:T(2,128)(2,1)S(1)}, u32[]{:S(2)}, u32[]{:S(2)}) async-start(bf16[24,8,2,512]{3,2,0,1:T(2,128)(2,1)} %bitcast.3), calls=%async_computation | async-start | bytes 786432 | tf_op jit(solution)/shard_map/all_to_all | solution.py:127
  10.9 0.6 %copy-done.2 = f32[4]{0:T(128)S(1)} copy-done((f32[4]{0:T(128)S(1)}, f32[4]{0:T(128)}, u32[]{:S(2)}) %copy-start.2) | copy-done | bytes 40
  11.6 0.6 dynamic_slice.15
  12.2 10.4 %all-to-all-done = bf16[24,8,2,512]{3,2,0,1:T(2,128)(2,1)S(1)} async-done(((bf16[24,8,2,512]{3,2,0,1:T(2,128)(2,1)}), bf16[24,8,2,512]{3,2,0,1:T(2,128)(2,1)S(1)}, u32[]{:S(2)}, u32[]{:S(2)}) %all-to-all-start) | async-done | bytes 393248 | tf_op jit(solution)/shard_map/all_to_all | solution.py:127
  23.3 0.7 %fusion.60 = f32[1,8,2,512]{3,2,0,1:T(2,128)S(1)} fusion(f32[3,8,2,512]{3,2,0,1:T(2,128)S(1)} %slice_convert_fusion, f32[]{:T(128)} %bitcast.4, bf16[24,8,2,512]{3,2,0,1:T(2,128)(2,1)S(1)} %all-to-all-done), kind=kLoop, calls=%fused_computation.117 | loop fusion | flops 40960 | bytes 147460 | tf_op jit(solution)/shard_map/mul | solution.py:153
  24.1 0.3 fusion.28
  24.6 0.9 %fusion.23 = f32[20,16,512]{2,1,0:T(8,128)S(1)} fusion(f32[20,16,512]{2,1,0:T(8,128)S(1)} %fusion.28, f32[20,16,2]{2,1,0:T(8,128)S(1)} %get-tuple-element.14, f32[20,16,2]{2,1,0:T(8,128)S(1)} %get-tuple-element.13), kind=kLoop, calls=%fused_computation.59 | loop fusion | flops 1802240 | bytes 1315840 | tf_op jit(solution)/shard_map/add | solution.py:87
  25.9 0.9 %fusion.57 = f32[16,512]{1,0:T(8,128)S(1)} fusion(f32[20,16,2]{2,1,0:T(8,128)S(1)} %get-tuple-element.12, f32[20,16,512]{2,1,0:T(8,128)S(1)} %fusion.34, f32[20,16,2]{2,1,0:T(8,128)S(1)} %get-tuple-element.11, bf16[20,16,512]{2,1,0:T(8,128)(2,1)S(1)} %slice.194), kind=kLoop, calls=%fused_computation.101 | loop fusion | flops 2285568 | bytes 1020928 | tf_op jit(solution)/shard_map/reduce_sum | solution.py:154
  26.8 0.7 %broadcast_in_dim.61 = f32[4,16,512]{2,1,0:T(8,128)} broadcast(f32[16,512]{1,0:T(8,128)S(1)} %fusion.57), dimensions={1,2} | broadcast | bytes 163840 | tf_op jit(solution)/shard_map/broadcast_in_dim | solution.py:106
  27.4 3.3 %all-to-all-start.1 = ((f32[4,16,512]{2,1,0:T(8,128)}), f32[4,16,512]{2,1,0:T(8,128)S(1)}, u32[]{:S(2)}, u32[]{:S(2)}) async-start(f32[4,16,512]{2,1,0:T(8,128)} %broadcast_in_dim.61), calls=%async_computation.1 | async-start | bytes 262144 | tf_op jit(solution)/shard_map/all_to_all | solution.py:106
  30.8 4.5 %all-to-all-done.1 = f32[4,16,512]{2,1,0:T(8,128)S(1)} async-done(((f32[4,16,512]{2,1,0:T(8,128)}), f32[4,16,512]{2,1,0:T(8,128)S(1)}, u32[]{:S(2)}, u32[]{:S(2)}) %all-to-all-start.1) | async-done | bytes 131104 | tf_op jit(solution)/shard_map/all_to_all | solution.py:106
  35.4 0.8 %fusion.65 = (f32[512]{0:T(512)S(1)}, f32[1,8,2,512]{3,2,0,1:T(2,128)S(1)}) fusion(f32[1,8,2,512]{3,2,1,0:T(2,128)S(1)} %reduce_sum.172, pred[8,2]{1,0:T(8,128)(4,1)S(1)} %fusion.69, s32[]{:T(128)S(6)} %select_n.111, s32[8,2]{1,0:T(8,128)S(1)} %get-tuple-element.27, s32[8,2]{1,0:T(8,128)S(1)} %get-tuple-element.28, f32[]{:T(128)} %bitcast.4, ...), kind=kLoop, calls=%fused_computation.124 | loop fusion | flops 65024 | bytes 84120 | tf_op jit(solution)/shard_map/reduce_sum | solution.py:148
  36.3 0.3 fusion.40
  36.7 0.9 %fusion.11 = f32[20,16,512]{2,1,0:T(8,128)S(1)} fusion(f32[20,16,512]{2,1,0:T(8,128)S(1)} %fusion.23, f32[20,16,512]{2,1,0:T(8,128)S(1)} %fusion.40, f32[20,16,2]{2,1,0:T(8,128)S(1)} %get-tuple-element.10, f32[20,16,2]{2,1,0:T(8,128)S(1)} %get-tuple-element.9), kind=kLoop, calls=%fused_computation.47 | loop fusion | flops 1966080 | bytes 1971200 | tf_op jit(solution)/shard_map/add | solution.py:155
  38.0 0.9 %fusion.58 = f32[16,512]{1,0:T(8,128)S(1)} fusion(f32[20,16,2]{2,1,0:T(8,128)S(1)} %get-tuple-element.8, f32[20,16,512]{2,1,0:T(8,128)S(1)} %fusion.46, f32[20,16,2]{2,1,0:T(8,128)S(1)} %get-tuple-element.7, bf16[20,16,512]{2,1,0:T(8,128)(2,1)S(1)} %slice.194), kind=kLoop, calls=%fused_computation.102 | loop fusion | flops 2285568 | bytes 1020928 | tf_op jit(solution)/shard_map/reduce_sum | solution.py:156
  39.2 11.2 %all_to_all.32 = f32[32,1,1280]{2,1,0:T(1,128)S(1)} all-to-all(f32[32,1,1280]{2,1,0:T(1,128)S(1)} %all_to_all.24), channel_id=1, replica_groups=mesh['grid'=8,'mem'=4] {'grid','mem'}, dimensions={0} | all-to-all | bytes 327680 | tf_op jit(solution)/shard_map/all_to_all | solution.py:97
  51.1 0.7 %broadcast_in_dim.66 = f32[32,1,512]{2,1,0:T(1,128)} broadcast(f32[512]{0:T(512)S(1)} %pad_maximum_fusion.10), dimensions={2} | broadcast | bytes 67584 | tf_op jit(solution)/shard_map/broadcast_in_dim | solution.py:95
  51.7 2.7 %all-to-all-start.3 = ((f32[32,1,512]{2,1,0:T(1,128)}), f32[32,1,512]{2,1,0:T(1,128)S(1)}, u32[]{:S(2)}, u32[]{:S(2)}) async-start(f32[32,1,512]{2,1,0:T(1,128)} %broadcast_in_dim.66), calls=%async_computation.3 | async-start | bytes 131072 | tf_op jit(solution)/shard_map/all_to_all | solution.py:97
  54.4 7.4 %all-to-all-done.3 = f32[32,1,512]{2,1,0:T(1,128)S(1)} async-done(((f32[32,1,512]{2,1,0:T(1,128)}), f32[32,1,512]{2,1,0:T(1,128)S(1)}, u32[]{:S(2)}, u32[]{:S(2)}) %all-to-all-start.3) | async-done | bytes 65568 | tf_op jit(solution)/shard_map/all_to_all | solution.py:97
  62.1 0.8 %add_convert_fusion = bf16[20,4,2,512]{3,2,1,0:T(2,128)(2,1)} fusion(bf16[20,4,2,512]{3,2,1,0:T(2,128)(2,1)S(1)} %copy-done, f32[4,2,512]{2,1,0:T(2,128)S(1)} %multiply_add_fusion), kind=kLoop, calls=%fused_computation.105 | loop fusion | flops 245760 | bytes 344064 | tf_op jit(solution)/shard_map/convert_element_type | solution.py:198
  62.9 0.6 constant_dynamic-slice_fusion
  (60 shorter events, 3.4 us)
Async XLA Ops:
  1.4 1.1 %copy-start.1 = (f32[4,2,512]{2,1,0:T(2,128)S(1)}, f32[4,2,512]{2,1,0:T(2,128)}, u32[]{:S(2)}) copy-start(f32[4,2,512]{2,1,0:T(2,128)} %param.5) | copy-start | bytes 49156
  3.6 19.0 %all-to-all-start = ((bf16[24,8,2,512]{3,2,0,1:T(2,128)(2,1)}), bf16[24,8,2,512]{3,2,0,1:T(2,128)(2,1)S(1)}, u32[]{:S(2)}, u32[]{:S(2)}) async-start(bf16[24,8,2,512]{3,2,0,1:T(2,128)(2,1)} %bitcast.3), calls=%async_computation | async-start | bytes 786432 | tf_op jit(solution)/shard_map/all_to_all | solution.py:127
  10.9 0.7 %copy-start.2 = (f32[4]{0:T(128)S(1)}, f32[4]{0:T(128)}, u32[]{:S(2)}) copy-start(f32[4]{0:T(128)} %param.7) | copy-start | bytes 52
  27.4 7.9 %all-to-all-start.1 = ((f32[4,16,512]{2,1,0:T(8,128)}), f32[4,16,512]{2,1,0:T(8,128)S(1)}, u32[]{:S(2)}, u32[]{:S(2)}) async-start(f32[4,16,512]{2,1,0:T(8,128)} %broadcast_in_dim.61), calls=%async_computation.1 | async-start | bytes 262144 | tf_op jit(solution)/shard_map/all_to_all | solution.py:106
  51.7 10.4 %copy-start = (bf16[20,4,2,512]{3,2,1,0:T(2,128)(2,1)S(1)}, bf16[20,4,2,512]{3,2,1,0:T(2,128)(2,1)}, u32[]{:S(2)}) copy-start(bf16[20,4,2,512]{3,2,1,0:T(2,128)(2,1)} %param.4) | copy-start | bytes 491524
  51.7 10.1 %all-to-all-start.3 = ((f32[32,1,512]{2,1,0:T(1,128)}), f32[32,1,512]{2,1,0:T(1,128)S(1)}, u32[]{:S(2)}, u32[]{:S(2)}) async-start(f32[32,1,512]{2,1,0:T(1,128)} %broadcast_in_dim.66), calls=%async_computation.3 | async-start | bytes 131072 | tf_op jit(solution)/shard_map/all_to_all | solution.py:97

commit v21 on v20

--- a/solution.py
+++ b/solution.py
@@ -134,7 +134,6 @@
     span = nlat // copies
     own = (lax.broadcasted_iota(jnp.int32, (nlat, nlon), 0) // span) == grid_index % copies
     first = mem_index == 0
-
     half = grid_index % copies
 
     def own_rows(field):
@@ -145,7 +144,9 @@
         return jnp.sum(mine * mine, axis=(0, 1))
 
     def weighted(total):
-        return jnp.where(first, jnp.sum(jnp.where(own, weight * total * total, 0.0), axis=0), 0.0)
+        mine = lax.dynamic_slice_in_dim(total, half * span, span, axis=0)
+        scale = lax.dynamic_slice_in_dim(weight, half * span, span, axis=0)
+        return jnp.where(first, jnp.sum(scale * mine * mine, axis=0), 0.0)
 
     def by_target(field):
         return jnp.repeat(field.reshape(grid_size, rows, nlon), mem_size, axis=0)

time: 64 us -> 63.2 us (0.988)
  other arithmetic: 8.73 us -> 7.95 us
    reduce_sum x1, other arithmetic: 0.76 us -> 0.03 us  [weighted(): return jnp.where(first, jnp.sum(scale * mine * mine, axis=0), 0.0)]
    mul x2 -> x1, other arithmetic: 0.75 us -> 0.07 us  [local_by_level(): residual = smooth_rows(widened * (weight * innov)[None])]
    mul x1, other arithmetic: 0.01 us -> 0.68 us  [local_by_level(): weight = got[count].astype(jnp.float32) * precision]
where the time goes in v21:
time: 63.2 us; the launch traced here: 62.8 us
  waiting for transfers between devices  22.4 us (35%)
  starting transfers between devices  13.3 us (21%)
  blocking collectives  11.2 us (18%)
  other arithmetic  7.95 us (13%)
  local copies, waits for them, and re-layouts  6.78 us (11%)
  between operations  0.94 us (1%)
    all_to_all x1, blocking collectives, exchange(): got = lax.all_to_all(parcel, ('grid', 'mem'), 0, 0, tiled=True)  11.2 us
    all_to_all x1, waiting for transfers between devices, local_by_level(): got = lax.all_to_all(packed, 'grid', 1, 2, tiled=True)[:, 0]  10.4 us
    all_to_all x1, waiting for transfers between devices, exchange(): got = lax.all_to_all(parcel, ('grid', 'mem'), 0, 0, tiled=True)  7.41 us
    all_to_all x1, starting transfers between devices, local_by_level(): got = lax.all_to_all(packed, 'grid', 1, 2, tiled=True)[:, 0]  7.28 us
    all_to_all x1, waiting for transfers between devices, mem_total(): lax.all_to_all(jnp.broadcast_to(part, (mem_size,) + part.shape), 'mem', 0...  4.55 us
    all_to_all x1, starting transfers between devices, mem_total(): lax.all_to_all(jnp.broadcast_to(part, (mem_size,) + part.shape), 'mem', 0...  3.33 us
    all_to_all x1, starting transfers between devices, exchange(): got = lax.all_to_all(parcel, ('grid', 'mem'), 0, 0, tiled=True)  2.7 us
    unnamed x10, local copies, waits for them, and re-layouts  1.75 us
  transfers between devices with their start and end apart: 3, of which 3 were waited for; matrix products, arithmetic and copies ran while one was open for 1% of the time, Pallas kernels for 0%

profile of v21, /device:TPU:0, one launch (start us, length us, event | category | flops | bytes accessed | tf_op | source)
XLA Modules:
  0.0 62.8 jit_solution(13325547275627384999)
XLA Ops:
  0.6 0.8 %fusion.80 = (bf16[2,512]{1,0:T(2,128)(2,1)S(1)}, f32[2,512]{1,0:T(2,128)S(1)}) fusion(s32[2,512]{1,0:T(2,128)} %param.6), kind=kLoop, calls=%fused_computation.179 | loop fusion | flops 2048 | bytes 10240 | tf_op jit(solution)/shard_map/convert_element_type | solution.py:120
  1.4 1.0 %constant_dynamic-update-slice_fusion.4 = bf16[24,4,2,512]{3,2,1,0:T(2,128)(2,1)S(1)} fusion(bf16[20,4,2,512]{3,2,1,0:T(2,128)(2,1)} %param.4), kind=kLoop, calls=%fused_computation.140 | loop fusion | bytes 327680
  2.7 0.9 %broadcast_in_dim.56 = bf16[24,4,2,2,512]{4,3,0,2,1:T(2,128)(2,1)} broadcast(bf16[24,4,2,512]{3,2,0,1:T(2,128)(2,1)S(1)} %copy.11), dimensions={0,1,3,4} | broadcast | bytes 589824 | tf_op jit(solution)/shard_map/broadcast_in_dim | solution.py:126
  3.6 7.3 %all-to-all-start = ((bf16[24,8,2,512]{3,2,0,1:T(2,128)(2,1)}), bf16[24,8,2,512]{3,2,0,1:T(2,128)(2,1)S(1)}, u32[]{:S(2)}, u32[]{:S(2)}) async-start(bf16[24,8,2,512]{3,2,0,1:T(2,128)(2,1)} %bitcast.3), calls=%async_computation | async-start | bytes 786432 | tf_op jit(solution)/shard_map/all_to_all | solution.py:127
  10.9 0.6 %copy-done.2 = f32[4]{0:T(128)S(1)} copy-done((f32[4]{0:T(128)S(1)}, f32[4]{0:T(128)}, u32[]{:S(2)}) %copy-start.2) | copy-done | bytes 40
  11.6 0.6 dynamic_slice.21
  12.2 10.4 %all-to-all-done = bf16[24,8,2,512]{3,2,0,1:T(2,128)(2,1)S(1)} async-done(((bf16[24,8,2,512]{3,2,0,1:T(2,128)(2,1)}), bf16[24,8,2,512]{3,2,0,1:T(2,128)(2,1)S(1)}, u32[]{:S(2)}, u32[]{:S(2)}) %all-to-all-start) | async-done | bytes 393248 | tf_op jit(solution)/shard_map/all_to_all | solution.py:127
  23.3 0.7 %convert_multiply_fusion.4 = (f32[1,8,2,512]{3,2,0,1:T(2,128)S(1)}, f32[1,8,2,512]{3,2,0,1:T(2,128)S(1)}) fusion(bf16[24,8,2,512]{3,2,0,1:T(2,128)(2,1)S(1)} %all-to-all-done, f32[]{:T(128)} %bitcast.4, f32[3,8,2,512]{3,2,0,1:T(2,128)S(1)} %slice_convert_fusion), kind=kLoop, calls=%fused_computation.117 | loop fusion | flops 40960 | bytes 180228 | tf_op jit(solution)/shard_map/mul | solution.py:131
  24.2 0.3 fusion.28
  24.6 0.9 %fusion.23 = f32[20,16,512]{2,1,0:T(8,128)S(1)} fusion(f32[20,16,512]{2,1,0:T(8,128)S(1)} %fusion.28, f32[20,16,2]{2,1,0:T(8,128)S(1)} %get-tuple-element.14, f32[20,16,2]{2,1,0:T(8,128)S(1)} %get-tuple-element.13), kind=kLoop, calls=%fused_computation.59 | loop fusion | flops 1802240 | bytes 1315840 | tf_op jit(solution)/shard_map/add | solution.py:87
  25.5 0.3 fusion.34
  26.0 0.9 %fusion.57 = f32[16,512]{1,0:T(8,128)S(1)} fusion(f32[20,16,2]{2,1,0:T(8,128)S(1)} %get-tuple-element.12, f32[20,16,512]{2,1,0:T(8,128)S(1)} %fusion.34, f32[20,16,2]{2,1,0:T(8,128)S(1)} %get-tuple-element.11, bf16[20,16,512]{2,1,0:T(8,128)(2,1)S(1)} %slice.194), kind=kLoop, calls=%fused_computation.101 | loop fusion | flops 2285568 | bytes 1020928 | tf_op jit(solution)/shard_map/reduce_sum | solution.py:155
  26.9 0.7 %broadcast_in_dim.57 = f32[4,16,512]{2,1,0:T(8,128)} broadcast(f32[16,512]{1,0:T(8,128)S(1)} %fusion.57), dimensions={1,2} | broadcast | bytes 163840 | tf_op jit(solution)/shard_map/broadcast_in_dim | solution.py:106
  27.5 3.3 %all-to-all-start.1 = ((f32[4,16,512]{2,1,0:T(8,128)}), f32[4,16,512]{2,1,0:T(8,128)S(1)}, u32[]{:S(2)}, u32[]{:S(2)}) async-start(f32[4,16,512]{2,1,0:T(8,128)} %broadcast_in_dim.57), calls=%async_computation.1 | async-start | bytes 262144 | tf_op jit(solution)/shard_map/all_to_all | solution.py:106
  30.9 4.5 %all-to-all-done.1 = f32[4,16,512]{2,1,0:T(8,128)S(1)} async-done(((f32[4,16,512]{2,1,0:T(8,128)}), f32[4,16,512]{2,1,0:T(8,128)S(1)}, u32[]{:S(2)}, u32[]{:S(2)}) %all-to-all-start.1) | async-done | bytes 131104 | tf_op jit(solution)/shard_map/all_to_all | solution.py:106
  35.6 0.3 fusion.40
  36.0 0.9 %fusion.11 = f32[20,16,512]{2,1,0:T(8,128)S(1)} fusion(f32[20,16,512]{2,1,0:T(8,128)S(1)} %fusion.23, f32[20,16,512]{2,1,0:T(8,128)S(1)} %fusion.40, f32[20,16,2]{2,1,0:T(8,128)S(1)} %get-tuple-element.10, f32[20,16,2]{2,1,0:T(8,128)S(1)} %get-tuple-element.9), kind=kLoop, calls=%fused_computation.47 | loop fusion | flops 1966080 | bytes 1971200 | tf_op jit(solution)/shard_map/add | solution.py:156
  37.4 0.9 %fusion.58 = f32[16,512]{1,0:T(8,128)S(1)} fusion(f32[20,16,2]{2,1,0:T(8,128)S(1)} %get-tuple-element.8, f32[20,16,512]{2,1,0:T(8,128)S(1)} %fusion.46, f32[20,16,2]{2,1,0:T(8,128)S(1)} %get-tuple-element.7, bf16[20,16,512]{2,1,0:T(8,128)(2,1)S(1)} %slice.194), kind=kLoop, calls=%fused_computation.102 | loop fusion | flops 2285568 | bytes 1020928 | tf_op jit(solution)/shard_map/reduce_sum | solution.py:157
  38.5 11.2 %all_to_all.32 = f32[32,1,1280]{2,1,0:T(1,128)S(1)} all-to-all(f32[32,1,1280]{2,1,0:T(1,128)S(1)} %all_to_all.24), channel_id=1, replica_groups=mesh['grid'=8,'mem'=4] {'grid','mem'}, dimensions={0} | all-to-all | bytes 327680 | tf_op jit(solution)/shard_map/all_to_all | solution.py:97
  50.3 0.7 %broadcast_in_dim.61 = f32[32,1,512]{2,1,0:T(1,128)} broadcast(f32[512]{0:T(512)S(1)} %pad_maximum_fusion.10), dimensions={2} | broadcast | bytes 67584 | tf_op jit(solution)/shard_map/broadcast_in_dim | solution.py:95
  51.0 2.7 %all-to-all-start.3 = ((f32[32,1,512]{2,1,0:T(1,128)}), f32[32,1,512]{2,1,0:T(1,128)S(1)}, u32[]{:S(2)}, u32[]{:S(2)}) async-start(f32[32,1,512]{2,1,0:T(1,128)} %broadcast_in_dim.61), calls=%async_computation.3 | async-start | bytes 131072 | tf_op jit(solution)/shard_map/all_to_all | solution.py:97
  53.7 7.4 %all-to-all-done.3 = f32[32,1,512]{2,1,0:T(1,128)S(1)} async-done(((f32[32,1,512]{2,1,0:T(1,128)}), f32[32,1,512]{2,1,0:T(1,128)S(1)}, u32[]{:S(2)}, u32[]{:S(2)}) %all-to-all-start.3) | async-done | bytes 65568 | tf_op jit(solution)/shard_map/all_to_all | solution.py:97
  61.4 0.8 %add_convert_fusion = bf16[20,4,2,512]{3,2,1,0:T(2,128)(2,1)} fusion(bf16[20,4,2,512]{3,2,1,0:T(2,128)(2,1)S(1)} %copy-done, f32[4,2,512]{2,1,0:T(2,128)S(1)} %multiply_add_fusion), kind=kLoop, calls=%fused_computation.105 | loop fusion | flops 245760 | bytes 344064 | tf_op jit(solution)/shard_map/convert_element_type | solution.py:199
  62.2 0.6 constant_dynamic-slice_fusion
  (55 shorter events, 3.1 us)
Async XLA Ops:
  1.4 1.1 %copy-start.1 = (f32[4,2,512]{2,1,0:T(2,128)S(1)}, f32[4,2,512]{2,1,0:T(2,128)}, u32[]{:S(2)}) copy-start(f32[4,2,512]{2,1,0:T(2,128)} %param.5) | copy-start | bytes 49156
  3.6 19.0 %all-to-all-start = ((bf16[24,8,2,512]{3,2,0,1:T(2,128)(2,1)}), bf16[24,8,2,512]{3,2,0,1:T(2,128)(2,1)S(1)}, u32[]{:S(2)}, u32[]{:S(2)}) async-start(bf16[24,8,2,512]{3,2,0,1:T(2,128)(2,1)} %bitcast.3), calls=%async_computation | async-start | bytes 786432 | tf_op jit(solution)/shard_map/all_to_all | solution.py:127
  10.9 0.7 %copy-start.2 = (f32[4]{0:T(128)S(1)}, f32[4]{0:T(128)}, u32[]{:S(2)}) copy-start(f32[4]{0:T(128)} %param.7) | copy-start | bytes 52
  27.5 7.9 %all-to-all-start.1 = ((f32[4,16,512]{2,1,0:T(8,128)}), f32[4,16,512]{2,1,0:T(8,128)S(1)}, u32[]{:S(2)}, u32[]{:S(2)}) async-start(f32[4,16,512]{2,1,0:T(8,128)} %broadcast_in_dim.57), calls=%async_computation.1 | async-start | bytes 262144 | tf_op jit(solution)/shard_map/all_to_all | solution.py:106
  51.0 10.4 %copy-start = (bf16[20,4,2,512]{3,2,1,0:T(2,128)(2,1)S(1)}, bf16[20,4,2,512]{3,2,1,0:T(2,128)(2,1)}, u32[]{:S(2)}) copy-start(bf16[20,4,2,512]{3,2,1,0:T(2,128)(2,1)} %param.4) | copy-start | bytes 491524
  51.0 10.1 %all-to-all-start.3 = ((f32[32,1,512]{2,1,0:T(1,128)}), f32[32,1,512]{2,1,0:T(1,128)S(1)}, u32[]{:S(2)}, u32[]{:S(2)}) async-start(f32[32,1,512]{2,1,0:T(1,128)} %broadcast_in_dim.61), calls=%async_computation.3 | async-start | bytes 131072 | tf_op jit(solution)/shard_map/all_to_all | solution.py:97
